TPU v7x, 32 devices: a whole 2x2x4 slice. The times are simulated.
32 devices in a mesh: ctx: 8 (over z, y), seq: 4 (over x, core).
Axes of the slice: x: 2, y: 2, z: 4, core: 2. Of those that a mesh axis runs over, the one named last changes fastest.
Arguments:
- queries: bfloat16 [32768, 2048], P(('ctx', 'seq')), may hold values from -6 to 6
- keys: bfloat16 [32768, 2048], P(('ctx', 'seq')), may hold values from -6 to 6
- values: bfloat16 [32768, 2048], P(('ctx', 'seq')), may hold values from -6 to 6
- mixing: float32 [10, 16, 32768], P(None, None, ('ctx', 'seq')), may hold values from 0 to 1, as said below
Outputs:
- attended: float32 [32768, 2048], P(('ctx', 'seq'))
Inputs may be any that keep to these rules, and one draw needn't show every extreme that they name: Every mixing weight is positive and at most 1.
All inputs are finite; a program needn't handle non-finite values.
Results may differ from a plain program's by a relative error of at most 0.0028.
Values sent between devices are 32-bit elements; how exact they have to be, the bound alone decides.
No kernel may reach another device: no remote copies, remote signals or barrier semaphores. Data moves between devices by JAX's collectives and lax.ppermute only.
A program may use at most 192 MiB of HBM per device.

v0:
```python
import functools

import numpy as np
import jax
import jax.numpy as jnp
from jax import lax
from jax.experimental import pallas as pl
from jax.experimental.pallas import tpu as pltpu
from jax.sharding import PartitionSpec as P

SPAN = 64
TQ = 256
CHUNKS = 4
LOCAL_GROUP = 2
CROSS_GROUP = 4


def level_masks(block, level_count):
    pos = np.arange(block)
    span = pos // SPAN
    crossed = span[:, None] ^ span[None, :]
    level = np.zeros_like(crossed)
    for power_index in range(level_count - 1):
        level = level + (crossed >= 2**power_index)
    causal = pos[:, None] >= pos[None, :]
    inner = int(np.log2(block // SPAN)) + 1
    return np.stack(
        [((level == l) & causal).astype(np.float32) for l in range(inner)]
    )


def state_kernel(head_count, k_ref, v_ref, o_ref):
    @pl.when(pl.program_id(0) == 0)
    def _():
        o_ref[...] = jnp.zeros_like(o_ref)

    dk = o_ref.shape[1]
    dv = o_ref.shape[2]
    for h in range(head_count):
        o_ref[h] += lax.dot_general(
            k_ref[:, h * dk:(h + 1) * dk], v_ref[:, h * dv:(h + 1) * dv],
            (((0,), (0,)), ((), ())), preferred_element_type=jnp.float32,
        )


def own_state(keys, values, head_count):
    rows, width = keys.shape
    dk = width // head_count
    dv = values.shape[1] // head_count
    tr = min(rows, 512)
    return pl.pallas_call(
        functools.partial(state_kernel, head_count),
        grid=(rows // tr,),
        in_specs=[
            pl.BlockSpec((tr, width), lambda r: (r, 0)),
            pl.BlockSpec((tr, values.shape[1]), lambda r: (r, 0)),
        ],
        out_specs=pl.BlockSpec((head_count, dk, dv), lambda r: (0, 0, 0)),
        out_shape=jax.ShapeDtypeStruct((head_count, dk, dv), jnp.float32),
        cost_estimate=pl.CostEstimate(
            flops=2 * rows * dk * dv * head_count,
            bytes_accessed=2 * rows * (dk + dv) * head_count + 4 * dk * dv * head_count,
            transcendentals=0,
        ),
        compiler_params=pltpu.CompilerParams(vmem_limit_bytes=64 * 1024 * 1024),
    )(keys, values)


def local_kernel(scale, rows, group, q_ref, k_ref, v_ref, m_ref, c_ref, *rest):
    o_ref = rest[-1]
    blocks = rows // TQ
    inner = c_ref.shape[0]
    dk = q_ref.shape[1] // group
    dv = v_ref.shape[1] // group
    for j in range(group):
        qc = slice(j * dk, (j + 1) * dk)
        vc = slice(j * dv, (j + 1) * dv)
        for a in range(blocks):
            r0 = a * TQ
            s = lax.dot_general(
                q_ref[r0:r0 + TQ, qc], k_ref[0:r0 + TQ, qc],
                (((1,), (1,)), ((), ())), preferred_element_type=jnp.float32,
            )
            s = s * scale
            mix = m_ref[j, r0:r0 + TQ, :]
            pieces = []
            for b in range(a):
                level = inner + (a ^ b).bit_length() - 1
                w = mix[:, level:level + 1]
                pieces.append((s[:, b * TQ:(b + 1) * TQ] * w).astype(jnp.bfloat16))
            wd = c_ref[0] * mix[:, 0:1]
            for l in range(1, inner):
                wd = wd + c_ref[l] * mix[:, l:l + 1]
            pieces.append((s[:, r0:r0 + TQ] * wd).astype(jnp.bfloat16))
            p = pieces[0] if len(pieces) == 1 else jnp.concatenate(pieces, axis=1)
            o_ref[r0:r0 + TQ, vc] = jnp.dot(
                p, v_ref[0:r0 + TQ, vc], preferred_element_type=jnp.float32
            )


def local_part(queries, keys, values, mix_t, masks, first, count, group, scale, prev):
    rows = queries.shape[0]
    head_count = mix_t.shape[0]
    dk = queries.shape[1] // head_count
    dv = values.shape[1] // head_count
    levels = mix_t.shape[2]
    blocks = rows // TQ
    tiles = blocks * (blocks + 1) // 2
    base = first // group
    in_specs = [
        pl.BlockSpec((rows, dk * group), lambda h: (0, h + base)),
        pl.BlockSpec((rows, dk * group), lambda h: (0, h + base)),
        pl.BlockSpec((rows, dv * group), lambda h: (0, h + base)),
        pl.BlockSpec((group, rows, levels), lambda h: (h + base, 0, 0)),
        pl.BlockSpec(masks.shape, lambda h: (0, 0, 0)),
    ]
    operands = [queries, keys, values, mix_t, masks]
    aliases = {}
    if prev is not None:
        in_specs.append(pl.BlockSpec(memory_space=pl.ANY))
        operands.append(prev)
        aliases = {5: 0}
    return pl.pallas_call(
        functools.partial(local_kernel, scale, rows, group),
        grid=(count // group,),
        in_specs=in_specs,
        out_specs=pl.BlockSpec((rows, dv * group), lambda h: (0, h + base)),
        out_shape=jax.ShapeDtypeStruct((rows, dv * head_count), jnp.float32),
        input_output_aliases=aliases,
        cost_estimate=pl.CostEstimate(
            flops=2 * tiles * TQ * TQ * (dk + dv) * count,
            bytes_accessed=(2 * rows * (2 * dk + dv) + 4 * rows * dv) * count,
            transcendentals=0,
        ),
        compiler_params=pltpu.CompilerParams(vmem_limit_bytes=64 * 1024 * 1024),
    )(*operands)


def cross_kernel(scale, rows, first_level, group, q_ref, s_ref, m_ref, l_ref, o_ref):
    bits = s_ref.shape[0]
    dk = s_ref.shape[2]
    dv = s_ref.shape[3]
    for j in range(group):
        sib = jnp.concatenate([s_ref[b, j] for b in range(bits)], axis=1)
        for a in range(rows // TQ):
            r0 = a * TQ
            t = jnp.dot(
                q_ref[r0:r0 + TQ, j * dk:(j + 1) * dk], sib,
                preferred_element_type=jnp.float32,
            )
            mix = m_ref[j, r0:r0 + TQ, :]
            cross = jnp.zeros((TQ, dv), jnp.float32)
            for b in range(bits):
                w = mix[:, first_level + b:first_level + b + 1] * scale
                cross = cross + w * t[:, b * dv:(b + 1) * dv]
            o_ref[r0:r0 + TQ, j * dv:(j + 1) * dv] = (
                l_ref[r0:r0 + TQ, j * dv:(j + 1) * dv] + cross
            )


def cross_all(queries, sibs, mix_t, local, scale, first_level, group):
    rows = queries.shape[0]
    head_count = mix_t.shape[0]
    dk = queries.shape[1] // head_count
    dv = sibs.shape[3]
    levels = mix_t.shape[2]
    bits = sibs.shape[0]
    return pl.pallas_call(
        functools.partial(cross_kernel, scale, rows, first_level, group),
        grid=(head_count // group,),
        in_specs=[
            pl.BlockSpec((rows, dk * group), lambda g: (0, g)),
            pl.BlockSpec((bits, group, dk, dv), lambda g: (0, g, 0, 0)),
            pl.BlockSpec((group, rows, levels), lambda g: (g, 0, 0)),
            pl.BlockSpec((rows, dv * group), lambda g: (0, g)),
        ],
        out_specs=pl.BlockSpec((rows, dv * group), lambda g: (0, g)),
        out_shape=jax.ShapeDtypeStruct((rows, dv * head_count), jnp.float32),
        input_output_aliases={3: 0},
        cost_estimate=pl.CostEstimate(
            flops=2 * rows * dk * dv * bits * head_count,
            bytes_accessed=(2 * rows * dk + 8 * rows * dv) * head_count,
            transcendentals=0,
        ),
        compiler_params=pltpu.CompilerParams(vmem_limit_bytes=64 * 1024 * 1024),
    )(queries, sibs, mix_t, local)


def swap(block, axis, bit, one_way=False):
    count = lax.axis_size(axis)
    route = []
    for low in range(count):
        high = low | 1 << bit
        if high != low and high < count:
            route.append((low, high))
            if not one_way:
                route.append((high, low))
    return lax.ppermute(block, axis, route)


def to_offset(block, axis, offset):
    count = lax.axis_size(axis)
    return lax.ppermute(block, axis, [(s, s ^ offset) for s in range(count)])


def shards(queries, keys, values, mixing):
    rows = queries.shape[0]
    head_count = mixing.shape[1]
    dk = queries.shape[1] // head_count
    scale = dk ** (-0.5)
    level_count = (rows // SPAN).bit_length()
    mix_t = mixing.transpose(1, 2, 0)
    masks = jnp.asarray(level_masks(TQ, level_count))

    state = own_state(keys, values, head_count)

    seq_count = lax.axis_size("seq")
    ctx_count = lax.axis_size("ctx")
    seq_bits = seq_count.bit_length() - 1
    ctx_bits = ctx_count.bit_length() - 1
    seq_place = lax.axis_index("seq")
    ctx_place = lax.axis_index("ctx")

    sibs = []
    flags = []
    running = state
    half = head_count // 2
    for bit in range(seq_bits):
        if bit == 0 or seq_count < 4:
            partner = swap(running, "seq", bit)
        else:
            mine = seq_place & 1
            sent = lax.dynamic_slice_in_dim(running, mine * half, half, 0)
            got = swap(sent, "seq", bit)
            other = swap(got, "seq", 0)
            lo = jnp.where(mine == 0, got, other)
            hi = jnp.where(mine == 0, other, got)
            partner = jnp.concatenate([lo, hi], axis=0)
        sibs.append(partner)
        flags.append(seq_place >> bit & 1)
        running = running + partner

    share = head_count // seq_count
    quarter = lax.dynamic_slice_in_dim(running, seq_place * share, share, 0)
    ctx_sibs = []
    for bit in range(ctx_bits):
        got = swap(quarter, "ctx", bit, one_way=(bit == ctx_bits - 1))
        ctx_sibs.append(got)
        if bit != ctx_bits - 1:
            quarter = quarter + got

    for bit in range(ctx_bits):
        part = ctx_sibs[bit]
        parts = {0: part}
        for offset in range(1, seq_count):
            if offset & 1 and offset > 1:
                parts[offset] = to_offset(parts[offset ^ 1], "seq", 1)
            else:
                parts[offset] = to_offset(part, "seq", offset)
        full = []
        for owner in range(seq_count):
            pick = jnp.zeros_like(part)
            for offset in range(seq_count):
                pick = jnp.where((seq_place ^ offset) == owner, parts[offset], pick)
            full.append(pick)
        sibs.append(jnp.concatenate(full, axis=0))
        flags.append(ctx_place >> bit & 1)

    rounded = [
        (flags[i].astype(jnp.float32) * sibs[i]).astype(jnp.bfloat16) for i in range(len(sibs))
    ]
    early = jnp.stack(rounded[:-1])
    last = rounded[-1][None]

    per = head_count // CHUNKS
    local = None
    for c in range(CHUNKS):
        local = local_part(
            queries, keys, values, mix_t, masks, c * per, per, LOCAL_GROUP, scale, local
        )
    out = cross_all(queries, early, mix_t, local, scale, level_count, CROSS_GROUP)
    return cross_all(
        queries, last, mix_t, out, scale, level_count + len(rounded) - 1, CROSS_GROUP
    )


def solution(mesh):
    return jax.shard_map(
        shards,
        mesh=mesh,
        in_specs=(
            P(("ctx", "seq"), None),
            P(("ctx", "seq"), None),
            P(("ctx", "seq"), None),
            P(None, None, ("ctx", "seq")),
        ),
        out_specs=P(("ctx", "seq"), None),
        check_vma=False,
    )
```

profile of v0, /device:TPU:25, one launch (start us, length us, event | category | flops | bytes accessed | tf_op | source)
XLA Modules:
  0.0 149.5 jit_solution(17090238369304564692)
XLA Ops:
  0.0 5.2 %shard_map.55 = f32[16,128,128]{2,1,0:T(8,128)} custom-call(bf16[1024,2048]{1,0:T(8,128)(2,1)} %k_ref.9, bf16[1024,2048]{1,0:T(8,128)(2,1)} %v_ref.9), custom_call_target="tpu_custom_call" | custom-call | flops 536870912 | bytes 9437184 | tf_op jit(solution)/shard_map/pallas_call | solution.py:51
  5.3 0.7 collective-permute-start
  5.9 2.5 %collective-permute-done = f32[16,128,128]{2,1,0:T(8,128)S(1)} collective-permute-done((f32[16,128,128]{2,1,0:T(8,128)}, f32[16,128,128]{2,1,0:T(8,128)S(1)}, u32[]{:S(2)}, u32[]{:S(2)}) %collective-permute-start) | collective-permute-done | bytes 1048608 | tf_op jit(solution)/shard_map/ppermute | solution.py:198
  8.4 2.3 %fusion.4 = (bf16[1,16,128,128]{3,2,1,0:T(8,128)(2,1)}, f32[16,128,128]{2,1,0:T(8,128)S(1)}) fusion(f32[16,128,128]{2,1,0:T(8,128)S(1)} %collective-permute-done, f32[]{:T(128)S(6)} %convert_element_type.60, f32[16,128,128]{2,1,0:T(8,128)} %shard_map.55), kind=kLoop, calls=%fused_computation.12 | loop fusion | flops 786432 | bytes 3670020 | tf_op jit(solution)/shard_map/stack | solution.py:272
  10.7 1.3 collective-permute-start.1
  12.0 11.9 %collective-permute-done.1 = f32[8,128,128]{2,1,0:T(8,128)S(1)} collective-permute-done((f32[8,128,128]{2,1,0:T(8,128)S(1)}, f32[8,128,128]{2,1,0:T(8,128)S(1)}, u32[]{:S(2)}, u32[]{:S(2)}) %collective-permute-start.1) | collective-permute-done | bytes 524320 | tf_op jit(solution)/shard_map/ppermute | solution.py:198
  23.9 1.2 collective-permute-start.2
  25.1 1.5 %collective-permute-done.2 = f32[8,128,128]{2,1,0:T(8,128)S(1)} collective-permute-done((f32[8,128,128]{2,1,0:T(8,128)S(1)}, f32[8,128,128]{2,1,0:T(8,128)S(1)}, u32[]{:S(2)}, u32[]{:S(2)}) %collective-permute-start.2) | collective-permute-done | bytes 524320 | tf_op jit(solution)/shard_map/ppermute | solution.py:198
  26.7 0.1 broadcast_select_fusion
  26.8 0.8 copy-done
  27.6 0.1 copy-done.1
  27.7 1.2 collective-permute-start.3
  29.0 6.3 %collective-permute-done.3 = f32[4,128,128]{2,1,0:T(8,128)S(1)} collective-permute-done((f32[4,128,128]{2,1,0:T(8,128)S(1)}, f32[4,128,128]{2,1,0:T(8,128)S(1)}, u32[]{:S(2)}, u32[]{:S(2)}) %collective-permute-start.3) | collective-permute-done | bytes 262176 | tf_op jit(solution)/shard_map/ppermute | solution.py:198
  35.2 1.2 collective-permute-start.9
  36.4 1.5 %collective-permute-start.11 = (f32[4,128,128]{2,1,0:T(8,128)S(1)}, f32[4,128,128]{2,1,0:T(8,128)S(1)}, u32[]{:S(2)}, u32[]{:S(2)}) collective-permute-start(f32[4,128,128]{2,1,0:T(8,128)S(1)} %collective-permute-done.3), channel_id=1, source_target_pairs={{0,1},{1,0},{2,3},{3,2},{4,5},{5,4},{6,7},{7,6},{8,9},{9,8},{10,11... | collective-permute-start | bytes 786440 | tf_op jit(solution)/shard_map/ppermute | solution.py:203
  38.0 3.9 %collective-permute-done.9 = f32[4,128,128]{2,1,0:T(8,128)S(1)} collective-permute-done((f32[4,128,128]{2,1,0:T(8,128)S(1)}, f32[4,128,128]{2,1,0:T(8,128)S(1)}, u32[]{:S(2)}, u32[]{:S(2)}) %collective-permute-start.9) | collective-permute-done | bytes 262176 | tf_op jit(solution)/shard_map/ppermute | solution.py:203
  41.9 2.1 %collective-permute-start.10 = (f32[4,128,128]{2,1,0:T(8,128)S(1)}, f32[4,128,128]{2,1,0:T(8,128)S(1)}, u32[]{:S(2)}, u32[]{:S(2)}) collective-permute-start(f32[4,128,128]{2,1,0:T(8,128)S(1)} %collective-permute-done.9), channel_id=1, source_target_pairs={{0,1},{1,0},{2,3},{3,2},{4,5},{5,4},{6,7},{7,6},{8,9},{9,8},{10,11... | collective-permute-start | bytes 786440 | tf_op jit(solution)/shard_map/ppermute | solution.py:203
  44.0 1.2 collective-permute-done.10
  45.1 1.0 select_bitcast_fusion.7
  46.1 0.7 copy-done.10
  46.8 0.2 collective-permute-start.4
  47.0 7.4 %collective-permute-done.4 = f32[4,128,128]{2,1,0:T(8,128)} collective-permute-done((f32[4,128,128]{2,1,0:T(8,128)S(1)}, f32[4,128,128]{2,1,0:T(8,128)}, u32[]{:S(2)}, u32[]{:S(2)}) %collective-permute-start.4) | collective-permute-done | bytes 262176 | tf_op jit(solution)/shard_map/ppermute | solution.py:198
  54.4 1.2 collective-permute-start.12
  55.6 4.7 %copy.11 = f32[10,16,1024]{0,2,1:T(8,128)} copy(f32[10,16,1024]{2,1,0:T(8,128)S(1)} %copy-done.11) | data formatting | bytes 1310720 | tf_op args[3]
  60.4 7.1 %shard_map.56.rest_0_ = f32[1024,2048]{1,0:T(8,128)} custom-call(bf16[1024,2048]{1,0:T(8,128)(2,1)} %q_ref.11, bf16[1024,2048]{1,0:T(8,128)(2,1)} %k_ref.9, bf16[1024,2048]{1,0:T(8,128)(2,1)} %v_ref.9, f32[16,1024,10]{2,1,0:T(8,128)} %bitcast.29, f32[3,256,256]{2,1,0:T(8,128)} %constant.27.clone.c_ref), custom_call_target="tpu_custom_call" | custom-call | flops 1342177280 | bytes 5242880 | tf_op jit(solution)/shard_map/pallas_call | solution.py:123
  67.5 7.0 %shard_map.57.rest_0_ = f32[1024,2048]{1,0:T(8,128)} custom-call(bf16[1024,2048]{1,0:T(8,128)(2,1)} %q_ref.11, bf16[1024,2048]{1,0:T(8,128)(2,1)} %k_ref.9, bf16[1024,2048]{1,0:T(8,128)(2,1)} %v_ref.9, f32[16,1024,10]{2,1,0:T(8,128)} %bitcast.30, f32[3,256,256]{2,1,0:T(8,128)} %constant.27.clone.c_ref, ...), custom_call_target="tpu_custom_call", output_to_operand_aliasing={{}: (5, {})} | custom-call | flops 1342177280 | bytes 5242880 | tf_op jit(solution)/shard_map/pallas_call | solution.py:123
  74.5 1.5 %collective-permute-start.14 = (f32[4,128,128]{2,1,0:T(8,128)}, f32[4,128,128]{2,1,0:T(8,128)}, u32[]{:S(2)}, u32[]{:S(2)}) collective-permute-start(f32[4,128,128]{2,1,0:T(8,128)} %collective-permute-done.4), channel_id=1, source_target_pairs={{0,1},{1,0},{2,3},{3,2},{4,5},{5,4},{6,7},{7,6},{8,9},{9,8},{10,11... | collective-permute-start | bytes 786440 | tf_op jit(solution)/shard_map/ppermute | solution.py:203
  76.0 0.1 collective-permute-start.13
  76.1 7.0 %shard_map.58.rest_0_ = f32[1024,2048]{1,0:T(8,128)} custom-call(bf16[1024,2048]{1,0:T(8,128)(2,1)} %q_ref.11, bf16[1024,2048]{1,0:T(8,128)(2,1)} %k_ref.9, bf16[1024,2048]{1,0:T(8,128)(2,1)} %v_ref.9, f32[16,1024,10]{2,1,0:T(8,128)} %bitcast.31, f32[3,256,256]{2,1,0:T(8,128)} %constant.27.clone.c_ref, ...), custom_call_target="tpu_custom_call", output_to_operand_aliasing={{}: (5, {})} | custom-call | flops 1342177280 | bytes 5242880 | tf_op jit(solution)/shard_map/pallas_call | solution.py:123
  83.0 7.0 %shard_map.59.l_ref = f32[1024,2048]{1,0:T(8,128)} custom-call(bf16[1024,2048]{1,0:T(8,128)(2,1)} %q_ref.11, bf16[1024,2048]{1,0:T(8,128)(2,1)} %k_ref.9, bf16[1024,2048]{1,0:T(8,128)(2,1)} %v_ref.9, f32[16,1024,10]{2,1,0:T(8,128)} %bitcast.32, f32[3,256,256]{2,1,0:T(8,128)} %constant.27.clone.c_ref, ...), custom_call_target="tpu_custom_call", output_to_operand_aliasing={{}: (5, {})} | custom-call | flops 1342177280 | bytes 5242880 | tf_op jit(solution)/shard_map/pallas_call | solution.py:123
  90.0 1.4 fusion.1
  91.5 1.5 select_bitcast_fusion.3
  92.9 1.5 collective-permute-start.5
  94.4 1.0 select_bitcast_fusion.6
  95.5 0.1 fusion.2
  95.6 14.0 %collective-permute-done.5 = f32[4,128,128]{2,1,0:T(8,128)} collective-permute-done((f32[4,128,128]{2,1,0:T(8,128)S(1)}, f32[4,128,128]{2,1,0:T(8,128)}, u32[]{:S(2)}, u32[]{:S(2)}) %collective-permute-start.5) | collective-permute-done | bytes 262176 | tf_op jit(solution)/shard_map/ppermute | solution.py:198
  109.6 0.3 collective-permute-start.6
  109.8 1.0 select_bitcast_fusion.2
  110.8 0.1 fusion.3
  111.0 0.8 collective-permute-start.8
  111.8 5.5 %collective-permute-done.6 = f32[4,128,128]{2,1,0:T(8,128)} collective-permute-done((f32[4,128,128]{2,1,0:T(8,128)}, f32[4,128,128]{2,1,0:T(8,128)}, u32[]{:S(2)}, u32[]{:S(2)}) %collective-permute-start.6) | collective-permute-done | bytes 262176 | tf_op jit(solution)/shard_map/ppermute | solution.py:203
  117.3 1.3 collective-permute-start.7
  118.6 1.6 %pad_maximum_fusion.s_ref = bf16[4,16,128,128]{3,2,1,0:T(8,128)(2,1)} fusion(bf16[1,16,128,128]{3,2,1,0:T(8,128)(2,1)S(1)} %fusion.3, bf16[1,16,128,128]{3,2,1,0:T(8,128)(2,1)S(1)} %fusion.2, bf16[1,16,128,128]{3,2,1,0:T(8,128)(2,1)S(1)} %fusion.1, bf16[1,16,128,128]{3,2,1,0:T(8,128)(2,1)S(1)} %copy-done.2), kind=kLoop, calls=%fused_computation | loop fusion | flops 3145728 | bytes 4194304 | tf_op jit(solution)/shard_map/stack | solution.py:272
  120.2 14.9 %shard_map.60.l_ref = f32[1024,2048]{1,0:T(8,128)} custom-call(bf16[1024,2048]{1,0:T(8,128)(2,1)} %q_ref.11, bf16[4,16,128,128]{3,2,1,0:T(8,128)(2,1)} %pad_maximum_fusion.s_ref, f32[16,1024,10]{2,1,0:T(8,128)} %bitcast.33, f32[1024,2048]{1,0:T(8,128)} %shard_map.59.l_ref), custom_call_target="tpu_custom_call", output_to_operand_aliasing={{}: (3, {})} | custom-call | flops 2147483648 | bytes 20971520 | tf_op jit(solution)/shard_map/pallas_call | solution.py:168
  135.2 1.0 select_bitcast_fusion.10
  136.2 1.3 select_bitcast_fusion.11
  137.5 1.0 fusion.s_ref
  138.5 11.0 %shard_map.61 = f32[1024,2048]{1,0:T(8,128)} custom-call(bf16[1024,2048]{1,0:T(8,128)(2,1)} %q_ref.11, bf16[1,16,128,128]{3,2,1,0:T(8,128)(2,1)} %fusion.s_ref, f32[16,1024,10]{2,1,0:T(8,128)} %bitcast.34, f32[1024,2048]{1,0:T(8,128)} %shard_map.60.l_ref), custom_call_target="tpu_custom_call", output_to_operand_aliasing={{}: (3, {})} | custom-call | flops 536870912 | bytes 20971520 | tf_op jit(solution)/shard_map/pallas_call | solution.py:168
  (29 shorter events, 0.1 us)
Async XLA Ops:
  5.3 3.2 %collective-permute-start = (f32[16,128,128]{2,1,0:T(8,128)}, f32[16,128,128]{2,1,0:T(8,128)S(1)}, u32[]{:S(2)}, u32[]{:S(2)}) collective-permute-start(f32[16,128,128]{2,1,0:T(8,128)} %shard_map.55), channel_id=1, source_target_pairs={{0,1},{1,0},{2,3},{3,2},{4,5},{5,4},{6,7},{7,6},{8,9},{9,8},{10,11... | collective-permute-start | bytes 3145736 | tf_op jit(solution)/shard_map/ppermute | solution.py:198
  10.7 44.9 %copy-start.11 = (f32[10,16,1024]{2,1,0:T(8,128)S(1)}, f32[10,16,1024]{2,1,0:T(8,128)}, u32[]{:S(2)}) copy-start(f32[10,16,1024]{2,1,0:T(8,128)} %param.8) | copy-start | bytes 1966084
  10.7 13.2 %collective-permute-start.1 = (f32[8,128,128]{2,1,0:T(8,128)S(1)}, f32[8,128,128]{2,1,0:T(8,128)S(1)}, u32[]{:S(2)}, u32[]{:S(2)}) collective-permute-start(f32[8,128,128]{2,1,0:T(8,128)S(1)} %constant_dynamic-slice_fusion), channel_id=1, source_target_pairs={{0,2},{2,0},{1,3},{3,1},{4,6},{6,4},{5,7},{7,5},{8,10},{10,8},{9,1... | collective-permute-start | bytes 1572872 | tf_op jit(solution)/shard_map/ppermute | solution.py:198
  23.9 2.8 %collective-permute-start.2 = (f32[8,128,128]{2,1,0:T(8,128)S(1)}, f32[8,128,128]{2,1,0:T(8,128)S(1)}, u32[]{:S(2)}, u32[]{:S(2)}) collective-permute-start(f32[8,128,128]{2,1,0:T(8,128)S(1)} %collective-permute-done.1), channel_id=1, source_target_pairs={{0,1},{1,0},{2,3},{3,2},{4,5},{5,4},{6,7},{7,6},{8,9},{9,8},{10,11... | collective-permute-start | bytes 1572872 | tf_op jit(solution)/shard_map/ppermute | solution.py:198
  26.8 0.8 copy-start
  26.8 1.0 copy-start.1
  27.7 7.5 %collective-permute-start.3 = (f32[4,128,128]{2,1,0:T(8,128)S(1)}, f32[4,128,128]{2,1,0:T(8,128)S(1)}, u32[]{:S(2)}, u32[]{:S(2)}) collective-permute-start(f32[4,128,128]{2,1,0:T(8,128)S(1)} %fusion.6), channel_id=1, source_target_pairs={{0,4},{4,0},{8,12},{12,8},{16,20},{20,16},{24,28},{28,24},{1,5},{5... | collective-permute-start | bytes 786440 | tf_op jit(solution)/shard_map/ppermute | solution.py:198
  35.2 25.1 %copy-start.3 = (f32[4,128,128]{2,1,0:T(8,128)}, f32[4,128,128]{2,1,0:T(8,128)S(1)}, u32[]{:S(2)}) copy-start(f32[4,128,128]{2,1,0:T(8,128)S(1)} %collective-permute-done.3) | copy-start | bytes 786436
  35.2 6.6 %collective-permute-start.9 = (f32[4,128,128]{2,1,0:T(8,128)S(1)}, f32[4,128,128]{2,1,0:T(8,128)S(1)}, u32[]{:S(2)}, u32[]{:S(2)}) collective-permute-start(f32[4,128,128]{2,1,0:T(8,128)S(1)} %collective-permute-done.3), channel_id=1, source_target_pairs={{0,2},{1,3},{2,0},{3,1},{4,6},{5,7},{6,4},{7,5},{8,10},{9,11},{10,... | collective-permute-start | bytes 786440 | tf_op jit(solution)/shard_map/ppermute | solution.py:203
  36.4 7.5 %collective-permute-start.11 = (f32[4,128,128]{2,1,0:T(8,128)S(1)}, f32[4,128,128]{2,1,0:T(8,128)S(1)}, u32[]{:S(2)}, u32[]{:S(2)}) collective-permute-start(f32[4,128,128]{2,1,0:T(8,128)S(1)} %collective-permute-done.3), channel_id=1, source_target_pairs={{0,1},{1,0},{2,3},{3,2},{4,5},{5,4},{6,7},{7,6},{8,9},{9,8},{10,11... | collective-permute-start | bytes 786440 | tf_op jit(solution)/shard_map/ppermute | solution.py:203
  41.9 18.5 %copy-start.4 = (f32[4,128,128]{2,1,0:T(8,128)}, f32[4,128,128]{2,1,0:T(8,128)S(1)}, u32[]{:S(2)}) copy-start(f32[4,128,128]{2,1,0:T(8,128)S(1)} %collective-permute-done.9) | copy-start | bytes 786436
  41.9 3.2 %collective-permute-start.10 = (f32[4,128,128]{2,1,0:T(8,128)S(1)}, f32[4,128,128]{2,1,0:T(8,128)S(1)}, u32[]{:S(2)}, u32[]{:S(2)}) collective-permute-start(f32[4,128,128]{2,1,0:T(8,128)S(1)} %collective-permute-done.9), channel_id=1, source_target_pairs={{0,1},{1,0},{2,3},{3,2},{4,5},{5,4},{6,7},{7,6},{8,9},{9,8},{10,11... | collective-permute-start | bytes 786440 | tf_op jit(solution)/shard_map/ppermute | solution.py:203
  44.0 16.4 %copy-start.5 = (f32[4,128,128]{2,1,0:T(8,128)}, f32[4,128,128]{2,1,0:T(8,128)S(1)}, u32[]{:S(2)}) copy-start(f32[4,128,128]{2,1,0:T(8,128)S(1)} %collective-permute-done.11) | copy-start | bytes 786436
  45.1 15.2 %copy-start.6 = (f32[4,128,128]{2,1,0:T(8,128)}, f32[4,128,128]{2,1,0:T(8,128)S(1)}, u32[]{:S(2)}) copy-start(f32[4,128,128]{2,1,0:T(8,128)S(1)} %collective-permute-done.10) | copy-start | bytes 786436
  46.1 0.7 copy-start.10
  46.8 7.6 %collective-permute-start.4 = (f32[4,128,128]{2,1,0:T(8,128)S(1)}, f32[4,128,128]{2,1,0:T(8,128)}, u32[]{:S(2)}, u32[]{:S(2)}) collective-permute-start(f32[4,128,128]{2,1,0:T(8,128)S(1)} %get-tuple-element.18), channel_id=1, source_target_pairs={{0,8},{8,0},{4,12},{12,4},{16,24},{24,16},{20,28},{28,20},{1,9},{9... | collective-permute-start | bytes 786440 | tf_op jit(solution)/shard_map/ppermute | solution.py:198
  54.4 21.6 %collective-permute-start.12 = (f32[4,128,128]{2,1,0:T(8,128)}, f32[4,128,128]{2,1,0:T(8,128)}, u32[]{:S(2)}, u32[]{:S(2)}) collective-permute-start(f32[4,128,128]{2,1,0:T(8,128)} %collective-permute-done.4), channel_id=1, source_target_pairs={{0,2},{1,3},{2,0},{3,1},{4,6},{5,7},{6,4},{7,5},{8,10},{9,11},{10,... | collective-permute-start | bytes 786440 | tf_op jit(solution)/shard_map/ppermute | solution.py:203
  74.5 16.9 %collective-permute-start.14 = (f32[4,128,128]{2,1,0:T(8,128)}, f32[4,128,128]{2,1,0:T(8,128)}, u32[]{:S(2)}, u32[]{:S(2)}) collective-permute-start(f32[4,128,128]{2,1,0:T(8,128)} %collective-permute-done.4), channel_id=1, source_target_pairs={{0,1},{1,0},{2,3},{3,2},{4,5},{5,4},{6,7},{7,6},{8,9},{9,8},{10,11... | collective-permute-start | bytes 786440 | tf_op jit(solution)/shard_map/ppermute | solution.py:203
  76.0 15.4 %collective-permute-start.13 = (f32[4,128,128]{2,1,0:T(8,128)}, f32[4,128,128]{2,1,0:T(8,128)}, u32[]{:S(2)}, u32[]{:S(2)}) collective-permute-start(f32[4,128,128]{2,1,0:T(8,128)} %collective-permute-done.12), channel_id=1, source_target_pairs={{0,1},{1,0},{2,3},{3,2},{4,5},{5,4},{6,7},{7,6},{8,9},{9,8},{10,11... | collective-permute-start | bytes 786440 | tf_op jit(solution)/shard_map/ppermute | solution.py:203
  90.0 5.4 %copy-start.7 = (f32[1,4,128,128]{3,2,1,0:T(8,128)S(1)}, f32[1,4,128,128]{3,2,1,0:T(8,128)}, u32[]{:S(2)}) copy-start(f32[1,4,128,128]{3,2,1,0:T(8,128)} %get-tuple-element.7) | copy-start | bytes 786436
  90.0 5.4 %copy-start.8 = (f32[1,4,128,128]{3,2,1,0:T(8,128)S(1)}, f32[1,4,128,128]{3,2,1,0:T(8,128)}, u32[]{:S(2)}) copy-start(f32[1,4,128,128]{3,2,1,0:T(8,128)} %get-tuple-element.8) | copy-start | bytes 786436
  90.0 5.4 %copy-start.9 = (f32[1,4,128,128]{3,2,1,0:T(8,128)S(1)}, f32[1,4,128,128]{3,2,1,0:T(8,128)}, u32[]{:S(2)}) copy-start(f32[1,4,128,128]{3,2,1,0:T(8,128)} %get-tuple-element.9) | copy-start | bytes 786436
  91.4 27.2 %copy-start.2 = (bf16[1,16,128,128]{3,2,1,0:T(8,128)(2,1)S(1)}, bf16[1,16,128,128]{3,2,1,0:T(8,128)(2,1)}, u32[]{:S(2)}) copy-start(bf16[1,16,128,128]{3,2,1,0:T(8,128)(2,1)} %get-tuple-element.5) | copy-start | bytes 1572868
  92.9 16.6 %collective-permute-start.5 = (f32[4,128,128]{2,1,0:T(8,128)S(1)}, f32[4,128,128]{2,1,0:T(8,128)}, u32[]{:S(2)}, u32[]{:S(2)}) collective-permute-start(f32[4,128,128]{2,1,0:T(8,128)S(1)} %get-tuple-element.19), channel_id=1, source_target_pairs={{0,16},{4,20},{8,24},{12,28},{1,17},{5,21},{9,25},{13,29},{2,18},{... | collective-permute-start | bytes 786440 | tf_op jit(solution)/shard_map/ppermute | solution.py:198
  109.6 7.7 %collective-permute-start.6 = (f32[4,128,128]{2,1,0:T(8,128)}, f32[4,128,128]{2,1,0:T(8,128)}, u32[]{:S(2)}, u32[]{:S(2)}) collective-permute-start(f32[4,128,128]{2,1,0:T(8,128)} %collective-permute-done.5), channel_id=1, source_target_pairs={{0,2},{1,3},{2,0},{3,1},{4,6},{5,7},{6,4},{7,5},{8,10},{9,11},{10,... | collective-permute-start | bytes 786440 | tf_op jit(solution)/shard_map/ppermute | solution.py:203
  111.0 24.2 %collective-permute-start.8 = (f32[4,128,128]{2,1,0:T(8,128)}, f32[4,128,128]{2,1,0:T(8,128)}, u32[]{:S(2)}, u32[]{:S(2)}) collective-permute-start(f32[4,128,128]{2,1,0:T(8,128)} %collective-permute-done.5), channel_id=1, source_target_pairs={{0,1},{1,0},{2,3},{3,2},{4,5},{5,4},{6,7},{7,6},{8,9},{9,8},{10,11... | collective-permute-start | bytes 786440 | tf_op jit(solution)/shard_map/ppermute | solution.py:203
  117.3 17.9 %collective-permute-start.7 = (f32[4,128,128]{2,1,0:T(8,128)}, f32[4,128,128]{2,1,0:T(8,128)}, u32[]{:S(2)}, u32[]{:S(2)}) collective-permute-start(f32[4,128,128]{2,1,0:T(8,128)} %collective-permute-done.6), channel_id=1, source_target_pairs={{0,1},{1,0},{2,3},{3,2},{4,5},{5,4},{6,7},{7,6},{8,9},{9,8},{10,11... | collective-permute-start | bytes 786440 | tf_op jit(solution)/shard_map/ppermute | solution.py:203
where the time goes:
time: 150 us
  Pallas kernels  59.2 us (39%)
  waiting for transfers between devices  54.1 us (36%)
  starting transfers between devices  16.1 us (11%)
  other arithmetic  13.5 us (9%)
  local copies, waits for them, and re-layouts  6.4 us (4%)
    ppermute x6, waiting for transfers between devices, swap(): return lax.ppermute(block, axis, route)  43.6 us
    pallas_call x4, Pallas kernels, local_part(): pl.pallas_call(functools.partial(local_kernel, scale, rows, group), grid=...  28.1 us
    pallas_call x2, Pallas kernels, cross_all(): pl.pallas_call(functools.partial(cross_kernel, scale, rows, first_level,...  25.9 us
    ppermute x9, waiting for transfers between devices, to_offset(): return lax.ppermute(block, axis, [(s, s ^ offset) for s in range(count)])  10.6 us
    ppermute x9, starting transfers between devices, to_offset(): return lax.ppermute(block, axis, [(s, s ^ offset) for s in range(count)])  10 us
    concatenate x6, other arithmetic, shards(): sibs.append(jnp.concatenate(full, axis=0))  6.8 us
    unnamed x25, local copies, waits for them, and re-layouts  6.36 us
    ppermute x6, starting transfers between devices, swap(): return lax.ppermute(block, axis, route)  6.06 us
  transfers between devices with their start and end apart: 15, of which 9 were waited for; matrix products, arithmetic and copies ran while one was open for 7% of the time, Pallas kernels for 29%

commit v1 on v0

--- a/solution.py
+++ b/solution.py
@@ -82,7 +82,7 @@
                 (((1,), (1,)), ((), ())), preferred_element_type=jnp.float32,
             )
             s = s * scale
-            mix = m_ref[j, r0:r0 + TQ, :]
+            mix = m_ref[j, :, r0:r0 + TQ].T
             pieces = []
             for b in range(a):
                 level = inner + (a ^ b).bit_length() - 1
@@ -103,7 +103,7 @@
     head_count = mix_t.shape[0]
     dk = queries.shape[1] // head_count
     dv = values.shape[1] // head_count
-    levels = mix_t.shape[2]
+    levels = mix_t.shape[1]
     blocks = rows // TQ
     tiles = blocks * (blocks + 1) // 2
     base = first // group
@@ -111,7 +111,7 @@
         pl.BlockSpec((rows, dk * group), lambda h: (0, h + base)),
         pl.BlockSpec((rows, dk * group), lambda h: (0, h + base)),
         pl.BlockSpec((rows, dv * group), lambda h: (0, h + base)),
-        pl.BlockSpec((group, rows, levels), lambda h: (h + base, 0, 0)),
+        pl.BlockSpec((group, levels, rows), lambda h: (h + base, 0, 0)),
         pl.BlockSpec(masks.shape, lambda h: (0, 0, 0)),
     ]
     operands = [queries, keys, values, mix_t, masks]
@@ -148,7 +148,7 @@
                 q_ref[r0:r0 + TQ, j * dk:(j + 1) * dk], sib,
                 preferred_element_type=jnp.float32,
             )
-            mix = m_ref[j, r0:r0 + TQ, :]
+            mix = m_ref[j, :, r0:r0 + TQ].T
             cross = jnp.zeros((TQ, dv), jnp.float32)
             for b in range(bits):
                 w = mix[:, first_level + b:first_level + b + 1] * scale
@@ -163,7 +163,7 @@
     head_count = mix_t.shape[0]
     dk = queries.shape[1] // head_count
     dv = sibs.shape[3]
-    levels = mix_t.shape[2]
+    levels = mix_t.shape[1]
     bits = sibs.shape[0]
     return pl.pallas_call(
         functools.partial(cross_kernel, scale, rows, first_level, group),
@@ -171,7 +171,7 @@
         in_specs=[
             pl.BlockSpec((rows, dk * group), lambda g: (0, g)),
             pl.BlockSpec((bits, group, dk, dv), lambda g: (0, g, 0, 0)),
-            pl.BlockSpec((group, rows, levels), lambda g: (g, 0, 0)),
+            pl.BlockSpec((group, levels, rows), lambda g: (g, 0, 0)),
             pl.BlockSpec((rows, dv * group), lambda g: (0, g)),
         ],
         out_specs=pl.BlockSpec((rows, dv * group), lambda g: (0, g)),
@@ -209,7 +209,8 @@
     dk = queries.shape[1] // head_count
     scale = dk ** (-0.5)
     level_count = (rows // SPAN).bit_length()
-    mix_t = mixing.transpose(1, 2, 0)
+    pad = -mixing.shape[0] % 8
+    mix_t = jnp.pad(mixing, ((0, pad), (0, 0), (0, 0))).transpose(1, 0, 2)
     masks = jnp.asarray(level_masks(TQ, level_count))
 
     state = own_state(keys, values, head_count)
@@ -266,11 +267,9 @@
         sibs.append(jnp.concatenate(full, axis=0))
         flags.append(ctx_place >> bit & 1)
 
-    rounded = [
-        (flags[i].astype(jnp.float32) * sibs[i]).astype(jnp.bfloat16) for i in range(len(sibs))
-    ]
-    early = jnp.stack(rounded[:-1])
-    last = rounded[-1][None]
+    rounded = jnp.stack(
+        [(flags[i].astype(jnp.float32) * sibs[i]).astype(jnp.bfloat16) for i in range(len(sibs))]
+    )
 
     per = head_count // CHUNKS
     local = None
@@ -278,10 +277,7 @@
         local = local_part(
             queries, keys, values, mix_t, masks, c * per, per, LOCAL_GROUP, scale, local
         )
-    out = cross_all(queries, early, mix_t, local, scale, level_count, CROSS_GROUP)
-    return cross_all(
-        queries, last, mix_t, out, scale, level_count + len(rounded) - 1, CROSS_GROUP
-    )
+    return cross_all(queries, rounded, mix_t, local, scale, level_count, CROSS_GROUP)
 
 
 def solution(mesh):

time: 150 us -> 138 us (0.920)
  Pallas kernels: 59.2 us -> 54.3 us
  local copies, waits for them, and re-layouts: 6.4 us -> 2.51 us
  waiting for transfers between devices: 54.1 us -> 51.6 us
    pallas_call x2 -> x1, Pallas kernels: 25.9 us -> 17.8 us  [cross_all(): pl.pallas_call(functools.partial(cross_kernel, scale, rows, first_level,...]
    concatenate x6 -> x4, other arithmetic: 6.8 us -> 1.6 us  [shards(): sibs.append(jnp.concatenate(full, axis=0))]
    unnamed x25 -> x33, local copies, waits for them, and re-layouts: 6.36 us -> 1.37 us
    unnamed x0 -> x4, other arithmetic: none -> 4.91 us
    pallas_call x4, Pallas kernels: 28.1 us -> 31.3 us  [local_part(): pl.pallas_call(functools.partial(local_kernel, scale, rows, group), grid=...]
    another operation x2 -> x1, other arithmetic: 3.9 us -> 0.93 us  [shards(): jnp.stack([(flags[i].astype(jnp.float32) * sibs[i]).astype(jnp.bfloat16)...]
    convert_element_type x4 -> x0, other arithmetic: 2.62 us -> none  [shards(): (flags[i].astype(jnp.float32) * sibs[i]).astype(jnp.bfloat16)]
    ppermute x6, waiting for transfers between devices: 43.6 us -> 41.3 us  [swap(): return lax.ppermute(block, axis, route)]
  transfers between devices with their start and end apart: 15 -> 15, of which waited for: 9 -> 9; matrix products, arithmetic and copies ran while one was open for 7% -> 6% of each run, Pallas kernels for 29% -> 23%
where the time goes in v1:
time: 138 us; the launch traced here: 137 us
  Pallas kernels  54.3 us (39%)
  waiting for transfers between devices  51.6 us (37%)
  starting transfers between devices  16.2 us (12%)
  other arithmetic  12.4 us (9%)
  local copies, waits for them, and re-layouts  2.51 us (2%)
    ppermute x6, waiting for transfers between devices, swap(): return lax.ppermute(block, axis, route)  41.3 us
    pallas_call x4, Pallas kernels, local_part(): pl.pallas_call(functools.partial(local_kernel, scale, rows, group), grid=...  31.3 us
    pallas_call x1, Pallas kernels, cross_all(): pl.pallas_call(functools.partial(cross_kernel, scale, rows, first_level,...  17.8 us
    ppermute x9, waiting for transfers between devices, to_offset(): return lax.ppermute(block, axis, [(s, s ^ offset) for s in range(count)])  10.3 us
    ppermute x9, starting transfers between devices, to_offset(): return lax.ppermute(block, axis, [(s, s ^ offset) for s in range(count)])  10 us
    ppermute x6, starting transfers between devices, swap(): return lax.ppermute(block, axis, route)  6.2 us
    pallas_call x1, Pallas kernels, own_state(): pl.pallas_call(functools.partial(state_kernel, head_count), grid=(rows //...  5.25 us
    unnamed x4, other arithmetic  4.91 us
  transfers between devices with their start and end apart: 15, of which 9 were waited for; matrix products, arithmetic and copies ran while one was open for 6% of the time, Pallas kernels for 23%

profile of v1, /device:TPU:25, one launch (start us, length us, event | category | flops | bytes accessed | tf_op | source)
XLA Modules:
  0.0 137.2 jit_solution(7700866237096982965)
XLA Ops:
  0.0 5.2 %shard_map.55 = f32[16,128,128]{2,1,0:T(8,128)} custom-call(bf16[1024,2048]{1,0:T(8,128)(2,1)} %k_ref.9, bf16[1024,2048]{1,0:T(8,128)(2,1)} %v_ref.9), custom_call_target="tpu_custom_call" | custom-call | flops 536870912 | bytes 9437184 | tf_op jit(solution)/shard_map/pallas_call | solution.py:51
  5.3 0.7 collective-permute-start
  5.9 2.5 %collective-permute-done = f32[16,128,128]{2,1,0:T(8,128)S(1)} collective-permute-done((f32[16,128,128]{2,1,0:T(8,128)}, f32[16,128,128]{2,1,0:T(8,128)S(1)}, u32[]{:S(2)}, u32[]{:S(2)}) %collective-permute-start) | collective-permute-done | bytes 1048608 | tf_op jit(solution)/shard_map/ppermute | solution.py:198
  8.4 1.7 %add.20 = f32[16,128,128]{2,1,0:T(8,128)S(1)} add(f32[16,128,128]{2,1,0:T(8,128)} %shard_map.55, f32[16,128,128]{2,1,0:T(8,128)S(1)} %collective-permute-done) | non-fusion elementwise | flops 262144 | bytes 3145728 | tf_op jit(solution)/shard_map/add | solution.py:242
  10.2 1.3 collective-permute-start.1
  11.5 11.9 %collective-permute-done.1 = f32[8,128,128]{2,1,0:T(8,128)S(1)} collective-permute-done((f32[8,128,128]{2,1,0:T(8,128)S(1)}, f32[8,128,128]{2,1,0:T(8,128)S(1)}, u32[]{:S(2)}, u32[]{:S(2)}) %collective-permute-start.1) | collective-permute-done | bytes 524320 | tf_op jit(solution)/shard_map/ppermute | solution.py:198
  23.4 1.2 collective-permute-start.2
  24.6 1.7 %collective-permute-done.2 = f32[8,128,128]{2,1,0:T(8,128)} collective-permute-done((f32[8,128,128]{2,1,0:T(8,128)S(1)}, f32[8,128,128]{2,1,0:T(8,128)}, u32[]{:S(2)}, u32[]{:S(2)}) %collective-permute-start.2) | collective-permute-done | bytes 524320 | tf_op jit(solution)/shard_map/ppermute | solution.py:198
  26.3 1.1 broadcast_select_fusion.1
  27.4 0.8 copy-done
  28.2 0.1 fusion.11
  28.3 0.1 copy-done.2
  28.4 1.2 collective-permute-start.3
  29.6 6.3 %collective-permute-done.3 = f32[4,128,128]{2,1,0:T(8,128)S(1)} collective-permute-done((f32[4,128,128]{2,1,0:T(8,128)S(1)}, f32[4,128,128]{2,1,0:T(8,128)S(1)}, u32[]{:S(2)}, u32[]{:S(2)}) %collective-permute-start.3) | collective-permute-done | bytes 262176 | tf_op jit(solution)/shard_map/ppermute | solution.py:198
  35.9 1.2 collective-permute-start.4
  37.1 1.5 %collective-permute-start.6 = (f32[4,128,128]{2,1,0:T(8,128)S(1)}, f32[4,128,128]{2,1,0:T(8,128)S(1)}, u32[]{:S(2)}, u32[]{:S(2)}) collective-permute-start(f32[4,128,128]{2,1,0:T(8,128)S(1)} %collective-permute-done.3), channel_id=1, source_target_pairs={{0,1},{1,0},{2,3},{3,2},{4,5},{5,4},{6,7},{7,6},{8,9},{9,8},{10,11... | collective-permute-start | bytes 786440 | tf_op jit(solution)/shard_map/ppermute | solution.py:203
  38.6 3.9 %collective-permute-done.4 = f32[4,128,128]{2,1,0:T(8,128)S(1)} collective-permute-done((f32[4,128,128]{2,1,0:T(8,128)S(1)}, f32[4,128,128]{2,1,0:T(8,128)S(1)}, u32[]{:S(2)}, u32[]{:S(2)}) %collective-permute-start.4) | collective-permute-done | bytes 262176 | tf_op jit(solution)/shard_map/ppermute | solution.py:203
  42.5 2.1 %collective-permute-start.5 = (f32[4,128,128]{2,1,0:T(8,128)S(1)}, f32[4,128,128]{2,1,0:T(8,128)S(1)}, u32[]{:S(2)}, u32[]{:S(2)}) collective-permute-start(f32[4,128,128]{2,1,0:T(8,128)S(1)} %collective-permute-done.4), channel_id=1, source_target_pairs={{0,1},{1,0},{2,3},{3,2},{4,5},{5,4},{6,7},{7,6},{8,9},{9,8},{10,11... | collective-permute-start | bytes 786440 | tf_op jit(solution)/shard_map/ppermute | solution.py:203
  44.6 1.2 collective-permute-done.5
  45.8 0.8 fusion.13
  46.6 0.2 collective-permute-start.7
  46.8 0.4 copy.10
  47.2 7.0 %collective-permute-done.7 = f32[4,128,128]{2,1,0:T(8,128)} collective-permute-done((f32[4,128,128]{2,1,0:T(8,128)S(1)}, f32[4,128,128]{2,1,0:T(8,128)}, u32[]{:S(2)}, u32[]{:S(2)}) %collective-permute-start.7) | collective-permute-done | bytes 262176 | tf_op jit(solution)/shard_map/ppermute | solution.py:198
  54.2 1.2 collective-permute-start.8
  55.4 1.1 pad_bitcast_fusion.m_ref
  56.5 7.9 %shard_map.56.rest_0_ = f32[1024,2048]{1,0:T(8,128)} custom-call(bf16[1024,2048]{1,0:T(8,128)(2,1)} %q_ref.9, bf16[1024,2048]{1,0:T(8,128)(2,1)} %k_ref.9, bf16[1024,2048]{1,0:T(8,128)(2,1)} %v_ref.9, f32[16,16,1024]{2,1,0:T(8,128)} %pad_bitcast_fusion.m_ref, f32[3,256,256]{2,1,0:T(8,128)} %constant.28.clone.c_ref), custom_call_target="tpu_custom_call" | custom-call | flops 1342177280 | bytes 5242880 | tf_op jit(solution)/shard_map/pallas_call | solution.py:123
  64.4 1.5 %collective-permute-start.10 = (f32[4,128,128]{2,1,0:T(8,128)}, f32[4,128,128]{2,1,0:T(8,128)}, u32[]{:S(2)}, u32[]{:S(2)}) collective-permute-start(f32[4,128,128]{2,1,0:T(8,128)} %collective-permute-done.7), channel_id=1, source_target_pairs={{0,1},{1,0},{2,3},{3,2},{4,5},{5,4},{6,7},{7,6},{8,9},{9,8},{10,11... | collective-permute-start | bytes 786440 | tf_op jit(solution)/shard_map/ppermute | solution.py:203
  65.9 0.1 collective-permute-start.9
  66.0 7.8 %shard_map.57.rest_0_ = f32[1024,2048]{1,0:T(8,128)} custom-call(bf16[1024,2048]{1,0:T(8,128)(2,1)} %q_ref.9, bf16[1024,2048]{1,0:T(8,128)(2,1)} %k_ref.9, bf16[1024,2048]{1,0:T(8,128)(2,1)} %v_ref.9, f32[16,16,1024]{2,1,0:T(8,128)} %pad_bitcast_fusion.m_ref, f32[3,256,256]{2,1,0:T(8,128)} %constant.28.clone.c_ref, ...), custom_call_target="tpu_custom_call", output_to_operand_aliasing={{}: (5, {})} | custom-call | flops 1342177280 | bytes 5242880 | tf_op jit(solution)/shard_map/pallas_call | solution.py:123
  73.8 7.8 %shard_map.58.rest_0_ = f32[1024,2048]{1,0:T(8,128)} custom-call(bf16[1024,2048]{1,0:T(8,128)(2,1)} %q_ref.9, bf16[1024,2048]{1,0:T(8,128)(2,1)} %k_ref.9, bf16[1024,2048]{1,0:T(8,128)(2,1)} %v_ref.9, f32[16,16,1024]{2,1,0:T(8,128)} %pad_bitcast_fusion.m_ref, f32[3,256,256]{2,1,0:T(8,128)} %constant.28.clone.c_ref, ...), custom_call_target="tpu_custom_call", output_to_operand_aliasing={{}: (5, {})} | custom-call | flops 1342177280 | bytes 5242880 | tf_op jit(solution)/shard_map/pallas_call | solution.py:123
  81.6 7.8 %shard_map.59.l_ref = f32[1024,2048]{1,0:T(8,128)} custom-call(bf16[1024,2048]{1,0:T(8,128)(2,1)} %q_ref.9, bf16[1024,2048]{1,0:T(8,128)(2,1)} %k_ref.9, bf16[1024,2048]{1,0:T(8,128)(2,1)} %v_ref.9, f32[16,16,1024]{2,1,0:T(8,128)} %pad_bitcast_fusion.m_ref, f32[3,256,256]{2,1,0:T(8,128)} %constant.28.clone.c_ref, ...), custom_call_target="tpu_custom_call", output_to_operand_aliasing={{}: (5, {})} | custom-call | flops 1342177280 | bytes 5242880 | tf_op jit(solution)/shard_map/pallas_call | solution.py:123
  89.4 1.2 fusion.12
  90.7 1.6 %collective-permute-start.11 = (f32[4,128,128]{2,1,0:T(8,128)S(1)}, f32[4,128,128]{2,1,0:T(8,128)S(1)}, u32[]{:S(2)}, u32[]{:S(2)}) collective-permute-start(f32[4,128,128]{2,1,0:T(8,128)S(1)} %get-tuple-element.16), channel_id=1, source_target_pairs={{0,16},{4,20},{8,24},{12,28},{1,17},{5,21},{9,25},{13,29},{2,18},{... | collective-permute-start | bytes 786440 | tf_op jit(solution)/shard_map/ppermute | solution.py:198
  92.3 2.1 %fusion.5 = bf16[5,16,128,128]{3,2,1,0:T(8,128)(2,1)} fusion(f32[16,128,128]{2,1,0:T(8,128)} %copy-done.4, f32[]{:T(128)S(6)} %convert_element_type.60), kind=kLoop, calls=%fused_computation.13 | loop fusion | flops 524287 | bytes 1572868
  94.4 0.9 fusion.9
  95.4 12.0 %collective-permute-done.11 = f32[4,128,128]{2,1,0:T(8,128)S(1)} collective-permute-done((f32[4,128,128]{2,1,0:T(8,128)S(1)}, f32[4,128,128]{2,1,0:T(8,128)S(1)}, u32[]{:S(2)}, u32[]{:S(2)}) %collective-permute-start.11) | collective-permute-done | bytes 262176 | tf_op jit(solution)/shard_map/ppermute | solution.py:198
  107.3 0.3 collective-permute-start.12
  107.7 0.1 select_bitcast_fusion.11
  107.8 0.9 fusion.8
  108.7 0.8 collective-permute-start.14
  109.5 5.2 %collective-permute-done.12 = f32[4,128,128]{2,1,0:T(8,128)S(1)} collective-permute-done((f32[4,128,128]{2,1,0:T(8,128)S(1)}, f32[4,128,128]{2,1,0:T(8,128)S(1)}, u32[]{:S(2)}, u32[]{:S(2)}) %collective-permute-start.12) | collective-permute-done | bytes 262176 | tf_op jit(solution)/shard_map/ppermute | solution.py:203
  114.7 1.3 collective-permute-start.13
  116.0 1.3 select_bitcast_fusion.7
  117.3 0.9 fusion.7
  118.3 0.1 select_bitcast_fusion.2
  118.3 0.1 select_bitcast_fusion.3
  118.5 0.9 fusion.6.s_ref
  119.4 17.8 %shard_map.60 = f32[1024,2048]{1,0:T(8,128)} custom-call(bf16[1024,2048]{1,0:T(8,128)(2,1)} %q_ref.9, bf16[5,16,128,128]{3,2,1,0:T(8,128)(2,1)} %fusion.6.s_ref, f32[16,16,1024]{2,1,0:T(8,128)} %pad_bitcast_fusion.m_ref, f32[1024,2048]{1,0:T(8,128)} %shard_map.59.l_ref), custom_call_target="tpu_custom_call", output_to_operand_aliasing={{}: (3, {})} | custom-call | flops 2684354560 | bytes 20971520 | tf_op jit(solution)/shard_map/pallas_call | solution.py:168
  (37 shorter events, 0.1 us)
Async XLA Ops:
  5.3 3.2 %collective-permute-start = (f32[16,128,128]{2,1,0:T(8,128)}, f32[16,128,128]{2,1,0:T(8,128)S(1)}, u32[]{:S(2)}, u32[]{:S(2)}) collective-permute-start(f32[16,128,128]{2,1,0:T(8,128)} %shard_map.55), channel_id=1, source_target_pairs={{0,1},{1,0},{2,3},{3,2},{4,5},{5,4},{6,7},{7,6},{8,9},{9,8},{10,11... | collective-permute-start | bytes 3145736 | tf_op jit(solution)/shard_map/ppermute | solution.py:198
  8.4 19.0 %copy-start.4 = (f32[16,128,128]{2,1,0:T(8,128)}, f32[16,128,128]{2,1,0:T(8,128)S(1)}, u32[]{:S(2)}) copy-start(f32[16,128,128]{2,1,0:T(8,128)S(1)} %collective-permute-done) | copy-start | bytes 3145732
  10.2 13.2 %collective-permute-start.1 = (f32[8,128,128]{2,1,0:T(8,128)S(1)}, f32[8,128,128]{2,1,0:T(8,128)S(1)}, u32[]{:S(2)}, u32[]{:S(2)}) collective-permute-start(f32[8,128,128]{2,1,0:T(8,128)S(1)} %constant_dynamic-slice_fusion), channel_id=1, source_target_pairs={{0,2},{2,0},{1,3},{3,1},{4,6},{6,4},{5,7},{7,5},{8,10},{10,8},{9,1... | collective-permute-start | bytes 1572872 | tf_op jit(solution)/shard_map/ppermute | solution.py:198
  23.4 2.9 %collective-permute-start.2 = (f32[8,128,128]{2,1,0:T(8,128)S(1)}, f32[8,128,128]{2,1,0:T(8,128)}, u32[]{:S(2)}, u32[]{:S(2)}) collective-permute-start(f32[8,128,128]{2,1,0:T(8,128)S(1)} %collective-permute-done.1), channel_id=1, source_target_pairs={{0,1},{1,0},{2,3},{3,2},{4,5},{5,4},{6,7},{7,6},{8,9},{9,8},{10,11... | collective-permute-start | bytes 1572872 | tf_op jit(solution)/shard_map/ppermute | solution.py:198
  24.6 22.2 %copy-start.15 = (f32[10,16,1024]{2,1,0:T(8,128)S(1)}, f32[10,16,1024]{2,1,0:T(8,128)}, u32[]{:S(2)}) copy-start(f32[10,16,1024]{2,1,0:T(8,128)} %param.8) | copy-start | bytes 1966084
  27.4 0.8 copy-start
  27.4 1.0 copy-start.2
  28.4 7.5 %collective-permute-start.3 = (f32[4,128,128]{2,1,0:T(8,128)S(1)}, f32[4,128,128]{2,1,0:T(8,128)S(1)}, u32[]{:S(2)}, u32[]{:S(2)}) collective-permute-start(f32[4,128,128]{2,1,0:T(8,128)S(1)} %fusion.11), channel_id=1, source_target_pairs={{0,4},{4,0},{8,12},{12,8},{16,20},{20,16},{24,28},{28,24},{1,5},{5... | collective-permute-start | bytes 786440 | tf_op jit(solution)/shard_map/ppermute | solution.py:198
  35.9 10.7 %copy-start.5 = (f32[4,128,128]{2,1,0:T(8,128)}, f32[4,128,128]{2,1,0:T(8,128)S(1)}, u32[]{:S(2)}) copy-start(f32[4,128,128]{2,1,0:T(8,128)S(1)} %collective-permute-done.3) | copy-start | bytes 786436
  35.9 6.6 %collective-permute-start.4 = (f32[4,128,128]{2,1,0:T(8,128)S(1)}, f32[4,128,128]{2,1,0:T(8,128)S(1)}, u32[]{:S(2)}, u32[]{:S(2)}) collective-permute-start(f32[4,128,128]{2,1,0:T(8,128)S(1)} %collective-permute-done.3), channel_id=1, source_target_pairs={{0,2},{1,3},{2,0},{3,1},{4,6},{5,7},{6,4},{7,5},{8,10},{9,11},{10,... | collective-permute-start | bytes 786440 | tf_op jit(solution)/shard_map/ppermute | solution.py:203
  37.1 7.5 %collective-permute-start.6 = (f32[4,128,128]{2,1,0:T(8,128)S(1)}, f32[4,128,128]{2,1,0:T(8,128)S(1)}, u32[]{:S(2)}, u32[]{:S(2)}) collective-permute-start(f32[4,128,128]{2,1,0:T(8,128)S(1)} %collective-permute-done.3), channel_id=1, source_target_pairs={{0,1},{1,0},{2,3},{3,2},{4,5},{5,4},{6,7},{7,6},{8,9},{9,8},{10,11... | collective-permute-start | bytes 786440 | tf_op jit(solution)/shard_map/ppermute | solution.py:203
  42.5 4.2 %copy-start.7 = (f32[4,128,128]{2,1,0:T(8,128)}, f32[4,128,128]{2,1,0:T(8,128)S(1)}, u32[]{:S(2)}) copy-start(f32[4,128,128]{2,1,0:T(8,128)S(1)} %collective-permute-done.4) | copy-start | bytes 786436
  42.5 3.2 %collective-permute-start.5 = (f32[4,128,128]{2,1,0:T(8,128)S(1)}, f32[4,128,128]{2,1,0:T(8,128)S(1)}, u32[]{:S(2)}, u32[]{:S(2)}) collective-permute-start(f32[4,128,128]{2,1,0:T(8,128)S(1)} %collective-permute-done.4), channel_id=1, source_target_pairs={{0,1},{1,0},{2,3},{3,2},{4,5},{5,4},{6,7},{7,6},{8,9},{9,8},{10,11... | collective-permute-start | bytes 786440 | tf_op jit(solution)/shard_map/ppermute | solution.py:203
  44.6 2.5 %copy-start.9 = (f32[4,128,128]{2,1,0:T(8,128)}, f32[4,128,128]{2,1,0:T(8,128)S(1)}, u32[]{:S(2)}) copy-start(f32[4,128,128]{2,1,0:T(8,128)S(1)} %collective-permute-done.6) | copy-start | bytes 786436
  45.8 8.4 %copy-start.11 = (f32[4,128,128]{2,1,0:T(8,128)}, f32[4,128,128]{2,1,0:T(8,128)S(1)}, u32[]{:S(2)}) copy-start(f32[4,128,128]{2,1,0:T(8,128)S(1)} %collective-permute-done.5) | copy-start | bytes 786436
  46.6 8.8 %copy-start.14 = (f32[4,128,128]{2,1,0:T(8,128)}, f32[4,128,128]{2,1,0:T(8,128)S(1)}, u32[]{:S(2)}) copy-start(f32[4,128,128]{2,1,0:T(8,128)S(1)} %get-tuple-element.18) | copy-start | bytes 786436
  46.6 7.6 %collective-permute-start.7 = (f32[4,128,128]{2,1,0:T(8,128)S(1)}, f32[4,128,128]{2,1,0:T(8,128)}, u32[]{:S(2)}, u32[]{:S(2)}) collective-permute-start(f32[4,128,128]{2,1,0:T(8,128)S(1)} %get-tuple-element.18), channel_id=1, source_target_pairs={{0,8},{8,0},{4,12},{12,4},{16,24},{24,16},{20,28},{28,20},{1,9},{9... | collective-permute-start | bytes 786440 | tf_op jit(solution)/shard_map/ppermute | solution.py:198
  54.2 11.8 %collective-permute-start.8 = (f32[4,128,128]{2,1,0:T(8,128)}, f32[4,128,128]{2,1,0:T(8,128)}, u32[]{:S(2)}, u32[]{:S(2)}) collective-permute-start(f32[4,128,128]{2,1,0:T(8,128)} %collective-permute-done.7), channel_id=1, source_target_pairs={{0,2},{1,3},{2,0},{3,1},{4,6},{5,7},{6,4},{7,5},{8,10},{9,11},{10,... | collective-permute-start | bytes 786440 | tf_op jit(solution)/shard_map/ppermute | solution.py:203
  64.4 25.0 %collective-permute-start.10 = (f32[4,128,128]{2,1,0:T(8,128)}, f32[4,128,128]{2,1,0:T(8,128)}, u32[]{:S(2)}, u32[]{:S(2)}) collective-permute-start(f32[4,128,128]{2,1,0:T(8,128)} %collective-permute-done.7), channel_id=1, source_target_pairs={{0,1},{1,0},{2,3},{3,2},{4,5},{5,4},{6,7},{7,6},{8,9},{9,8},{10,11... | collective-permute-start | bytes 786440 | tf_op jit(solution)/shard_map/ppermute | solution.py:203
  65.9 23.5 %collective-permute-start.9 = (f32[4,128,128]{2,1,0:T(8,128)}, f32[4,128,128]{2,1,0:T(8,128)}, u32[]{:S(2)}, u32[]{:S(2)}) collective-permute-start(f32[4,128,128]{2,1,0:T(8,128)} %collective-permute-done.8), channel_id=1, source_target_pairs={{0,1},{1,0},{2,3},{3,2},{4,5},{5,4},{6,7},{7,6},{8,9},{9,8},{10,11... | collective-permute-start | bytes 786440 | tf_op jit(solution)/shard_map/ppermute | solution.py:203
  89.3 5.1 %copy-start.1 = (f32[8,128,128]{2,1,0:T(8,128)S(1)}, f32[8,128,128]{2,1,0:T(8,128)}, u32[]{:S(2)}) copy-start(f32[8,128,128]{2,1,0:T(8,128)} %copy-done) | copy-start | bytes 1572868
  89.3 5.1 %copy-start.3 = (f32[8,128,128]{2,1,0:T(8,128)S(1)}, f32[8,128,128]{2,1,0:T(8,128)}, u32[]{:S(2)}) copy-start(f32[8,128,128]{2,1,0:T(8,128)} %copy-done.2) | copy-start | bytes 1572868
  89.3 18.3 %copy-start.6 = (f32[4,128,128]{2,1,0:T(8,128)S(1)}, f32[4,128,128]{2,1,0:T(8,128)}, u32[]{:S(2)}) copy-start(f32[4,128,128]{2,1,0:T(8,128)} %copy-done.5) | copy-start | bytes 786436
  89.4 18.3 %copy-start.8 = (f32[4,128,128]{2,1,0:T(8,128)S(1)}, f32[4,128,128]{2,1,0:T(8,128)}, u32[]{:S(2)}) copy-start(f32[4,128,128]{2,1,0:T(8,128)} %copy-done.7) | copy-start | bytes 786436
  89.4 18.3 %copy-start.10 = (f32[4,128,128]{2,1,0:T(8,128)S(1)}, f32[4,128,128]{2,1,0:T(8,128)}, u32[]{:S(2)}) copy-start(f32[4,128,128]{2,1,0:T(8,128)} %copy-done.9) | copy-start | bytes 786436
  89.4 18.3 %copy-start.12 = (f32[4,128,128]{2,1,0:T(8,128)S(1)}, f32[4,128,128]{2,1,0:T(8,128)}, u32[]{:S(2)}) copy-start(f32[4,128,128]{2,1,0:T(8,128)} %copy-done.11) | copy-start | bytes 786436
  90.7 17.2 %copy-start.13 = (f32[1,4,128,128]{3,2,1,0:T(8,128)S(1)}, f32[1,4,128,128]{3,2,1,0:T(8,128)}, u32[]{:S(2)}) copy-start(f32[1,4,128,128]{3,2,1,0:T(8,128)} %get-tuple-element.19) | copy-start | bytes 786436
  90.7 16.7 %collective-permute-start.11 = (f32[4,128,128]{2,1,0:T(8,128)S(1)}, f32[4,128,128]{2,1,0:T(8,128)S(1)}, u32[]{:S(2)}, u32[]{:S(2)}) collective-permute-start(f32[4,128,128]{2,1,0:T(8,128)S(1)} %get-tuple-element.16), channel_id=1, source_target_pairs={{0,16},{4,20},{8,24},{12,28},{1,17},{5,21},{9,25},{13,29},{2,18},{... | collective-permute-start | bytes 786440 | tf_op jit(solution)/shard_map/ppermute | solution.py:198
  107.3 7.4 %collective-permute-start.12 = (f32[4,128,128]{2,1,0:T(8,128)S(1)}, f32[4,128,128]{2,1,0:T(8,128)S(1)}, u32[]{:S(2)}, u32[]{:S(2)}) collective-permute-start(f32[4,128,128]{2,1,0:T(8,128)S(1)} %collective-permute-done.11), channel_id=1, source_target_pairs={{0,2},{1,3},{2,0},{3,1},{4,6},{5,7},{6,4},{7,5},{8,10},{9,11},{10,... | collective-permute-start | bytes 786440 | tf_op jit(solution)/shard_map/ppermute | solution.py:203
  108.7 9.5 %collective-permute-start.14 = (f32[4,128,128]{2,1,0:T(8,128)S(1)}, f32[4,128,128]{2,1,0:T(8,128)S(1)}, u32[]{:S(2)}, u32[]{:S(2)}) collective-permute-start(f32[4,128,128]{2,1,0:T(8,128)S(1)} %collective-permute-done.11), channel_id=1, source_target_pairs={{0,1},{1,0},{2,3},{3,2},{4,5},{5,4},{6,7},{7,6},{8,9},{9,8},{10,11... | collective-permute-start | bytes 786440 | tf_op jit(solution)/shard_map/ppermute | solution.py:203
  114.7 3.6 %collective-permute-start.13 = (f32[4,128,128]{2,1,0:T(8,128)S(1)}, f32[4,128,128]{2,1,0:T(8,128)S(1)}, u32[]{:S(2)}, u32[]{:S(2)}) collective-permute-start(f32[4,128,128]{2,1,0:T(8,128)S(1)} %collective-permute-done.12), channel_id=1, source_target_pairs={{0,1},{1,0},{2,3},{3,2},{4,5},{5,4},{6,7},{7,6},{8,9},{9,8},{10,11... | collective-permute-start | bytes 786440 | tf_op jit(solution)/shard_map/ppermute | solution.py:203

commit v2 on v0

--- a/solution.py
+++ b/solution.py
@@ -250,7 +250,7 @@
             quarter = quarter + got
 
     for bit in range(ctx_bits):
-        part = ctx_sibs[bit]
+        part = lax.optimization_barrier(ctx_sibs[bit])
         parts = {0: part}
         for offset in range(1, seq_count):
             if offset & 1 and offset > 1:
@@ -266,11 +266,9 @@
         sibs.append(jnp.concatenate(full, axis=0))
         flags.append(ctx_place >> bit & 1)
 
-    rounded = [
-        (flags[i].astype(jnp.float32) * sibs[i]).astype(jnp.bfloat16) for i in range(len(sibs))
-    ]
-    early = jnp.stack(rounded[:-1])
-    last = rounded[-1][None]
+    rounded = jnp.stack(
+        [(flags[i].astype(jnp.float32) * sibs[i]).astype(jnp.bfloat16) for i in range(len(sibs))]
+    )
 
     per = head_count // CHUNKS
     local = None
@@ -278,10 +276,7 @@
         local = local_part(
             queries, keys, values, mix_t, masks, c * per, per, LOCAL_GROUP, scale, local
         )
-    out = cross_all(queries, early, mix_t, local, scale, level_count, CROSS_GROUP)
-    return cross_all(
-        queries, last, mix_t, out, scale, level_count + len(rounded) - 1, CROSS_GROUP
-    )
+    return cross_all(queries, rounded, mix_t, local, scale, level_count, CROSS_GROUP)
 
 
 def solution(mesh):

time: 150 us -> 116 us (0.77)
  waiting for transfers between devices: 54.1 us -> 31 us
  Pallas kernels: 59.2 us -> 49.9 us
  starting transfers between devices: 16.1 us -> 11.7 us
  other arithmetic: 13.5 us -> 16.8 us
    ppermute x6, waiting for transfers between devices: 43.6 us -> 26.8 us  [swap(): return lax.ppermute(block, axis, route)]
    pallas_call x2 -> x1, Pallas kernels: 25.9 us -> 16.6 us  [cross_all(): pl.pallas_call(functools.partial(cross_kernel, scale, rows, first_level,...]
    ppermute x9, waiting for transfers between devices: 10.6 us -> 4.24 us  [to_offset(): return lax.ppermute(block, axis, [(s, s ^ offset) for s in range(count)])]
    unnamed x0 -> x4, other arithmetic: none -> 5.01 us
    ppermute x9, starting transfers between devices: 10 us -> 5.67 us  [to_offset(): return lax.ppermute(block, axis, [(s, s ^ offset) for s in range(count)])]
    another operation x2 -> x1, other arithmetic: 3.9 us -> 0.93 us  [shards(): jnp.stack([(flags[i].astype(jnp.float32) * sibs[i]).astype(jnp.bfloat16)...]
    add x0 -> x2, other arithmetic: none -> 2.83 us  [shards(): quarter = quarter + got]
    convert_element_type x4 -> x0, other arithmetic: 2.62 us -> none  [shards(): (flags[i].astype(jnp.float32) * sibs[i]).astype(jnp.bfloat16)]
  transfers between devices with their start and end apart: 15 -> 15, of which waited for: 9 -> 5; matrix products, arithmetic and copies ran while one was open for 7% -> 13% of each run, Pallas kernels for 29% -> 24%
where the time goes in v2:
time: 116 us; the launch traced here: 115 us
  Pallas kernels  49.9 us (43%)
  waiting for transfers between devices  31 us (27%)
  other arithmetic  16.8 us (14%)
  starting transfers between devices  11.7 us (10%)
  local copies, waits for them, and re-layouts  5.6 us (5%)
    pallas_call x4, Pallas kernels, local_part(): pl.pallas_call(functools.partial(local_kernel, scale, rows, group), grid=...  28 us
    ppermute x6, waiting for transfers between devices, swap(): return lax.ppermute(block, axis, route)  26.8 us
    pallas_call x1, Pallas kernels, cross_all(): pl.pallas_call(functools.partial(cross_kernel, scale, rows, first_level,...  16.6 us
    ppermute x6, starting transfers between devices, swap(): return lax.ppermute(block, axis, route)  6.06 us
    ppermute x9, starting transfers between devices, to_offset(): return lax.ppermute(block, axis, [(s, s ^ offset) for s in range(count)])  5.67 us
    unnamed x13, local copies, waits for them, and re-layouts  5.55 us
    pallas_call x1, Pallas kernels, own_state(): pl.pallas_call(functools.partial(state_kernel, head_count), grid=(rows //...  5.25 us
    unnamed x4, other arithmetic  5.01 us
  transfers between devices with their start and end apart: 15, of which 5 were waited for; matrix products, arithmetic and copies ran while one was open for 13% of the time, Pallas kernels for 24%

profile of v2, /device:TPU:25, one launch (start us, length us, event | category | flops | bytes accessed | tf_op | source)
XLA Modules:
  0.0 115.2 jit_solution(5512691474418423271)
XLA Ops:
  0.0 5.2 %shard_map.55 = f32[16,128,128]{2,1,0:T(8,128)} custom-call(bf16[1024,2048]{1,0:T(8,128)(2,1)} %k_ref.9, bf16[1024,2048]{1,0:T(8,128)(2,1)} %v_ref.9), custom_call_target="tpu_custom_call" | custom-call | flops 536870912 | bytes 9437184 | tf_op jit(solution)/shard_map/pallas_call | solution.py:51
  5.3 0.7 collective-permute-start
  5.9 2.5 %collective-permute-done = f32[16,128,128]{2,1,0:T(8,128)S(1)} collective-permute-done((f32[16,128,128]{2,1,0:T(8,128)}, f32[16,128,128]{2,1,0:T(8,128)S(1)}, u32[]{:S(2)}, u32[]{:S(2)}) %collective-permute-start) | collective-permute-done | bytes 1048608 | tf_op jit(solution)/shard_map/ppermute | solution.py:198
  8.4 1.7 %add.18 = f32[16,128,128]{2,1,0:T(8,128)S(1)} add(f32[16,128,128]{2,1,0:T(8,128)} %shard_map.55, f32[16,128,128]{2,1,0:T(8,128)S(1)} %collective-permute-done) | non-fusion elementwise | flops 262144 | bytes 3145728 | tf_op jit(solution)/shard_map/add | solution.py:241
  10.1 0.0 copy-start.5
  10.2 1.3 %collective-permute-start.1 = (f32[8,128,128]{2,1,0:T(8,128)S(1)}, f32[8,128,128]{2,1,0:T(8,128)S(1)}, u32[]{:S(2)}, u32[]{:S(2)}) collective-permute-start(f32[8,128,128]{2,1,0:T(8,128)S(1)} %constant_dynamic-slice_fusion), channel_id=1, source_target_pairs={{0,2},{2,0},{1,3},{3,1},{4,6},{6,4},{5,7},{7,5},{8,10},{10,8},{9,1... | collective-permute-start | bytes 1572872 | tf_op jit(solution)/shard_map/ppermute | solution.py:198
  11.5 11.9 %collective-permute-done.1 = f32[8,128,128]{2,1,0:T(8,128)S(1)} collective-permute-done((f32[8,128,128]{2,1,0:T(8,128)S(1)}, f32[8,128,128]{2,1,0:T(8,128)S(1)}, u32[]{:S(2)}, u32[]{:S(2)}) %collective-permute-start.1) | collective-permute-done | bytes 524320 | tf_op jit(solution)/shard_map/ppermute | solution.py:198
  23.4 1.2 %collective-permute-start.2 = (f32[8,128,128]{2,1,0:T(8,128)S(1)}, f32[8,128,128]{2,1,0:T(8,128)}, u32[]{:S(2)}, u32[]{:S(2)}) collective-permute-start(f32[8,128,128]{2,1,0:T(8,128)S(1)} %collective-permute-done.1), channel_id=1, source_target_pairs={{0,1},{1,0},{2,3},{3,2},{4,5},{5,4},{6,7},{7,6},{8,9},{9,8},{10,11... | collective-permute-start | bytes 1572872 | tf_op jit(solution)/shard_map/ppermute | solution.py:198
  24.6 1.7 %collective-permute-done.2 = f32[8,128,128]{2,1,0:T(8,128)} collective-permute-done((f32[8,128,128]{2,1,0:T(8,128)S(1)}, f32[8,128,128]{2,1,0:T(8,128)}, u32[]{:S(2)}, u32[]{:S(2)}) %collective-permute-start.2) | collective-permute-done | bytes 524320 | tf_op jit(solution)/shard_map/ppermute | solution.py:198
  26.3 1.1 broadcast_select_fusion.1
  27.5 0.8 copy-done
  28.3 0.8 fusion.11
  29.0 1.2 %collective-permute-start.3 = (f32[4,128,128]{2,1,0:T(8,128)}, f32[4,128,128]{2,1,0:T(8,128)}, u32[]{:S(2)}, u32[]{:S(2)}) collective-permute-start(f32[4,128,128]{2,1,0:T(8,128)} %fusion.11), channel_id=1, source_target_pairs={{0,4},{4,0},{8,12},{12,8},{16,20},{20,16},{24,28},{28,24},{1,5},{5... | collective-permute-start | bytes 786440 | tf_op jit(solution)/shard_map/ppermute | solution.py:198
  30.3 4.7 %copy.10 = f32[10,16,1024]{0,2,1:T(8,128)} copy(f32[10,16,1024]{2,1,0:T(8,128)S(1)} %copy-done.5) | data formatting | bytes 1310720 | tf_op args[3]
  35.0 7.1 %shard_map.56.rest_0_ = f32[1024,2048]{1,0:T(8,128)} custom-call(bf16[1024,2048]{1,0:T(8,128)(2,1)} %q_ref.9, bf16[1024,2048]{1,0:T(8,128)(2,1)} %k_ref.9, bf16[1024,2048]{1,0:T(8,128)(2,1)} %v_ref.9, f32[16,1024,10]{2,1,0:T(8,128)} %bitcast.31, f32[3,256,256]{2,1,0:T(8,128)} %constant.27.clone.c_ref), custom_call_target="tpu_custom_call" | custom-call | flops 1342177280 | bytes 5242880 | tf_op jit(solution)/shard_map/pallas_call | solution.py:123
  42.1 1.8 %add.22 = f32[4,128,128]{2,1,0:T(8,128)} add(f32[4,128,128]{2,1,0:T(8,128)} %fusion.11, f32[4,128,128]{2,1,0:T(8,128)} %collective-permute-done.3) | non-fusion elementwise | flops 65536 | bytes 786432 | tf_op jit(solution)/shard_map/add | solution.py:250
  43.9 0.2 collective-permute-start.7
  44.1 1.2 %collective-permute-start.4 = (f32[4,128,128]{2,1,0:T(8,128)}, f32[4,128,128]{2,1,0:T(8,128)}, u32[]{:S(2)}, u32[]{:S(2)}) collective-permute-start(f32[4,128,128]{2,1,0:T(8,128)} %collective-permute-done.3), channel_id=1, source_target_pairs={{0,2},{1,3},{2,0},{3,1},{4,6},{5,7},{6,4},{7,5},{8,10},{9,11},{10,... | collective-permute-start | bytes 786440 | tf_op jit(solution)/shard_map/ppermute | solution.py:203
  45.3 7.0 %shard_map.57.rest_0_ = f32[1024,2048]{1,0:T(8,128)} custom-call(bf16[1024,2048]{1,0:T(8,128)(2,1)} %q_ref.9, bf16[1024,2048]{1,0:T(8,128)(2,1)} %k_ref.9, bf16[1024,2048]{1,0:T(8,128)(2,1)} %v_ref.9, f32[16,1024,10]{2,1,0:T(8,128)} %bitcast.32, f32[3,256,256]{2,1,0:T(8,128)} %constant.27.clone.c_ref, ...), custom_call_target="tpu_custom_call", output_to_operand_aliasing={{}: (5, {})} | custom-call | flops 1342177280 | bytes 5242880 | tf_op jit(solution)/shard_map/pallas_call | solution.py:123
  52.2 7.0 %shard_map.58.rest_0_ = f32[1024,2048]{1,0:T(8,128)} custom-call(bf16[1024,2048]{1,0:T(8,128)(2,1)} %q_ref.9, bf16[1024,2048]{1,0:T(8,128)(2,1)} %k_ref.9, bf16[1024,2048]{1,0:T(8,128)(2,1)} %v_ref.9, f32[16,1024,10]{2,1,0:T(8,128)} %bitcast.33, f32[3,256,256]{2,1,0:T(8,128)} %constant.27.clone.c_ref, ...), custom_call_target="tpu_custom_call", output_to_operand_aliasing={{}: (5, {})} | custom-call | flops 1342177280 | bytes 5242880 | tf_op jit(solution)/shard_map/pallas_call | solution.py:123
  59.2 7.0 %shard_map.59.l_ref = f32[1024,2048]{1,0:T(8,128)} custom-call(bf16[1024,2048]{1,0:T(8,128)(2,1)} %q_ref.9, bf16[1024,2048]{1,0:T(8,128)(2,1)} %k_ref.9, bf16[1024,2048]{1,0:T(8,128)(2,1)} %v_ref.9, f32[16,1024,10]{2,1,0:T(8,128)} %bitcast.34, f32[3,256,256]{2,1,0:T(8,128)} %constant.27.clone.c_ref, ...), custom_call_target="tpu_custom_call", output_to_operand_aliasing={{}: (5, {})} | custom-call | flops 1342177280 | bytes 5242880 | tf_op jit(solution)/shard_map/pallas_call | solution.py:123
  66.2 1.3 %collective-permute-start.6 = (f32[4,128,128]{2,1,0:T(8,128)}, f32[4,128,128]{2,1,0:T(8,128)S(1)}, u32[]{:S(2)}, u32[]{:S(2)}) collective-permute-start(f32[4,128,128]{2,1,0:T(8,128)} %collective-permute-done.3), channel_id=1, source_target_pairs={{0,1},{1,0},{2,3},{3,2},{4,5},{5,4},{6,7},{7,6},{8,9},{9,8},{10,11... | collective-permute-start | bytes 786440 | tf_op jit(solution)/shard_map/ppermute | solution.py:203
  67.5 1.1 add.23
  68.5 1.5 %collective-permute-start.11 = (f32[4,128,128]{2,1,0:T(8,128)S(1)}, f32[4,128,128]{2,1,0:T(8,128)S(1)}, u32[]{:S(2)}, u32[]{:S(2)}) collective-permute-start(f32[4,128,128]{2,1,0:T(8,128)S(1)} %add.23), channel_id=1, source_target_pairs={{0,16},{4,20},{8,24},{12,28},{1,17},{5,21},{9,25},{13,29},{2,18},{... | collective-permute-start | bytes 786440 | tf_op jit(solution)/shard_map/ppermute | solution.py:198
  70.0 0.3 collective-permute-start.8
  70.3 0.4 collective-permute-start.5
  70.7 2.2 %fusion.5 = bf16[5,16,128,128]{3,2,1,0:T(8,128)(2,1)} fusion(f32[16,128,128]{2,1,0:T(8,128)} %copy-done.4, f32[]{:T(128)S(6)} %convert_element_type.58), kind=kLoop, calls=%fused_computation.12 | loop fusion | flops 524287 | bytes 1572868
  72.9 0.9 fusion.9
  73.8 0.1 collective-permute-start.10
  74.0 10.7 %collective-permute-done.11 = f32[4,128,128]{2,1,0:T(8,128)S(1)} collective-permute-done((f32[4,128,128]{2,1,0:T(8,128)S(1)}, f32[4,128,128]{2,1,0:T(8,128)S(1)}, u32[]{:S(2)}, u32[]{:S(2)}) %collective-permute-start.11) | collective-permute-done | bytes 262176 | tf_op jit(solution)/shard_map/ppermute | solution.py:198
  84.7 0.9 collective-permute-start.14
  85.7 0.0 collective-permute-done.6
  85.7 0.3 collective-permute-start.12
  85.9 0.0 collective-permute-done.8
  85.9 0.3 collective-permute-start.9
  86.2 1.1 select_bitcast_fusion.11
  87.4 1.0 select_bitcast_fusion.10
  88.4 0.9 fusion.8
  89.3 4.2 %collective-permute-done.12 = f32[4,128,128]{2,1,0:T(8,128)S(1)} collective-permute-done((f32[4,128,128]{2,1,0:T(8,128)S(1)}, f32[4,128,128]{2,1,0:T(8,128)S(1)}, u32[]{:S(2)}, u32[]{:S(2)}) %collective-permute-start.12) | collective-permute-done | bytes 262176 | tf_op jit(solution)/shard_map/ppermute | solution.py:203
  93.5 0.9 collective-permute-start.13
  94.4 0.0 collective-permute-done.9
  94.4 1.1 select_bitcast_fusion.7
  95.5 1.0 select_bitcast_fusion.6
  96.5 0.9 fusion.7
  97.5 0.1 select_bitcast_fusion.2
  97.5 0.1 select_bitcast_fusion.3
  97.6 0.9 fusion.6.s_ref
  98.6 16.6 %shard_map.60 = f32[1024,2048]{1,0:T(8,128)} custom-call(bf16[1024,2048]{1,0:T(8,128)(2,1)} %q_ref.9, bf16[5,16,128,128]{3,2,1,0:T(8,128)(2,1)} %fusion.6.s_ref, f32[16,1024,10]{2,1,0:T(8,128)} %bitcast.35, f32[1024,2048]{1,0:T(8,128)} %shard_map.59.l_ref), custom_call_target="tpu_custom_call", output_to_operand_aliasing={{}: (3, {})} | custom-call | flops 2684354560 | bytes 20971520 | tf_op jit(solution)/shard_map/pallas_call | solution.py:168
  (18 shorter events, 0.1 us)
Async XLA Ops:
  5.3 3.2 %collective-permute-start = (f32[16,128,128]{2,1,0:T(8,128)}, f32[16,128,128]{2,1,0:T(8,128)S(1)}, u32[]{:S(2)}, u32[]{:S(2)}) collective-permute-start(f32[16,128,128]{2,1,0:T(8,128)} %shard_map.55), channel_id=1, source_target_pairs={{0,1},{1,0},{2,3},{3,2},{4,5},{5,4},{6,7},{7,6},{8,9},{9,8},{10,11... | collective-permute-start | bytes 3145736 | tf_op jit(solution)/shard_map/ppermute | solution.py:198
  8.4 19.0 %copy-start.4 = (f32[16,128,128]{2,1,0:T(8,128)}, f32[16,128,128]{2,1,0:T(8,128)S(1)}, u32[]{:S(2)}) copy-start(f32[16,128,128]{2,1,0:T(8,128)S(1)} %collective-permute-done) | copy-start | bytes 3145732
  10.1 20.1 %copy-start.5 = (f32[10,16,1024]{2,1,0:T(8,128)S(1)}, f32[10,16,1024]{2,1,0:T(8,128)}, u32[]{:S(2)}) copy-start(f32[10,16,1024]{2,1,0:T(8,128)} %param.8) | copy-start | bytes 1966084
  10.2 13.2 %collective-permute-start.1 = (f32[8,128,128]{2,1,0:T(8,128)S(1)}, f32[8,128,128]{2,1,0:T(8,128)S(1)}, u32[]{:S(2)}, u32[]{:S(2)}) collective-permute-start(f32[8,128,128]{2,1,0:T(8,128)S(1)} %constant_dynamic-slice_fusion), channel_id=1, source_target_pairs={{0,2},{2,0},{1,3},{3,1},{4,6},{6,4},{5,7},{7,5},{8,10},{10,8},{9,1... | collective-permute-start | bytes 1572872 | tf_op jit(solution)/shard_map/ppermute | solution.py:198
  23.4 2.9 %collective-permute-start.2 = (f32[8,128,128]{2,1,0:T(8,128)S(1)}, f32[8,128,128]{2,1,0:T(8,128)}, u32[]{:S(2)}, u32[]{:S(2)}) collective-permute-start(f32[8,128,128]{2,1,0:T(8,128)S(1)} %collective-permute-done.1), channel_id=1, source_target_pairs={{0,1},{1,0},{2,3},{3,2},{4,5},{5,4},{6,7},{7,6},{8,9},{9,8},{10,11... | collective-permute-start | bytes 1572872 | tf_op jit(solution)/shard_map/ppermute | solution.py:198
  27.4 0.8 copy-start
  27.4 1.6 %copy-start.2 = (f32[8,128,128]{2,1,0:T(8,128)}, f32[8,128,128]{2,1,0:T(8,128)S(1)}, u32[]{:S(2)}) copy-start(f32[8,128,128]{2,1,0:T(8,128)S(1)} %get-tuple-element.15) | copy-start | bytes 1572868
  29.0 13.1 %collective-permute-start.3 = (f32[4,128,128]{2,1,0:T(8,128)}, f32[4,128,128]{2,1,0:T(8,128)}, u32[]{:S(2)}, u32[]{:S(2)}) collective-permute-start(f32[4,128,128]{2,1,0:T(8,128)} %fusion.11), channel_id=1, source_target_pairs={{0,4},{4,0},{8,12},{12,8},{16,20},{20,16},{24,28},{28,24},{1,5},{5... | collective-permute-start | bytes 786440 | tf_op jit(solution)/shard_map/ppermute | solution.py:198
  43.9 23.6 %collective-permute-start.7 = (f32[4,128,128]{2,1,0:T(8,128)}, f32[4,128,128]{2,1,0:T(8,128)}, u32[]{:S(2)}, u32[]{:S(2)}) collective-permute-start(f32[4,128,128]{2,1,0:T(8,128)} %add.22), channel_id=1, source_target_pairs={{0,8},{8,0},{4,12},{12,4},{16,24},{24,16},{20,28},{28,20},{1,9},{9... | collective-permute-start | bytes 786440 | tf_op jit(solution)/shard_map/ppermute | solution.py:198
  44.1 26.3 %collective-permute-start.4 = (f32[4,128,128]{2,1,0:T(8,128)}, f32[4,128,128]{2,1,0:T(8,128)}, u32[]{:S(2)}, u32[]{:S(2)}) collective-permute-start(f32[4,128,128]{2,1,0:T(8,128)} %collective-permute-done.3), channel_id=1, source_target_pairs={{0,2},{1,3},{2,0},{3,1},{4,6},{5,7},{6,4},{7,5},{8,10},{9,11},{10,... | collective-permute-start | bytes 786440 | tf_op jit(solution)/shard_map/ppermute | solution.py:203
  66.2 6.7 %copy-start.1 = (f32[8,128,128]{2,1,0:T(8,128)S(1)}, f32[8,128,128]{2,1,0:T(8,128)}, u32[]{:S(2)}) copy-start(f32[8,128,128]{2,1,0:T(8,128)} %copy-done) | copy-start | bytes 1572868
  66.2 6.7 %copy-start.3 = (f32[8,128,128]{2,1,0:T(8,128)S(1)}, f32[8,128,128]{2,1,0:T(8,128)}, u32[]{:S(2)}) copy-start(f32[8,128,128]{2,1,0:T(8,128)} %copy-done.2) | copy-start | bytes 1572868
  66.2 19.5 %collective-permute-start.6 = (f32[4,128,128]{2,1,0:T(8,128)}, f32[4,128,128]{2,1,0:T(8,128)S(1)}, u32[]{:S(2)}, u32[]{:S(2)}) collective-permute-start(f32[4,128,128]{2,1,0:T(8,128)} %collective-permute-done.3), channel_id=1, source_target_pairs={{0,1},{1,0},{2,3},{3,2},{4,5},{5,4},{6,7},{7,6},{8,9},{9,8},{10,11... | collective-permute-start | bytes 786440 | tf_op jit(solution)/shard_map/ppermute | solution.py:203
  68.5 16.2 %collective-permute-start.11 = (f32[4,128,128]{2,1,0:T(8,128)S(1)}, f32[4,128,128]{2,1,0:T(8,128)S(1)}, u32[]{:S(2)}, u32[]{:S(2)}) collective-permute-start(f32[4,128,128]{2,1,0:T(8,128)S(1)} %add.23), channel_id=1, source_target_pairs={{0,16},{4,20},{8,24},{12,28},{1,17},{5,21},{9,25},{13,29},{2,18},{... | collective-permute-start | bytes 786440 | tf_op jit(solution)/shard_map/ppermute | solution.py:198
  70.0 15.9 %collective-permute-start.8 = (f32[4,128,128]{2,1,0:T(8,128)}, f32[4,128,128]{2,1,0:T(8,128)S(1)}, u32[]{:S(2)}, u32[]{:S(2)}) collective-permute-start(f32[4,128,128]{2,1,0:T(8,128)} %collective-permute-done.7), channel_id=1, source_target_pairs={{0,2},{1,3},{2,0},{3,1},{4,6},{5,7},{6,4},{7,5},{8,10},{9,11},{10,... | collective-permute-start | bytes 786440 | tf_op jit(solution)/shard_map/ppermute | solution.py:203
  70.3 15.9 %collective-permute-start.5 = (f32[4,128,128]{2,1,0:T(8,128)}, f32[4,128,128]{2,1,0:T(8,128)S(1)}, u32[]{:S(2)}, u32[]{:S(2)}) collective-permute-start(f32[4,128,128]{2,1,0:T(8,128)} %collective-permute-done.4), channel_id=1, source_target_pairs={{0,1},{1,0},{2,3},{3,2},{4,5},{5,4},{6,7},{7,6},{8,9},{9,8},{10,11... | collective-permute-start | bytes 786440 | tf_op jit(solution)/shard_map/ppermute | solution.py:203
  73.8 20.5 %collective-permute-start.10 = (f32[4,128,128]{2,1,0:T(8,128)}, f32[4,128,128]{2,1,0:T(8,128)S(1)}, u32[]{:S(2)}, u32[]{:S(2)}) collective-permute-start(f32[4,128,128]{2,1,0:T(8,128)} %collective-permute-done.7), channel_id=1, source_target_pairs={{0,1},{1,0},{2,3},{3,2},{4,5},{5,4},{6,7},{7,6},{8,9},{9,8},{10,11... | collective-permute-start | bytes 786440 | tf_op jit(solution)/shard_map/ppermute | solution.py:203
  84.7 12.7 %collective-permute-start.14 = (f32[4,128,128]{2,1,0:T(8,128)S(1)}, f32[4,128,128]{2,1,0:T(8,128)S(1)}, u32[]{:S(2)}, u32[]{:S(2)}) collective-permute-start(f32[4,128,128]{2,1,0:T(8,128)S(1)} %collective-permute-done.11), channel_id=1, source_target_pairs={{0,1},{1,0},{2,3},{3,2},{4,5},{5,4},{6,7},{7,6},{8,9},{9,8},{10,11... | collective-permute-start | bytes 786440 | tf_op jit(solution)/shard_map/ppermute | solution.py:203
  85.7 7.9 %collective-permute-start.12 = (f32[4,128,128]{2,1,0:T(8,128)S(1)}, f32[4,128,128]{2,1,0:T(8,128)S(1)}, u32[]{:S(2)}, u32[]{:S(2)}) collective-permute-start(f32[4,128,128]{2,1,0:T(8,128)S(1)} %collective-permute-done.11), channel_id=1, source_target_pairs={{0,2},{1,3},{2,0},{3,1},{4,6},{5,7},{6,4},{7,5},{8,10},{9,11},{10,... | collective-permute-start | bytes 786440 | tf_op jit(solution)/shard_map/ppermute | solution.py:203
  85.9 8.5 %collective-permute-start.9 = (f32[4,128,128]{2,1,0:T(8,128)S(1)}, f32[4,128,128]{2,1,0:T(8,128)S(1)}, u32[]{:S(2)}, u32[]{:S(2)}) collective-permute-start(f32[4,128,128]{2,1,0:T(8,128)S(1)} %collective-permute-done.8), channel_id=1, source_target_pairs={{0,1},{1,0},{2,3},{3,2},{4,5},{5,4},{6,7},{7,6},{8,9},{9,8},{10,11... | collective-permute-start | bytes 786440 | tf_op jit(solution)/shard_map/ppermute | solution.py:203
  93.5 3.9 %collective-permute-start.13 = (f32[4,128,128]{2,1,0:T(8,128)S(1)}, f32[4,128,128]{2,1,0:T(8,128)S(1)}, u32[]{:S(2)}, u32[]{:S(2)}) collective-permute-start(f32[4,128,128]{2,1,0:T(8,128)S(1)} %collective-permute-done.12), channel_id=1, source_target_pairs={{0,1},{1,0},{2,3},{3,2},{4,5},{5,4},{6,7},{7,6},{8,9},{9,8},{10,11... | collective-permute-start | bytes 786440 | tf_op jit(solution)/shard_map/ppermute | solution.py:203

commit v3 on v2

--- a/solution.py
+++ b/solution.py
@@ -12,7 +12,6 @@
 TQ = 256
 CHUNKS = 4
 LOCAL_GROUP = 2
-CROSS_GROUP = 4
 
 
 def level_masks(block, level_count):
@@ -136,12 +135,30 @@
     )(*operands)
 
 
-def cross_kernel(scale, rows, first_level, group, q_ref, s_ref, m_ref, l_ref, o_ref):
-    bits = s_ref.shape[0]
-    dk = s_ref.shape[2]
-    dv = s_ref.shape[3]
+def cross_kernel(scale, rows, first_level, group, n_seq, n_ctx, n_off, sp_ref, q_ref, m_ref, l_ref, *rest):
+    o_ref = rest[-1]
+    seq_refs = rest[:n_seq]
+    part_refs = rest[n_seq:n_seq + n_ctx * n_off]
+    bits = n_seq + n_ctx
+    dv = l_ref.shape[1] // group
+    dk = q_ref.shape[1] // group
+    off = jnp.bitwise_xor(sp_ref[0], pl.program_id(0))
     for j in range(group):
-        sib = jnp.concatenate([s_ref[b, j] for b in range(bits)], axis=1)
+        blocks = []
+        for b in range(n_seq):
+            blocks.append(seq_refs[b][j])
+        for c in range(n_ctx):
+            pick = part_refs[c * n_off][j]
+            for o in range(1, n_off):
+                pick = jnp.where(off == o, part_refs[c * n_off + o][j], pick)
+            blocks.append(pick)
+        sib = jnp.concatenate(
+            [
+                (sp_ref[1 + b].astype(jnp.float32) * blocks[b]).astype(jnp.bfloat16)
+                for b in range(bits)
+            ],
+            axis=1,
+        )
         for a in range(rows // TQ):
             r0 = a * TQ
             t = jnp.dot(
@@ -149,32 +166,46 @@
                 preferred_element_type=jnp.float32,
             )
             mix = m_ref[j, r0:r0 + TQ, :]
+            w_all = mix[:, first_level:first_level + bits] * scale
             cross = jnp.zeros((TQ, dv), jnp.float32)
             for b in range(bits):
-                w = mix[:, first_level + b:first_level + b + 1] * scale
-                cross = cross + w * t[:, b * dv:(b + 1) * dv]
+                cross = cross + w_all[:, b:b + 1] * t[:, b * dv:(b + 1) * dv]
             o_ref[r0:r0 + TQ, j * dv:(j + 1) * dv] = (
                 l_ref[r0:r0 + TQ, j * dv:(j + 1) * dv] + cross
             )
 
 
-def cross_all(queries, sibs, mix_t, local, scale, first_level, group):
+def cross_all(queries, scalars, seq_sibs, ctx_parts, mix_t, local, scale, first_level, group):
     rows = queries.shape[0]
     head_count = mix_t.shape[0]
     dk = queries.shape[1] // head_count
-    dv = sibs.shape[3]
+    dv = seq_sibs[0].shape[2] if seq_sibs else ctx_parts[0][0].shape[2]
     levels = mix_t.shape[2]
-    bits = sibs.shape[0]
+    n_seq = len(seq_sibs)
+    n_ctx = len(ctx_parts)
+    n_off = len(ctx_parts[0]) if ctx_parts else 1
+    bits = n_seq + n_ctx
+    in_specs = [
+        pl.BlockSpec((rows, dk * group), lambda g, sp: (0, g)),
+        pl.BlockSpec((group, rows, levels), lambda g, sp: (g, 0, 0)),
+        pl.BlockSpec((rows, dv * group), lambda g, sp: (0, g)),
+    ]
+    operands = [queries, mix_t, local]
+    for x in seq_sibs:
+        in_specs.append(pl.BlockSpec((group, dk, dv), lambda g, sp: (g, 0, 0)))
+        operands.append(x)
+    for parts in ctx_parts:
+        for x in parts:
+            in_specs.append(pl.BlockSpec(x.shape, lambda g, sp: (0, 0, 0)))
+            operands.append(x)
     return pl.pallas_call(
-        functools.partial(cross_kernel, scale, rows, first_level, group),
-        grid=(head_count // group,),
-        in_specs=[
-            pl.BlockSpec((rows, dk * group), lambda g: (0, g)),
-            pl.BlockSpec((bits, group, dk, dv), lambda g: (0, g, 0, 0)),
-            pl.BlockSpec((group, rows, levels), lambda g: (g, 0, 0)),
-            pl.BlockSpec((rows, dv * group), lambda g: (0, g)),
-        ],
-        out_specs=pl.BlockSpec((rows, dv * group), lambda g: (0, g)),
+        functools.partial(cross_kernel, scale, rows, first_level, group, n_seq, n_ctx, n_off),
+        grid_spec=pltpu.PrefetchScalarGridSpec(
+            num_scalar_prefetch=1,
+            grid=(head_count // group,),
+            in_specs=in_specs,
+            out_specs=pl.BlockSpec((rows, dv * group), lambda g, sp: (0, g)),
+        ),
         out_shape=jax.ShapeDtypeStruct((rows, dv * head_count), jnp.float32),
         input_output_aliases={3: 0},
         cost_estimate=pl.CostEstimate(
@@ -183,7 +214,7 @@
             transcendentals=0,
         ),
         compiler_params=pltpu.CompilerParams(vmem_limit_bytes=64 * 1024 * 1024),
-    )(queries, sibs, mix_t, local)
+    )(scalars, *operands)
 
 
 def swap(block, axis, bit, one_way=False):
@@ -249,6 +280,7 @@
         if bit != ctx_bits - 1:
             quarter = quarter + got
 
+    ctx_parts = []
     for bit in range(ctx_bits):
         part = lax.optimization_barrier(ctx_sibs[bit])
         parts = {0: part}
@@ -257,18 +289,9 @@
                 parts[offset] = to_offset(parts[offset ^ 1], "seq", 1)
             else:
                 parts[offset] = to_offset(part, "seq", offset)
-        full = []
-        for owner in range(seq_count):
-            pick = jnp.zeros_like(part)
-            for offset in range(seq_count):
-                pick = jnp.where((seq_place ^ offset) == owner, parts[offset], pick)
-            full.append(pick)
-        sibs.append(jnp.concatenate(full, axis=0))
+        ctx_parts.append([parts[o] for o in range(seq_count)])
         flags.append(ctx_place >> bit & 1)
-
-    rounded = jnp.stack(
-        [(flags[i].astype(jnp.float32) * sibs[i]).astype(jnp.bfloat16) for i in range(len(sibs))]
-    )
+    scalars = jnp.stack([seq_place] + flags).astype(jnp.int32)
 
     per = head_count // CHUNKS
     local = None
@@ -276,7 +299,10 @@
         local = local_part(
             queries, keys, values, mix_t, masks, c * per, per, LOCAL_GROUP, scale, local
         )
-    return cross_all(queries, rounded, mix_t, local, scale, level_count, CROSS_GROUP)
+    return cross_all(
+        queries, scalars, sibs, ctx_parts, mix_t, local, scale, level_count,
+        head_count // seq_count,
+    )
 
 
 def solution(mesh):

time: 116 us -> 115 us (level)
  other arithmetic: 16.8 us -> 7.16 us
  waiting for transfers between devices: 31 us -> 35.7 us
  Pallas kernels: 49.9 us -> 52.4 us
    ppermute x6, waiting for transfers between devices: 26.8 us -> 35.7 us  [swap(): return lax.ppermute(block, axis, route)]
    unnamed x4 -> x0, other arithmetic: 5.01 us -> none
    ppermute x9, waiting for transfers between devices: 4.24 us -> 0.02 us  [to_offset(): return lax.ppermute(block, axis, [(s, s ^ offset) for s in range(count)])]
    pallas_call x1, Pallas kernels: 16.6 us -> 19.1 us  [cross_all(): pl.pallas_call(functools.partial(cross_kernel, scale, rows, first_level,...]
    concatenate x6 -> x1, other arithmetic: 4.44 us -> 2.28 us  [shards(): partner = jnp.concatenate([lo, hi], axis=0)]
    ppermute x9, starting transfers between devices: 5.67 us -> 6.84 us  [to_offset(): return lax.ppermute(block, axis, [(s, s ^ offset) for s in range(count)])]
    unnamed x13 -> x9, local copies, waits for them, and re-layouts: 5.55 us -> 5.69 us
  transfers between devices with their start and end apart: 15 -> 15, of which waited for: 5 -> 6; matrix products, arithmetic and copies ran while one was open for 13% -> 7% of each run, Pallas kernels for 24% -> 24%
where the time goes in v3:
time: 115 us
  Pallas kernels  52.4 us (46%)
  waiting for transfers between devices  35.7 us (31%)
  starting transfers between devices  12.8 us (11%)
  other arithmetic  7.16 us (6%)
  local copies, waits for them, and re-layouts  6.39 us (6%)
    ppermute x6, waiting for transfers between devices, swap(): return lax.ppermute(block, axis, route)  35.7 us
    pallas_call x4, Pallas kernels, local_part(): pl.pallas_call(functools.partial(local_kernel, scale, rows, group), grid=...  28 us
    pallas_call x1, Pallas kernels, cross_all(): pl.pallas_call(functools.partial(cross_kernel, scale, rows, first_level,...  19.1 us
    ppermute x9, starting transfers between devices, to_offset(): return lax.ppermute(block, axis, [(s, s ^ offset) for s in range(count)])  6.84 us
    ppermute x6, starting transfers between devices, swap(): return lax.ppermute(block, axis, route)  5.95 us
    unnamed x9, local copies, waits for them, and re-layouts  5.69 us
    pallas_call x1, Pallas kernels, own_state(): pl.pallas_call(functools.partial(state_kernel, head_count), grid=(rows //...  5.25 us
  transfers between devices with their start and end apart: 15, of which 6 were waited for; matrix products, arithmetic and copies ran while one was open for 7% of the time, Pallas kernels for 24%

profile of v3, /device:TPU:25, one launch (start us, length us, event | category | flops | bytes accessed | tf_op | source)
XLA Modules:
  0.0 114.5 jit_solution(4914266627870198606)
XLA Ops:
  0.0 5.2 %shard_map.59 = f32[16,128,128]{2,1,0:T(8,128)} custom-call(bf16[1024,2048]{1,0:T(8,128)(2,1)} %k_ref.9, bf16[1024,2048]{1,0:T(8,128)(2,1)} %v_ref.9), custom_call_target="tpu_custom_call" | custom-call | flops 536870912 | bytes 9437184 | tf_op jit(solution)/shard_map/pallas_call | solution.py:50
  5.3 0.7 collective-permute-start
  5.9 2.5 %collective-permute-done.rest_0_ = f32[16,128,128]{2,1,0:T(8,128)S(1)} collective-permute-done((f32[16,128,128]{2,1,0:T(8,128)}, f32[16,128,128]{2,1,0:T(8,128)S(1)}, u32[]{:S(2)}, u32[]{:S(2)}) %collective-permute-start) | collective-permute-done | bytes 1048608 | tf_op jit(solution)/shard_map/ppermute | solution.py:229
  8.4 1.7 %add.18 = f32[16,128,128]{2,1,0:T(8,128)S(1)} add(f32[16,128,128]{2,1,0:T(8,128)} %shard_map.59, f32[16,128,128]{2,1,0:T(8,128)S(1)} %collective-permute-done.rest_0_) | non-fusion elementwise | flops 262144 | bytes 3145728 | tf_op jit(solution)/shard_map/add | solution.py:272
  10.2 1.3 %collective-permute-start.1 = (f32[8,128,128]{2,1,0:T(8,128)S(1)}, f32[8,128,128]{2,1,0:T(8,128)S(1)}, u32[]{:S(2)}, u32[]{:S(2)}) collective-permute-start(f32[8,128,128]{2,1,0:T(8,128)S(1)} %constant_dynamic-slice_fusion), channel_id=1, source_target_pairs={{0,2},{2,0},{1,3},{3,1},{4,6},{6,4},{5,7},{7,5},{8,10},{10,8},{9,1... | collective-permute-start | bytes 1572872 | tf_op jit(solution)/shard_map/ppermute | solution.py:229
  11.5 11.9 %collective-permute-done.1 = f32[8,128,128]{2,1,0:T(8,128)S(1)} collective-permute-done((f32[8,128,128]{2,1,0:T(8,128)S(1)}, f32[8,128,128]{2,1,0:T(8,128)S(1)}, u32[]{:S(2)}, u32[]{:S(2)}) %collective-permute-start.1) | collective-permute-done | bytes 524320 | tf_op jit(solution)/shard_map/ppermute | solution.py:229
  23.4 1.2 %collective-permute-start.2 = (f32[8,128,128]{2,1,0:T(8,128)S(1)}, f32[8,128,128]{2,1,0:T(8,128)}, u32[]{:S(2)}, u32[]{:S(2)}) collective-permute-start(f32[8,128,128]{2,1,0:T(8,128)S(1)} %collective-permute-done.1), channel_id=1, source_target_pairs={{0,1},{1,0},{2,3},{3,2},{4,5},{5,4},{6,7},{7,6},{8,9},{9,8},{10,11... | collective-permute-start | bytes 1572872 | tf_op jit(solution)/shard_map/ppermute | solution.py:229
  24.6 1.7 %collective-permute-done.2 = f32[8,128,128]{2,1,0:T(8,128)} collective-permute-done((f32[8,128,128]{2,1,0:T(8,128)S(1)}, f32[8,128,128]{2,1,0:T(8,128)}, u32[]{:S(2)}, u32[]{:S(2)}) %collective-permute-start.2) | collective-permute-done | bytes 524320 | tf_op jit(solution)/shard_map/ppermute | solution.py:229
  26.3 1.1 broadcast_select_fusion.1
  27.4 0.0 copy-start
  27.4 0.0 copy-start.1
  27.4 0.8 copy-done
  28.2 0.1 fusion.1
  28.3 0.1 copy-done.1
  28.4 1.2 %collective-permute-start.3 = (f32[4,128,128]{2,1,0:T(8,128)S(1)}, f32[4,128,128]{2,1,0:T(8,128)}, u32[]{:S(2)}, u32[]{:S(2)}) collective-permute-start(f32[4,128,128]{2,1,0:T(8,128)S(1)} %fusion.1), channel_id=1, source_target_pairs={{0,4},{4,0},{8,12},{12,8},{16,20},{20,16},{24,28},{28,24},{1,5},{5... | collective-permute-start | bytes 786440 | tf_op jit(solution)/shard_map/ppermute | solution.py:229
  29.6 6.4 %collective-permute-done.3.rest_2_ = f32[4,128,128]{2,1,0:T(8,128)} collective-permute-done((f32[4,128,128]{2,1,0:T(8,128)S(1)}, f32[4,128,128]{2,1,0:T(8,128)}, u32[]{:S(2)}, u32[]{:S(2)}) %collective-permute-start.3) | collective-permute-done | bytes 262176 | tf_op jit(solution)/shard_map/ppermute | solution.py:229
  36.0 1.0 add.22
  37.0 0.2 collective-permute-start.7
  37.2 6.6 %collective-permute-done.7.rest_6_ = f32[4,128,128]{2,1,0:T(8,128)} collective-permute-done((f32[4,128,128]{2,1,0:T(8,128)S(1)}, f32[4,128,128]{2,1,0:T(8,128)}, u32[]{:S(2)}, u32[]{:S(2)}) %collective-permute-start.7) | collective-permute-done | bytes 262176 | tf_op jit(solution)/shard_map/ppermute | solution.py:229
  43.8 1.0 add.23
  44.8 1.3 %collective-permute-start.11 = (f32[4,128,128]{2,1,0:T(8,128)S(1)}, f32[4,128,128]{2,1,0:T(8,128)}, u32[]{:S(2)}, u32[]{:S(2)}) collective-permute-start(f32[4,128,128]{2,1,0:T(8,128)S(1)} %add.23), channel_id=1, source_target_pairs={{0,16},{4,20},{8,24},{12,28},{1,17},{5,21},{9,25},{13,29},{2,18},{... | collective-permute-start | bytes 786440 | tf_op jit(solution)/shard_map/ppermute | solution.py:229
  46.1 4.8 %copy.10 = f32[10,16,1024]{0,2,1:T(8,128)} copy(f32[10,16,1024]{2,1,0:T(8,128)S(1)} %copy-done.3) | data formatting | bytes 1310720 | tf_op args[3]
  50.9 1.2 %collective-permute-start.5 = (f32[4,128,128]{2,1,0:T(8,128)}, f32[4,128,128]{2,1,0:T(8,128)}, u32[]{:S(2)}, u32[]{:S(2)}) collective-permute-start(f32[4,128,128]{2,1,0:T(8,128)} %collective-permute-done.3.rest_2_), channel_id=1, source_target_pairs={{0,2},{1,3},{2,0},{3,1},{4,6},{5,7},{6,4},{7,5},{8,10},{9,11},{10,... | collective-permute-start | bytes 786440 | tf_op jit(solution)/shard_map/ppermute | solution.py:234
  52.1 2.4 %collective-permute-start.4 = (f32[4,128,128]{2,1,0:T(8,128)}, f32[4,128,128]{2,1,0:T(8,128)}, u32[]{:S(2)}, u32[]{:S(2)}) collective-permute-start(f32[4,128,128]{2,1,0:T(8,128)} %collective-permute-done.3.rest_2_), channel_id=1, source_target_pairs={{0,1},{1,0},{2,3},{3,2},{4,5},{5,4},{6,7},{7,6},{8,9},{9,8},{10,11... | collective-permute-start | bytes 786440 | tf_op jit(solution)/shard_map/ppermute | solution.py:234
  54.4 0.3 collective-permute-start.9
  54.7 6.7 %collective-permute-done.11.rest_10_ = f32[4,128,128]{2,1,0:T(8,128)} collective-permute-done((f32[4,128,128]{2,1,0:T(8,128)S(1)}, f32[4,128,128]{2,1,0:T(8,128)}, u32[]{:S(2)}, u32[]{:S(2)}) %collective-permute-start.11) | collective-permute-done | bytes 262176 | tf_op jit(solution)/shard_map/ppermute | solution.py:229
  61.4 1.2 %collective-permute-start.13 = (f32[4,128,128]{2,1,0:T(8,128)}, f32[4,128,128]{2,1,0:T(8,128)}, u32[]{:S(2)}, u32[]{:S(2)}) collective-permute-start(f32[4,128,128]{2,1,0:T(8,128)} %collective-permute-done.11.rest_10_), channel_id=1, source_target_pairs={{0,2},{1,3},{2,0},{3,1},{4,6},{5,7},{6,4},{7,5},{8,10},{9,11},{10,... | collective-permute-start | bytes 786440 | tf_op jit(solution)/shard_map/ppermute | solution.py:234
  62.6 7.1 %shard_map.55.rest_0_ = f32[1024,2048]{1,0:T(8,128)} custom-call(bf16[1024,2048]{1,0:T(8,128)(2,1)} %q_ref.9, bf16[1024,2048]{1,0:T(8,128)(2,1)} %k_ref.9, bf16[1024,2048]{1,0:T(8,128)(2,1)} %v_ref.9, f32[16,1024,10]{2,1,0:T(8,128)} %bitcast.7, f32[3,256,256]{2,1,0:T(8,128)} %constant.23.clone.c_ref), custom_call_target="tpu_custom_call" | custom-call | flops 1342177280 | bytes 5242880 | tf_op jit(solution)/shard_map/pallas_call | solution.py:122
  69.7 0.7 stack.27.sp_ref
  70.4 7.0 %shard_map.56.rest_0_ = f32[1024,2048]{1,0:T(8,128)} custom-call(bf16[1024,2048]{1,0:T(8,128)(2,1)} %q_ref.9, bf16[1024,2048]{1,0:T(8,128)(2,1)} %k_ref.9, bf16[1024,2048]{1,0:T(8,128)(2,1)} %v_ref.9, f32[16,1024,10]{2,1,0:T(8,128)} %bitcast.8, f32[3,256,256]{2,1,0:T(8,128)} %constant.23.clone.c_ref, ...), custom_call_target="tpu_custom_call", output_to_operand_aliasing={{}: (5, {})} | custom-call | flops 1342177280 | bytes 5242880 | tf_op jit(solution)/shard_map/pallas_call | solution.py:122
  77.3 7.0 %shard_map.57.rest_0_ = f32[1024,2048]{1,0:T(8,128)} custom-call(bf16[1024,2048]{1,0:T(8,128)(2,1)} %q_ref.9, bf16[1024,2048]{1,0:T(8,128)(2,1)} %k_ref.9, bf16[1024,2048]{1,0:T(8,128)(2,1)} %v_ref.9, f32[16,1024,10]{2,1,0:T(8,128)} %bitcast.9, f32[3,256,256]{2,1,0:T(8,128)} %constant.23.clone.c_ref, ...), custom_call_target="tpu_custom_call", output_to_operand_aliasing={{}: (5, {})} | custom-call | flops 1342177280 | bytes 5242880 | tf_op jit(solution)/shard_map/pallas_call | solution.py:122
  84.3 0.8 collective-permute-start.8
  85.1 0.0 collective-permute-done.5.rest_4_
  85.1 0.1 collective-permute-start.6
  85.2 0.0 collective-permute-done.4.rest_3_
  85.2 0.4 collective-permute-start.12
  85.6 0.0 collective-permute-done.9.rest_8_
  85.6 0.1 collective-permute-start.10
  85.7 0.0 collective-permute-done.13.rest_12_
  85.7 0.4 collective-permute-start.14
  86.1 7.0 %shard_map.58.l_ref = f32[1024,2048]{1,0:T(8,128)} custom-call(bf16[1024,2048]{1,0:T(8,128)(2,1)} %q_ref.9, bf16[1024,2048]{1,0:T(8,128)(2,1)} %k_ref.9, bf16[1024,2048]{1,0:T(8,128)(2,1)} %v_ref.9, f32[16,1024,10]{2,1,0:T(8,128)} %bitcast.10, f32[3,256,256]{2,1,0:T(8,128)} %constant.23.clone.c_ref, ...), custom_call_target="tpu_custom_call", output_to_operand_aliasing={{}: (5, {})} | custom-call | flops 1342177280 | bytes 5242880 | tf_op jit(solution)/shard_map/pallas_call | solution.py:122
  93.1 2.3 %pad_maximum_fusion.rest_1_ = f32[16,128,128]{2,1,0:T(8,128)} fusion(f32[8,128,128]{2,1,0:T(8,128)} %copy-done.1, f32[8,128,128]{2,1,0:T(8,128)} %copy-done), kind=kLoop, calls=%fused_computation.1 | loop fusion | flops 262144 | bytes 2097152 | tf_op jit(solution)/shard_map/concatenate | solution.py:269
  95.4 0.0 collective-permute-done.8.rest_7_
  95.4 0.0 collective-permute-done.6.rest_5_
  95.4 0.0 collective-permute-done.12.rest_11_
  95.4 0.0 collective-permute-done.10.rest_9_
  95.4 0.0 collective-permute-done.14.rest_13_
  95.4 19.1 %shard_map.60 = f32[1024,2048]{1,0:T(8,128)} custom-call(s32[6]{0:T(128)} %stack.27.sp_ref, bf16[1024,2048]{1,0:T(8,128)(2,1)} %q_ref.9, f32[16,1024,10]{2,1,0:T(8,128)} %bitcast.11, f32[1024,2048]{1,0:T(8,128)} %shard_map.58.l_ref, f32[16,128,128]{2,1,0:T(8,128)} %copy-done.2, ...), custom_call_target="tpu_custom_call", output_to_operand_aliasing={{}: (3, {})} | custom-call | flops 2684354560 | bytes 20971520 | tf_op jit(solution)/shard_map/pallas_call | solution.py:201
  (5 shorter events, 0.1 us)
Async XLA Ops:
  5.3 40.8 %copy-start.3 = (f32[10,16,1024]{2,1,0:T(8,128)S(1)}, f32[10,16,1024]{2,1,0:T(8,128)}, u32[]{:S(2)}) copy-start(f32[10,16,1024]{2,1,0:T(8,128)} %param.8) | copy-start | bytes 1966084
  5.3 3.2 %collective-permute-start = (f32[16,128,128]{2,1,0:T(8,128)}, f32[16,128,128]{2,1,0:T(8,128)S(1)}, u32[]{:S(2)}, u32[]{:S(2)}) collective-permute-start(f32[16,128,128]{2,1,0:T(8,128)} %shard_map.59), channel_id=1, source_target_pairs={{0,1},{1,0},{2,3},{3,2},{4,5},{5,4},{6,7},{7,6},{8,9},{9,8},{10,11... | collective-permute-start | bytes 3145736 | tf_op jit(solution)/shard_map/ppermute | solution.py:229
  8.4 42.4 %copy-start.2 = (f32[16,128,128]{2,1,0:T(8,128)}, f32[16,128,128]{2,1,0:T(8,128)S(1)}, u32[]{:S(2)}) copy-start(f32[16,128,128]{2,1,0:T(8,128)S(1)} %collective-permute-done.rest_0_) | copy-start | bytes 3145732
  10.2 13.2 %collective-permute-start.1 = (f32[8,128,128]{2,1,0:T(8,128)S(1)}, f32[8,128,128]{2,1,0:T(8,128)S(1)}, u32[]{:S(2)}, u32[]{:S(2)}) collective-permute-start(f32[8,128,128]{2,1,0:T(8,128)S(1)} %constant_dynamic-slice_fusion), channel_id=1, source_target_pairs={{0,2},{2,0},{1,3},{3,1},{4,6},{6,4},{5,7},{7,5},{8,10},{10,8},{9,1... | collective-permute-start | bytes 1572872 | tf_op jit(solution)/shard_map/ppermute | solution.py:229
  23.4 2.9 %collective-permute-start.2 = (f32[8,128,128]{2,1,0:T(8,128)S(1)}, f32[8,128,128]{2,1,0:T(8,128)}, u32[]{:S(2)}, u32[]{:S(2)}) collective-permute-start(f32[8,128,128]{2,1,0:T(8,128)S(1)} %collective-permute-done.1), channel_id=1, source_target_pairs={{0,1},{1,0},{2,3},{3,2},{4,5},{5,4},{6,7},{7,6},{8,9},{9,8},{10,11... | collective-permute-start | bytes 1572872 | tf_op jit(solution)/shard_map/ppermute | solution.py:229
  27.4 0.8 copy-start
  27.4 1.0 copy-start.1
  28.4 7.6 %collective-permute-start.3 = (f32[4,128,128]{2,1,0:T(8,128)S(1)}, f32[4,128,128]{2,1,0:T(8,128)}, u32[]{:S(2)}, u32[]{:S(2)}) collective-permute-start(f32[4,128,128]{2,1,0:T(8,128)S(1)} %fusion.1), channel_id=1, source_target_pairs={{0,4},{4,0},{8,12},{12,8},{16,20},{20,16},{24,28},{28,24},{1,5},{5... | collective-permute-start | bytes 786440 | tf_op jit(solution)/shard_map/ppermute | solution.py:229
  37.0 6.8 %collective-permute-start.7 = (f32[4,128,128]{2,1,0:T(8,128)S(1)}, f32[4,128,128]{2,1,0:T(8,128)}, u32[]{:S(2)}, u32[]{:S(2)}) collective-permute-start(f32[4,128,128]{2,1,0:T(8,128)S(1)} %add.22), channel_id=1, source_target_pairs={{0,8},{8,0},{4,12},{12,4},{16,24},{24,16},{20,28},{28,20},{1,9},{9... | collective-permute-start | bytes 786440 | tf_op jit(solution)/shard_map/ppermute | solution.py:229
  44.8 16.6 %collective-permute-start.11 = (f32[4,128,128]{2,1,0:T(8,128)S(1)}, f32[4,128,128]{2,1,0:T(8,128)}, u32[]{:S(2)}, u32[]{:S(2)}) collective-permute-start(f32[4,128,128]{2,1,0:T(8,128)S(1)} %add.23), channel_id=1, source_target_pairs={{0,16},{4,20},{8,24},{12,28},{1,17},{5,21},{9,25},{13,29},{2,18},{... | collective-permute-start | bytes 786440 | tf_op jit(solution)/shard_map/ppermute | solution.py:229
  50.9 34.2 %collective-permute-start.5 = (f32[4,128,128]{2,1,0:T(8,128)}, f32[4,128,128]{2,1,0:T(8,128)}, u32[]{:S(2)}, u32[]{:S(2)}) collective-permute-start(f32[4,128,128]{2,1,0:T(8,128)} %collective-permute-done.3.rest_2_), channel_id=1, source_target_pairs={{0,2},{1,3},{2,0},{3,1},{4,6},{5,7},{6,4},{7,5},{8,10},{9,11},{10,... | collective-permute-start | bytes 786440 | tf_op jit(solution)/shard_map/ppermute | solution.py:234
  52.1 33.1 %collective-permute-start.4 = (f32[4,128,128]{2,1,0:T(8,128)}, f32[4,128,128]{2,1,0:T(8,128)}, u32[]{:S(2)}, u32[]{:S(2)}) collective-permute-start(f32[4,128,128]{2,1,0:T(8,128)} %collective-permute-done.3.rest_2_), channel_id=1, source_target_pairs={{0,1},{1,0},{2,3},{3,2},{4,5},{5,4},{6,7},{7,6},{8,9},{9,8},{10,11... | collective-permute-start | bytes 786440 | tf_op jit(solution)/shard_map/ppermute | solution.py:234
  54.4 31.2 %collective-permute-start.9 = (f32[4,128,128]{2,1,0:T(8,128)}, f32[4,128,128]{2,1,0:T(8,128)}, u32[]{:S(2)}, u32[]{:S(2)}) collective-permute-start(f32[4,128,128]{2,1,0:T(8,128)} %collective-permute-done.7.rest_6_), channel_id=1, source_target_pairs={{0,2},{1,3},{2,0},{3,1},{4,6},{5,7},{6,4},{7,5},{8,10},{9,11},{10,... | collective-permute-start | bytes 786440 | tf_op jit(solution)/shard_map/ppermute | solution.py:234
  61.4 24.3 %collective-permute-start.13 = (f32[4,128,128]{2,1,0:T(8,128)}, f32[4,128,128]{2,1,0:T(8,128)}, u32[]{:S(2)}, u32[]{:S(2)}) collective-permute-start(f32[4,128,128]{2,1,0:T(8,128)} %collective-permute-done.11.rest_10_), channel_id=1, source_target_pairs={{0,2},{1,3},{2,0},{3,1},{4,6},{5,7},{6,4},{7,5},{8,10},{9,11},{10,... | collective-permute-start | bytes 786440 | tf_op jit(solution)/shard_map/ppermute | solution.py:234
  84.3 11.1 %collective-permute-start.8 = (f32[4,128,128]{2,1,0:T(8,128)}, f32[4,128,128]{2,1,0:T(8,128)}, u32[]{:S(2)}, u32[]{:S(2)}) collective-permute-start(f32[4,128,128]{2,1,0:T(8,128)} %collective-permute-done.7.rest_6_), channel_id=1, source_target_pairs={{0,1},{1,0},{2,3},{3,2},{4,5},{5,4},{6,7},{7,6},{8,9},{9,8},{10,11... | collective-permute-start | bytes 786440 | tf_op jit(solution)/shard_map/ppermute | solution.py:234
  85.1 10.3 %collective-permute-start.6 = (f32[4,128,128]{2,1,0:T(8,128)}, f32[4,128,128]{2,1,0:T(8,128)}, u32[]{:S(2)}, u32[]{:S(2)}) collective-permute-start(f32[4,128,128]{2,1,0:T(8,128)} %collective-permute-done.5.rest_4_), channel_id=1, source_target_pairs={{0,1},{1,0},{2,3},{3,2},{4,5},{5,4},{6,7},{7,6},{8,9},{9,8},{10,11... | collective-permute-start | bytes 786440 | tf_op jit(solution)/shard_map/ppermute | solution.py:234
  85.2 10.2 %collective-permute-start.12 = (f32[4,128,128]{2,1,0:T(8,128)}, f32[4,128,128]{2,1,0:T(8,128)}, u32[]{:S(2)}, u32[]{:S(2)}) collective-permute-start(f32[4,128,128]{2,1,0:T(8,128)} %collective-permute-done.11.rest_10_), channel_id=1, source_target_pairs={{0,1},{1,0},{2,3},{3,2},{4,5},{5,4},{6,7},{7,6},{8,9},{9,8},{10,11... | collective-permute-start | bytes 786440 | tf_op jit(solution)/shard_map/ppermute | solution.py:234
  85.6 9.8 %collective-permute-start.10 = (f32[4,128,128]{2,1,0:T(8,128)}, f32[4,128,128]{2,1,0:T(8,128)}, u32[]{:S(2)}, u32[]{:S(2)}) collective-permute-start(f32[4,128,128]{2,1,0:T(8,128)} %collective-permute-done.9.rest_8_), channel_id=1, source_target_pairs={{0,1},{1,0},{2,3},{3,2},{4,5},{5,4},{6,7},{7,6},{8,9},{9,8},{10,11... | collective-permute-start | bytes 786440 | tf_op jit(solution)/shard_map/ppermute | solution.py:234
  85.7 9.7 %collective-permute-start.14 = (f32[4,128,128]{2,1,0:T(8,128)}, f32[4,128,128]{2,1,0:T(8,128)}, u32[]{:S(2)}, u32[]{:S(2)}) collective-permute-start(f32[4,128,128]{2,1,0:T(8,128)} %collective-permute-done.13.rest_12_), channel_id=1, source_target_pairs={{0,1},{1,0},{2,3},{3,2},{4,5},{5,4},{6,7},{7,6},{8,9},{9,8},{10,11... | collective-permute-start | bytes 786440 | tf_op jit(solution)/shard_map/ppermute | solution.py:234

commit v4 on v1

--- a/solution.py
+++ b/solution.py
@@ -66,44 +66,51 @@
     )(keys, values)
 
 
-def local_kernel(scale, rows, group, q_ref, k_ref, v_ref, m_ref, c_ref, *rest):
+def local_kernel(scale, rows, group, first, head_count, steps, q_ref, k_ref, v_ref, m_ref, c_ref, *rest):
     o_ref = rest[-1]
     blocks = rows // TQ
     inner = c_ref.shape[0]
     dk = q_ref.shape[1] // group
     dv = v_ref.shape[1] // group
-    for j in range(group):
-        qc = slice(j * dk, (j + 1) * dk)
-        vc = slice(j * dv, (j + 1) * dv)
-        for a in range(blocks):
-            r0 = a * TQ
-            s = lax.dot_general(
-                q_ref[r0:r0 + TQ, qc], k_ref[0:r0 + TQ, qc],
-                (((1,), (1,)), ((), ())), preferred_element_type=jnp.float32,
-            )
-            s = s * scale
-            mix = m_ref[j, :, r0:r0 + TQ].T
-            pieces = []
-            for b in range(a):
-                level = inner + (a ^ b).bit_length() - 1
-                w = mix[:, level:level + 1]
-                pieces.append((s[:, b * TQ:(b + 1) * TQ] * w).astype(jnp.bfloat16))
-            wd = c_ref[0] * mix[:, 0:1]
-            for l in range(1, inner):
-                wd = wd + c_ref[l] * mix[:, l:l + 1]
-            pieces.append((s[:, r0:r0 + TQ] * wd).astype(jnp.bfloat16))
-            p = pieces[0] if len(pieces) == 1 else jnp.concatenate(pieces, axis=1)
-            o_ref[r0:r0 + TQ, vc] = jnp.dot(
-                p, v_ref[0:r0 + TQ, vc], preferred_element_type=jnp.float32
-            )
-
-
-def local_part(queries, keys, values, mix_t, masks, first, count, group, scale, prev):
+
+    def column(r0, level, head):
+        c = level * head_count + head
+        return m_ref[r0:r0 + TQ, c:c + 1]
+
+    def body(step):
+        for j in range(group):
+            head = first + step * group + j
+            qc = slice(j * dk, (j + 1) * dk)
+            vc = slice(j * dv, (j + 1) * dv)
+            for a in range(blocks):
+                r0 = a * TQ
+                s = lax.dot_general(
+                    q_ref[r0:r0 + TQ, qc], k_ref[0:r0 + TQ, qc],
+                    (((1,), (1,)), ((), ())), preferred_element_type=jnp.float32,
+                )
+                s = s * scale
+                pieces = []
+                for b in range(a):
+                    level = inner + (a ^ b).bit_length() - 1
+                    w = column(r0, level, head)
+                    pieces.append((s[:, b * TQ:(b + 1) * TQ] * w).astype(jnp.bfloat16))
+                wd = c_ref[0] * column(r0, 0, head)
+                for l in range(1, inner):
+                    wd = wd + c_ref[l] * column(r0, l, head)
+                pieces.append((s[:, r0:r0 + TQ] * wd).astype(jnp.bfloat16))
+                p = pieces[0] if len(pieces) == 1 else jnp.concatenate(pieces, axis=1)
+                o_ref[r0:r0 + TQ, vc] = jnp.dot(
+                    p, v_ref[0:r0 + TQ, vc], preferred_element_type=jnp.float32
+                )
+
+    for step in range(steps):
+        pl.when(pl.program_id(0) == step)(functools.partial(body, step))
+
+
+def local_part(queries, keys, values, mix_t, masks, first, count, group, scale, prev, head_count):
     rows = queries.shape[0]
-    head_count = mix_t.shape[0]
     dk = queries.shape[1] // head_count
     dv = values.shape[1] // head_count
-    levels = mix_t.shape[1]
     blocks = rows // TQ
     tiles = blocks * (blocks + 1) // 2
     base = first // group
@@ -111,7 +118,7 @@
         pl.BlockSpec((rows, dk * group), lambda h: (0, h + base)),
         pl.BlockSpec((rows, dk * group), lambda h: (0, h + base)),
         pl.BlockSpec((rows, dv * group), lambda h: (0, h + base)),
-        pl.BlockSpec((group, levels, rows), lambda h: (h + base, 0, 0)),
+        pl.BlockSpec(mix_t.shape, lambda h: (0, 0)),
         pl.BlockSpec(masks.shape, lambda h: (0, 0, 0)),
     ]
     operands = [queries, keys, values, mix_t, masks]
@@ -121,7 +128,7 @@
         operands.append(prev)
         aliases = {5: 0}
     return pl.pallas_call(
-        functools.partial(local_kernel, scale, rows, group),
+        functools.partial(local_kernel, scale, rows, group, first, head_count, count // group),
         grid=(count // group,),
         in_specs=in_specs,
         out_specs=pl.BlockSpec((rows, dv * group), lambda h: (0, h + base)),
@@ -209,8 +216,7 @@
     dk = queries.shape[1] // head_count
     scale = dk ** (-0.5)
     level_count = (rows // SPAN).bit_length()
-    pad = -mixing.shape[0] % 8
-    mix_t = jnp.pad(mixing, ((0, pad), (0, 0), (0, 0))).transpose(1, 0, 2)
+    mix_t = mixing.reshape(-1, rows).T
     masks = jnp.asarray(level_masks(TQ, level_count))
 
     state = own_state(keys, values, head_count)
@@ -251,7 +257,7 @@
             quarter = quarter + got
 
     for bit in range(ctx_bits):
-        part = ctx_sibs[bit]
+        part = lax.optimization_barrier(ctx_sibs[bit])
         parts = {0: part}
         for offset in range(1, seq_count):
             if offset & 1 and offset > 1:
@@ -275,9 +281,12 @@
     local = None
     for c in range(CHUNKS):
         local = local_part(
-            queries, keys, values, mix_t, masks, c * per, per, LOCAL_GROUP, scale, local
+            queries, keys, values, mix_t, masks, c * per, per, LOCAL_GROUP, scale, local,
+            head_count,
         )
-    return cross_all(queries, rounded, mix_t, local, scale, level_count, CROSS_GROUP)
+    pad = -mixing.shape[0] % 8
+    mix_c = jnp.pad(mixing, ((0, pad), (0, 0), (0, 0))).transpose(1, 0, 2)
+    return cross_all(queries, rounded, mix_c, local, scale, level_count, CROSS_GROUP)
 
 
 def solution(mesh):

time: 138 us -> 116 us (0.84)
  waiting for transfers between devices: 51.6 us -> 29.5 us
  local copies, waits for them, and re-layouts: 2.51 us -> 7.08 us
  starting transfers between devices: 16.2 us -> 12.3 us
  other arithmetic: 12.4 us -> 15.5 us
  Pallas kernels: 54.3 us -> 51.2 us
    ppermute x6, waiting for transfers between devices: 41.3 us -> 27 us  [swap(): return lax.ppermute(block, axis, route)]
    ppermute x9, waiting for transfers between devices: 10.3 us -> 2.45 us  [to_offset(): return lax.ppermute(block, axis, [(s, s ^ offset) for s in range(count)])]
    ppermute x9, starting transfers between devices: 10 us -> 6.44 us  [to_offset(): return lax.ppermute(block, axis, [(s, s ^ offset) for s in range(count)])]
    pallas_call x4, Pallas kernels: 31.3 us -> 28.1 us  [local_part(): pl.pallas_call(functools.partial(local_kernel, scale, rows, group, first,...]
    concatenate x4 -> x6, other arithmetic: 1.6 us -> 4.44 us  [shards(): sibs.append(jnp.concatenate(full, axis=0))]
    unnamed x33 -> x15, local copies, waits for them, and re-layouts: 1.37 us -> 3.26 us
    transpose x1, local copies, waits for them, and re-layouts: 1.1 us -> 2.48 us  [shards(): mix_c = jnp.pad(mixing, ((0, pad), (0, 0), (0, 0))).transpose(1, 0, 2)]
  transfers between devices with their start and end apart: 15 -> 15, of which waited for: 9 -> 5; matrix products, arithmetic and copies ran while one was open for 6% -> 13% of each run, Pallas kernels for 23% -> 24%
where the time goes in v4:
time: 116 us
  Pallas kernels  51.2 us (44%)
  waiting for transfers between devices  29.5 us (25%)
  other arithmetic  15.5 us (13%)
  starting transfers between devices  12.3 us (11%)
  local copies, waits for them, and re-layouts  7.08 us (6%)
    pallas_call x4, Pallas kernels, local_part(): pl.pallas_call(functools.partial(local_kernel, scale, rows, group, first,...  28.1 us
    ppermute x6, waiting for transfers between devices, swap(): return lax.ppermute(block, axis, route)  27 us
    pallas_call x1, Pallas kernels, cross_all(): pl.pallas_call(functools.partial(cross_kernel, scale, rows, first_level,...  17.8 us
    ppermute x9, starting transfers between devices, to_offset(): return lax.ppermute(block, axis, [(s, s ^ offset) for s in range(count)])  6.44 us
    ppermute x6, starting transfers between devices, swap(): return lax.ppermute(block, axis, route)  5.88 us
    pallas_call x1, Pallas kernels, own_state(): pl.pallas_call(functools.partial(state_kernel, head_count), grid=(rows //...  5.25 us
    concatenate x6, other arithmetic, shards(): sibs.append(jnp.concatenate(full, axis=0))  4.44 us
    unnamed x4, other arithmetic  3.71 us
  transfers between devices with their start and end apart: 15, of which 5 were waited for; matrix products, arithmetic and copies ran while one was open for 13% of the time, Pallas kernels for 24%

profile of v4, /device:TPU:25, one launch (start us, length us, event | category | flops | bytes accessed | tf_op | source)
XLA Modules:
  0.0 115.7 jit_solution(2886357989526152920)
XLA Ops:
  0.0 5.2 %shard_map.55 = f32[16,128,128]{2,1,0:T(8,128)} custom-call(bf16[1024,2048]{1,0:T(8,128)(2,1)} %k_ref.9, bf16[1024,2048]{1,0:T(8,128)(2,1)} %v_ref.9), custom_call_target="tpu_custom_call" | custom-call | flops 536870912 | bytes 9437184 | tf_op jit(solution)/shard_map/pallas_call | solution.py:51
  5.3 0.7 collective-permute-start
  5.9 2.5 %collective-permute-done = f32[16,128,128]{2,1,0:T(8,128)S(1)} collective-permute-done((f32[16,128,128]{2,1,0:T(8,128)}, f32[16,128,128]{2,1,0:T(8,128)S(1)}, u32[]{:S(2)}, u32[]{:S(2)}) %collective-permute-start) | collective-permute-done | bytes 1048608 | tf_op jit(solution)/shard_map/ppermute | solution.py:205
  8.4 1.7 %add.20 = f32[16,128,128]{2,1,0:T(8,128)S(1)} add(f32[16,128,128]{2,1,0:T(8,128)} %shard_map.55, f32[16,128,128]{2,1,0:T(8,128)S(1)} %collective-permute-done) | non-fusion elementwise | flops 262144 | bytes 3145728 | tf_op jit(solution)/shard_map/add | solution.py:248
  10.2 1.3 %collective-permute-start.1 = (f32[8,128,128]{2,1,0:T(8,128)S(1)}, f32[8,128,128]{2,1,0:T(8,128)S(1)}, u32[]{:S(2)}, u32[]{:S(2)}) collective-permute-start(f32[8,128,128]{2,1,0:T(8,128)S(1)} %constant_dynamic-slice_fusion), channel_id=1, source_target_pairs={{0,2},{2,0},{1,3},{3,1},{4,6},{6,4},{5,7},{7,5},{8,10},{10,8},{9,1... | collective-permute-start | bytes 1572872 | tf_op jit(solution)/shard_map/ppermute | solution.py:205
  11.5 11.9 %collective-permute-done.1 = f32[8,128,128]{2,1,0:T(8,128)S(1)} collective-permute-done((f32[8,128,128]{2,1,0:T(8,128)S(1)}, f32[8,128,128]{2,1,0:T(8,128)S(1)}, u32[]{:S(2)}, u32[]{:S(2)}) %collective-permute-start.1) | collective-permute-done | bytes 524320 | tf_op jit(solution)/shard_map/ppermute | solution.py:205
  23.4 1.2 %collective-permute-start.2 = (f32[8,128,128]{2,1,0:T(8,128)S(1)}, f32[8,128,128]{2,1,0:T(8,128)}, u32[]{:S(2)}, u32[]{:S(2)}) collective-permute-start(f32[8,128,128]{2,1,0:T(8,128)S(1)} %collective-permute-done.1), channel_id=1, source_target_pairs={{0,1},{1,0},{2,3},{3,2},{4,5},{5,4},{6,7},{7,6},{8,9},{9,8},{10,11... | collective-permute-start | bytes 1572872 | tf_op jit(solution)/shard_map/ppermute | solution.py:205
  24.6 1.3 %copy.13 = f32[160,1024]{0,1:T(8,128)} copy(f32[160,1024]{1,0:T(8,128)S(1)} %bitcast.40) | data formatting | bytes 1310720 | tf_op jit(solution)/shard_map/reshape | solution.py:219
  25.9 0.4 collective-permute-done.2
  26.3 1.1 broadcast_select_fusion.1
  27.4 0.8 copy-done
  28.2 0.8 fusion.11
  29.0 1.2 %collective-permute-start.3 = (f32[4,128,128]{2,1,0:T(8,128)}, f32[4,128,128]{2,1,0:T(8,128)}, u32[]{:S(2)}, u32[]{:S(2)}) collective-permute-start(f32[4,128,128]{2,1,0:T(8,128)} %fusion.11), channel_id=1, source_target_pairs={{0,4},{4,0},{8,12},{12,8},{16,20},{20,16},{24,28},{28,24},{1,5},{5... | collective-permute-start | bytes 786440 | tf_op jit(solution)/shard_map/ppermute | solution.py:205
  30.2 7.0 %shard_map.56.rest_0_ = f32[1024,2048]{1,0:T(8,128)} custom-call(bf16[1024,2048]{1,0:T(8,128)(2,1)} %q_ref.9, bf16[1024,2048]{1,0:T(8,128)(2,1)} %k_ref.9, bf16[1024,2048]{1,0:T(8,128)(2,1)} %v_ref.9, f32[1024,160]{1,0:T(8,128)} %bitcast.34, f32[3,256,256]{2,1,0:T(8,128)} %constant.28.clone.c_ref), custom_call_target="tpu_custom_call" | custom-call | flops 1342177280 | bytes 5242880 | tf_op jit(solution)/shard_map/pallas_call | solution.py:130
  37.2 2.5 %copy.12 = f32[10,16,1024]{2,0,1:T(8,128)} copy(f32[10,16,1024]{2,1,0:T(8,128)} %param.8) | data formatting | bytes 1310720 | tf_op args[3]
  39.6 7.0 %shard_map.57.rest_0_ = f32[1024,2048]{1,0:T(8,128)} custom-call(bf16[1024,2048]{1,0:T(8,128)(2,1)} %q_ref.9, bf16[1024,2048]{1,0:T(8,128)(2,1)} %k_ref.9, bf16[1024,2048]{1,0:T(8,128)(2,1)} %v_ref.9, f32[1024,160]{1,0:T(8,128)} %bitcast.35, f32[3,256,256]{2,1,0:T(8,128)} %constant.28.clone.c_ref, ...), custom_call_target="tpu_custom_call", output_to_operand_aliasing={{}: (5, {})} | custom-call | flops 1342177280 | bytes 5242880 | tf_op jit(solution)/shard_map/pallas_call | solution.py:130
  46.6 7.2 %shard_map.58.rest_0_ = f32[1024,2048]{1,0:T(8,128)} custom-call(bf16[1024,2048]{1,0:T(8,128)(2,1)} %q_ref.9, bf16[1024,2048]{1,0:T(8,128)(2,1)} %k_ref.9, bf16[1024,2048]{1,0:T(8,128)(2,1)} %v_ref.9, f32[1024,160]{1,0:T(8,128)} %bitcast.36, f32[3,256,256]{2,1,0:T(8,128)} %constant.28.clone.c_ref, ...), custom_call_target="tpu_custom_call", output_to_operand_aliasing={{}: (5, {})} | custom-call | flops 1342177280 | bytes 5242880 | tf_op jit(solution)/shard_map/pallas_call | solution.py:130
  53.8 0.0 collective-permute-done.3
  53.8 1.8 %add.24 = f32[4,128,128]{2,1,0:T(8,128)} add(f32[4,128,128]{2,1,0:T(8,128)} %fusion.11, f32[4,128,128]{2,1,0:T(8,128)} %collective-permute-done.3) | non-fusion elementwise | flops 65536 | bytes 786432 | tf_op jit(solution)/shard_map/add | solution.py:257
  55.6 0.2 collective-permute-start.7
  55.7 1.2 %collective-permute-start.4 = (f32[4,128,128]{2,1,0:T(8,128)}, f32[4,128,128]{2,1,0:T(8,128)}, u32[]{:S(2)}, u32[]{:S(2)}) collective-permute-start(f32[4,128,128]{2,1,0:T(8,128)} %collective-permute-done.3), channel_id=1, source_target_pairs={{0,2},{1,3},{2,0},{3,1},{4,6},{5,7},{6,4},{7,5},{8,10},{9,11},{10,... | collective-permute-start | bytes 786440 | tf_op jit(solution)/shard_map/ppermute | solution.py:210
  57.0 7.0 %shard_map.59.l_ref = f32[1024,2048]{1,0:T(8,128)} custom-call(bf16[1024,2048]{1,0:T(8,128)(2,1)} %q_ref.9, bf16[1024,2048]{1,0:T(8,128)(2,1)} %k_ref.9, bf16[1024,2048]{1,0:T(8,128)(2,1)} %v_ref.9, f32[1024,160]{1,0:T(8,128)} %bitcast.37, f32[3,256,256]{2,1,0:T(8,128)} %constant.28.clone.c_ref, ...), custom_call_target="tpu_custom_call", output_to_operand_aliasing={{}: (5, {})} | custom-call | flops 1342177280 | bytes 5242880 | tf_op jit(solution)/shard_map/pallas_call | solution.py:130
  63.9 2.5 %pad_bitcast_fusion.m_ref = f32[16,16,1024]{2,1,0:T(8,128)} fusion(f32[10,16,1024]{2,0,1:T(8,128)} %copy.12), kind=kLoop, calls=%fused_computation.10 | loop fusion | bytes 1703936 | tf_op jit(solution)/shard_map/transpose | solution.py:288
  66.4 1.2 %collective-permute-start.6 = (f32[4,128,128]{2,1,0:T(8,128)}, f32[4,128,128]{2,1,0:T(8,128)S(1)}, u32[]{:S(2)}, u32[]{:S(2)}) collective-permute-start(f32[4,128,128]{2,1,0:T(8,128)} %collective-permute-done.3), channel_id=1, source_target_pairs={{0,1},{1,0},{2,3},{3,2},{4,5},{5,4},{6,7},{7,6},{8,9},{9,8},{10,11... | collective-permute-start | bytes 786440 | tf_op jit(solution)/shard_map/ppermute | solution.py:210
  67.6 1.1 add.25
  68.7 1.3 %collective-permute-start.11 = (f32[4,128,128]{2,1,0:T(8,128)S(1)}, f32[4,128,128]{2,1,0:T(8,128)S(1)}, u32[]{:S(2)}, u32[]{:S(2)}) collective-permute-start(f32[4,128,128]{2,1,0:T(8,128)S(1)} %add.25), channel_id=1, source_target_pairs={{0,16},{4,20},{8,24},{12,28},{1,17},{5,21},{9,25},{13,29},{2,18},{... | collective-permute-start | bytes 786440 | tf_op jit(solution)/shard_map/ppermute | solution.py:205
  70.0 0.3 collective-permute-start.8
  70.3 0.0 collective-permute-done.4
  70.3 0.3 collective-permute-start.5
  70.6 0.9 fusion.5
  71.5 0.9 fusion.9
  72.5 0.2 collective-permute-start.10
  72.7 12.3 %collective-permute-done.11 = f32[4,128,128]{2,1,0:T(8,128)S(1)} collective-permute-done((f32[4,128,128]{2,1,0:T(8,128)S(1)}, f32[4,128,128]{2,1,0:T(8,128)S(1)}, u32[]{:S(2)}, u32[]{:S(2)}) %collective-permute-start.11) | collective-permute-done | bytes 262176 | tf_op jit(solution)/shard_map/ppermute | solution.py:205
  85.0 0.3 collective-permute-start.12
  85.2 1.1 collective-permute-start.14
  86.4 0.1 collective-permute-start.9
  86.5 1.1 select_bitcast_fusion.11
  87.6 1.0 select_bitcast_fusion.10
  88.6 0.9 fusion.8
  89.6 2.4 %collective-permute-done.12 = f32[4,128,128]{2,1,0:T(8,128)S(1)} collective-permute-done((f32[4,128,128]{2,1,0:T(8,128)S(1)}, f32[4,128,128]{2,1,0:T(8,128)S(1)}, u32[]{:S(2)}, u32[]{:S(2)}) %collective-permute-start.12) | collective-permute-done | bytes 262176 | tf_op jit(solution)/shard_map/ppermute | solution.py:210
  92.0 1.7 %collective-permute-start.13 = (f32[4,128,128]{2,1,0:T(8,128)S(1)}, f32[4,128,128]{2,1,0:T(8,128)S(1)}, u32[]{:S(2)}, u32[]{:S(2)}) collective-permute-start(f32[4,128,128]{2,1,0:T(8,128)S(1)} %collective-permute-done.12), channel_id=1, source_target_pairs={{0,1},{1,0},{2,3},{3,2},{4,5},{5,4},{6,7},{7,6},{8,9},{9,8},{10,11... | collective-permute-start | bytes 786440 | tf_op jit(solution)/shard_map/ppermute | solution.py:210
  93.7 1.1 select_bitcast_fusion.7
  94.8 1.0 select_bitcast_fusion.6
  95.8 0.9 fusion.7
  96.7 0.1 select_bitcast_fusion.2
  96.8 0.1 select_bitcast_fusion.3
  96.9 0.9 fusion.6.s_ref
  97.9 17.8 %shard_map.60 = f32[1024,2048]{1,0:T(8,128)} custom-call(bf16[1024,2048]{1,0:T(8,128)(2,1)} %q_ref.9, bf16[5,16,128,128]{3,2,1,0:T(8,128)(2,1)} %fusion.6.s_ref, f32[16,16,1024]{2,1,0:T(8,128)} %pad_bitcast_fusion.m_ref, f32[1024,2048]{1,0:T(8,128)} %shard_map.59.l_ref), custom_call_target="tpu_custom_call", output_to_operand_aliasing={{}: (3, {})} | custom-call | flops 2684354560 | bytes 20971520 | tf_op jit(solution)/shard_map/pallas_call | solution.py:175
  (22 shorter events, 0.1 us)
Async XLA Ops:
  5.3 19.4 %copy-start.6 = (f32[10,16,1024]{2,1,0:T(8,128)S(1)}, f32[10,16,1024]{2,1,0:T(8,128)}, u32[]{:S(2)}) copy-start(f32[10,16,1024]{2,1,0:T(8,128)} %param.8) | copy-start | bytes 1966084
  5.3 3.2 %collective-permute-start = (f32[16,128,128]{2,1,0:T(8,128)}, f32[16,128,128]{2,1,0:T(8,128)S(1)}, u32[]{:S(2)}, u32[]{:S(2)}) collective-permute-start(f32[16,128,128]{2,1,0:T(8,128)} %shard_map.55), channel_id=1, source_target_pairs={{0,1},{1,0},{2,3},{3,2},{4,5},{5,4},{6,7},{7,6},{8,9},{9,8},{10,11... | collective-permute-start | bytes 3145736 | tf_op jit(solution)/shard_map/ppermute | solution.py:205
  8.4 17.5 %copy-start.4 = (f32[16,128,128]{2,1,0:T(8,128)}, f32[16,128,128]{2,1,0:T(8,128)S(1)}, u32[]{:S(2)}) copy-start(f32[16,128,128]{2,1,0:T(8,128)S(1)} %collective-permute-done) | copy-start | bytes 3145732
  10.2 13.2 %collective-permute-start.1 = (f32[8,128,128]{2,1,0:T(8,128)S(1)}, f32[8,128,128]{2,1,0:T(8,128)S(1)}, u32[]{:S(2)}, u32[]{:S(2)}) collective-permute-start(f32[8,128,128]{2,1,0:T(8,128)S(1)} %constant_dynamic-slice_fusion), channel_id=1, source_target_pairs={{0,2},{2,0},{1,3},{3,1},{4,6},{6,4},{5,7},{7,5},{8,10},{10,8},{9,1... | collective-permute-start | bytes 1572872 | tf_op jit(solution)/shard_map/ppermute | solution.py:205
  23.4 2.9 %collective-permute-start.2 = (f32[8,128,128]{2,1,0:T(8,128)S(1)}, f32[8,128,128]{2,1,0:T(8,128)}, u32[]{:S(2)}, u32[]{:S(2)}) collective-permute-start(f32[8,128,128]{2,1,0:T(8,128)S(1)} %collective-permute-done.1), channel_id=1, source_target_pairs={{0,1},{1,0},{2,3},{3,2},{4,5},{5,4},{6,7},{7,6},{8,9},{9,8},{10,11... | collective-permute-start | bytes 1572872 | tf_op jit(solution)/shard_map/ppermute | solution.py:205
  27.4 0.8 copy-start
  27.4 1.5 %copy-start.2 = (f32[8,128,128]{2,1,0:T(8,128)}, f32[8,128,128]{2,1,0:T(8,128)S(1)}, u32[]{:S(2)}) copy-start(f32[8,128,128]{2,1,0:T(8,128)S(1)} %get-tuple-element.15) | copy-start | bytes 1572868
  29.0 24.8 %collective-permute-start.3 = (f32[4,128,128]{2,1,0:T(8,128)}, f32[4,128,128]{2,1,0:T(8,128)}, u32[]{:S(2)}, u32[]{:S(2)}) collective-permute-start(f32[4,128,128]{2,1,0:T(8,128)} %fusion.11), channel_id=1, source_target_pairs={{0,4},{4,0},{8,12},{12,8},{16,20},{20,16},{24,28},{28,24},{1,5},{5... | collective-permute-start | bytes 786440 | tf_op jit(solution)/shard_map/ppermute | solution.py:205
  55.6 12.1 %collective-permute-start.7 = (f32[4,128,128]{2,1,0:T(8,128)}, f32[4,128,128]{2,1,0:T(8,128)}, u32[]{:S(2)}, u32[]{:S(2)}) collective-permute-start(f32[4,128,128]{2,1,0:T(8,128)} %add.24), channel_id=1, source_target_pairs={{0,8},{8,0},{4,12},{12,4},{16,24},{24,16},{20,28},{28,20},{1,9},{9... | collective-permute-start | bytes 786440 | tf_op jit(solution)/shard_map/ppermute | solution.py:205
  55.7 14.6 %collective-permute-start.4 = (f32[4,128,128]{2,1,0:T(8,128)}, f32[4,128,128]{2,1,0:T(8,128)}, u32[]{:S(2)}, u32[]{:S(2)}) collective-permute-start(f32[4,128,128]{2,1,0:T(8,128)} %collective-permute-done.3), channel_id=1, source_target_pairs={{0,2},{1,3},{2,0},{3,1},{4,6},{5,7},{6,4},{7,5},{8,10},{9,11},{10,... | collective-permute-start | bytes 786440 | tf_op jit(solution)/shard_map/ppermute | solution.py:210
  63.9 6.7 %copy-start.5 = (f32[16,128,128]{2,1,0:T(8,128)S(1)}, f32[16,128,128]{2,1,0:T(8,128)}, u32[]{:S(2)}) copy-start(f32[16,128,128]{2,1,0:T(8,128)} %copy-done.4) | copy-start | bytes 3145732
  63.9 7.6 %copy-start.1 = (f32[8,128,128]{2,1,0:T(8,128)S(1)}, f32[8,128,128]{2,1,0:T(8,128)}, u32[]{:S(2)}) copy-start(f32[8,128,128]{2,1,0:T(8,128)} %copy-done) | copy-start | bytes 1572868
  63.9 7.6 %copy-start.3 = (f32[8,128,128]{2,1,0:T(8,128)S(1)}, f32[8,128,128]{2,1,0:T(8,128)}, u32[]{:S(2)}) copy-start(f32[8,128,128]{2,1,0:T(8,128)} %copy-done.2) | copy-start | bytes 1572868
  66.4 18.8 %collective-permute-start.6 = (f32[4,128,128]{2,1,0:T(8,128)}, f32[4,128,128]{2,1,0:T(8,128)S(1)}, u32[]{:S(2)}, u32[]{:S(2)}) collective-permute-start(f32[4,128,128]{2,1,0:T(8,128)} %collective-permute-done.3), channel_id=1, source_target_pairs={{0,1},{1,0},{2,3},{3,2},{4,5},{5,4},{6,7},{7,6},{8,9},{9,8},{10,11... | collective-permute-start | bytes 786440 | tf_op jit(solution)/shard_map/ppermute | solution.py:210
  68.7 16.3 %collective-permute-start.11 = (f32[4,128,128]{2,1,0:T(8,128)S(1)}, f32[4,128,128]{2,1,0:T(8,128)S(1)}, u32[]{:S(2)}, u32[]{:S(2)}) collective-permute-start(f32[4,128,128]{2,1,0:T(8,128)S(1)} %add.25), channel_id=1, source_target_pairs={{0,16},{4,20},{8,24},{12,28},{1,17},{5,21},{9,25},{13,29},{2,18},{... | collective-permute-start | bytes 786440 | tf_op jit(solution)/shard_map/ppermute | solution.py:205
  70.0 16.4 %collective-permute-start.8 = (f32[4,128,128]{2,1,0:T(8,128)}, f32[4,128,128]{2,1,0:T(8,128)S(1)}, u32[]{:S(2)}, u32[]{:S(2)}) collective-permute-start(f32[4,128,128]{2,1,0:T(8,128)} %collective-permute-done.7), channel_id=1, source_target_pairs={{0,2},{1,3},{2,0},{3,1},{4,6},{5,7},{6,4},{7,5},{8,10},{9,11},{10,... | collective-permute-start | bytes 786440 | tf_op jit(solution)/shard_map/ppermute | solution.py:210
  70.3 16.1 %collective-permute-start.5 = (f32[4,128,128]{2,1,0:T(8,128)}, f32[4,128,128]{2,1,0:T(8,128)S(1)}, u32[]{:S(2)}, u32[]{:S(2)}) collective-permute-start(f32[4,128,128]{2,1,0:T(8,128)} %collective-permute-done.4), channel_id=1, source_target_pairs={{0,1},{1,0},{2,3},{3,2},{4,5},{5,4},{6,7},{7,6},{8,9},{9,8},{10,11... | collective-permute-start | bytes 786440 | tf_op jit(solution)/shard_map/ppermute | solution.py:210
  72.5 21.2 %collective-permute-start.10 = (f32[4,128,128]{2,1,0:T(8,128)}, f32[4,128,128]{2,1,0:T(8,128)S(1)}, u32[]{:S(2)}, u32[]{:S(2)}) collective-permute-start(f32[4,128,128]{2,1,0:T(8,128)} %collective-permute-done.7), channel_id=1, source_target_pairs={{0,1},{1,0},{2,3},{3,2},{4,5},{5,4},{6,7},{7,6},{8,9},{9,8},{10,11... | collective-permute-start | bytes 786440 | tf_op jit(solution)/shard_map/ppermute | solution.py:210
  85.0 7.0 %collective-permute-start.12 = (f32[4,128,128]{2,1,0:T(8,128)S(1)}, f32[4,128,128]{2,1,0:T(8,128)S(1)}, u32[]{:S(2)}, u32[]{:S(2)}) collective-permute-start(f32[4,128,128]{2,1,0:T(8,128)S(1)} %collective-permute-done.11), channel_id=1, source_target_pairs={{0,2},{1,3},{2,0},{3,1},{4,6},{5,7},{6,4},{7,5},{8,10},{9,11},{10,... | collective-permute-start | bytes 786440 | tf_op jit(solution)/shard_map/ppermute | solution.py:210
  85.2 11.5 %collective-permute-start.14 = (f32[4,128,128]{2,1,0:T(8,128)S(1)}, f32[4,128,128]{2,1,0:T(8,128)S(1)}, u32[]{:S(2)}, u32[]{:S(2)}) collective-permute-start(f32[4,128,128]{2,1,0:T(8,128)S(1)} %collective-permute-done.11), channel_id=1, source_target_pairs={{0,1},{1,0},{2,3},{3,2},{4,5},{5,4},{6,7},{7,6},{8,9},{9,8},{10,11... | collective-permute-start | bytes 786440 | tf_op jit(solution)/shard_map/ppermute | solution.py:210
  86.4 7.3 %collective-permute-start.9 = (f32[4,128,128]{2,1,0:T(8,128)S(1)}, f32[4,128,128]{2,1,0:T(8,128)S(1)}, u32[]{:S(2)}, u32[]{:S(2)}) collective-permute-start(f32[4,128,128]{2,1,0:T(8,128)S(1)} %collective-permute-done.8), channel_id=1, source_target_pairs={{0,1},{1,0},{2,3},{3,2},{4,5},{5,4},{6,7},{7,6},{8,9},{9,8},{10,11... | collective-permute-start | bytes 786440 | tf_op jit(solution)/shard_map/ppermute | solution.py:210
  92.0 4.8 %collective-permute-start.13 = (f32[4,128,128]{2,1,0:T(8,128)S(1)}, f32[4,128,128]{2,1,0:T(8,128)S(1)}, u32[]{:S(2)}, u32[]{:S(2)}) collective-permute-start(f32[4,128,128]{2,1,0:T(8,128)S(1)} %collective-permute-done.12), channel_id=1, source_target_pairs={{0,1},{1,0},{2,3},{3,2},{4,5},{5,4},{6,7},{7,6},{8,9},{9,8},{10,11... | collective-permute-start | bytes 786440 | tf_op jit(solution)/shard_map/ppermute | solution.py:210

commit v5 on v2

--- a/solution.py
+++ b/solution.py
@@ -148,11 +148,10 @@
                 q_ref[r0:r0 + TQ, j * dk:(j + 1) * dk], sib,
                 preferred_element_type=jnp.float32,
             )
-            mix = m_ref[j, r0:r0 + TQ, :]
-            cross = jnp.zeros((TQ, dv), jnp.float32)
-            for b in range(bits):
-                w = mix[:, first_level + b:first_level + b + 1] * scale
-                cross = cross + w * t[:, b * dv:(b + 1) * dv]
+            w_all = m_ref[j, r0:r0 + TQ, first_level:first_level + bits] * scale
+            cross = w_all[:, 0:1] * t[:, 0:dv]
+            for b in range(1, bits):
+                cross = cross + w_all[:, b:b + 1] * t[:, b * dv:(b + 1) * dv]
             o_ref[r0:r0 + TQ, j * dv:(j + 1) * dv] = (
                 l_ref[r0:r0 + TQ, j * dv:(j + 1) * dv] + cross
             )

time: 116 us -> 116 us (level)
  no operation moved by 1% of the time
where the time goes in v5:
time: 116 us; the launch traced here: 115 us
  Pallas kernels  49.9 us (43%)
  waiting for transfers between devices  31 us (27%)
  other arithmetic  16.8 us (14%)
  starting transfers between devices  11.7 us (10%)
  local copies, waits for them, and re-layouts  5.6 us (5%)
    pallas_call x4, Pallas kernels, local_part(): pl.pallas_call(functools.partial(local_kernel, scale, rows, group), grid=...  28 us
    ppermute x6, waiting for transfers between devices, swap(): return lax.ppermute(block, axis, route)  26.8 us
    pallas_call x1, Pallas kernels, cross_all(): pl.pallas_call(functools.partial(cross_kernel, scale, rows, first_level,...  16.6 us
    ppermute x6, starting transfers between devices, swap(): return lax.ppermute(block, axis, route)  6.06 us
    ppermute x9, starting transfers between devices, to_offset(): return lax.ppermute(block, axis, [(s, s ^ offset) for s in range(count)])  5.67 us
    unnamed x13, local copies, waits for them, and re-layouts  5.55 us
    pallas_call x1, Pallas kernels, own_state(): pl.pallas_call(functools.partial(state_kernel, head_count), grid=(rows //...  5.25 us
    unnamed x4, other arithmetic  5.01 us
  transfers between devices with their start and end apart: 15, of which 5 were waited for; matrix products, arithmetic and copies ran while one was open for 13% of the time, Pallas kernels for 24%

profile of v5, /device:TPU:25, one launch (start us, length us, event | category | flops | bytes accessed | tf_op | source)
XLA Modules:
  0.0 115.2 jit_solution(5512691474418423271)
XLA Ops:
  0.0 5.2 %shard_map.55 = f32[16,128,128]{2,1,0:T(8,128)} custom-call(bf16[1024,2048]{1,0:T(8,128)(2,1)} %k_ref.9, bf16[1024,2048]{1,0:T(8,128)(2,1)} %v_ref.9), custom_call_target="tpu_custom_call" | custom-call | flops 536870912 | bytes 9437184 | tf_op jit(solution)/shard_map/pallas_call | solution.py:51
  5.3 0.7 collective-permute-start
  5.9 2.5 %collective-permute-done = f32[16,128,128]{2,1,0:T(8,128)S(1)} collective-permute-done((f32[16,128,128]{2,1,0:T(8,128)}, f32[16,128,128]{2,1,0:T(8,128)S(1)}, u32[]{:S(2)}, u32[]{:S(2)}) %collective-permute-start) | collective-permute-done | bytes 1048608 | tf_op jit(solution)/shard_map/ppermute | solution.py:197
  8.4 1.7 %add.18 = f32[16,128,128]{2,1,0:T(8,128)S(1)} add(f32[16,128,128]{2,1,0:T(8,128)} %shard_map.55, f32[16,128,128]{2,1,0:T(8,128)S(1)} %collective-permute-done) | non-fusion elementwise | flops 262144 | bytes 3145728 | tf_op jit(solution)/shard_map/add | solution.py:240
  10.1 0.0 copy-start.5
  10.2 1.3 %collective-permute-start.1 = (f32[8,128,128]{2,1,0:T(8,128)S(1)}, f32[8,128,128]{2,1,0:T(8,128)S(1)}, u32[]{:S(2)}, u32[]{:S(2)}) collective-permute-start(f32[8,128,128]{2,1,0:T(8,128)S(1)} %constant_dynamic-slice_fusion), channel_id=1, source_target_pairs={{0,2},{2,0},{1,3},{3,1},{4,6},{6,4},{5,7},{7,5},{8,10},{10,8},{9,1... | collective-permute-start | bytes 1572872 | tf_op jit(solution)/shard_map/ppermute | solution.py:197
  11.5 11.9 %collective-permute-done.1 = f32[8,128,128]{2,1,0:T(8,128)S(1)} collective-permute-done((f32[8,128,128]{2,1,0:T(8,128)S(1)}, f32[8,128,128]{2,1,0:T(8,128)S(1)}, u32[]{:S(2)}, u32[]{:S(2)}) %collective-permute-start.1) | collective-permute-done | bytes 524320 | tf_op jit(solution)/shard_map/ppermute | solution.py:197
  23.4 1.2 %collective-permute-start.2 = (f32[8,128,128]{2,1,0:T(8,128)S(1)}, f32[8,128,128]{2,1,0:T(8,128)}, u32[]{:S(2)}, u32[]{:S(2)}) collective-permute-start(f32[8,128,128]{2,1,0:T(8,128)S(1)} %collective-permute-done.1), channel_id=1, source_target_pairs={{0,1},{1,0},{2,3},{3,2},{4,5},{5,4},{6,7},{7,6},{8,9},{9,8},{10,11... | collective-permute-start | bytes 1572872 | tf_op jit(solution)/shard_map/ppermute | solution.py:197
  24.6 1.7 %collective-permute-done.2 = f32[8,128,128]{2,1,0:T(8,128)} collective-permute-done((f32[8,128,128]{2,1,0:T(8,128)S(1)}, f32[8,128,128]{2,1,0:T(8,128)}, u32[]{:S(2)}, u32[]{:S(2)}) %collective-permute-start.2) | collective-permute-done | bytes 524320 | tf_op jit(solution)/shard_map/ppermute | solution.py:197
  26.3 1.1 broadcast_select_fusion.1
  27.5 0.8 copy-done
  28.3 0.8 fusion.11
  29.0 1.2 %collective-permute-start.3 = (f32[4,128,128]{2,1,0:T(8,128)}, f32[4,128,128]{2,1,0:T(8,128)}, u32[]{:S(2)}, u32[]{:S(2)}) collective-permute-start(f32[4,128,128]{2,1,0:T(8,128)} %fusion.11), channel_id=1, source_target_pairs={{0,4},{4,0},{8,12},{12,8},{16,20},{20,16},{24,28},{28,24},{1,5},{5... | collective-permute-start | bytes 786440 | tf_op jit(solution)/shard_map/ppermute | solution.py:197
  30.3 4.7 %copy.10 = f32[10,16,1024]{0,2,1:T(8,128)} copy(f32[10,16,1024]{2,1,0:T(8,128)S(1)} %copy-done.5) | data formatting | bytes 1310720 | tf_op args[3]
  35.0 7.1 %shard_map.56.rest_0_ = f32[1024,2048]{1,0:T(8,128)} custom-call(bf16[1024,2048]{1,0:T(8,128)(2,1)} %q_ref.9, bf16[1024,2048]{1,0:T(8,128)(2,1)} %k_ref.9, bf16[1024,2048]{1,0:T(8,128)(2,1)} %v_ref.9, f32[16,1024,10]{2,1,0:T(8,128)} %bitcast.31, f32[3,256,256]{2,1,0:T(8,128)} %constant.27.clone.c_ref), custom_call_target="tpu_custom_call" | custom-call | flops 1342177280 | bytes 5242880 | tf_op jit(solution)/shard_map/pallas_call | solution.py:123
  42.1 1.8 %add.22 = f32[4,128,128]{2,1,0:T(8,128)} add(f32[4,128,128]{2,1,0:T(8,128)} %fusion.11, f32[4,128,128]{2,1,0:T(8,128)} %collective-permute-done.3) | non-fusion elementwise | flops 65536 | bytes 786432 | tf_op jit(solution)/shard_map/add | solution.py:249
  43.9 0.2 collective-permute-start.7
  44.1 1.2 %collective-permute-start.4 = (f32[4,128,128]{2,1,0:T(8,128)}, f32[4,128,128]{2,1,0:T(8,128)}, u32[]{:S(2)}, u32[]{:S(2)}) collective-permute-start(f32[4,128,128]{2,1,0:T(8,128)} %collective-permute-done.3), channel_id=1, source_target_pairs={{0,2},{1,3},{2,0},{3,1},{4,6},{5,7},{6,4},{7,5},{8,10},{9,11},{10,... | collective-permute-start | bytes 786440 | tf_op jit(solution)/shard_map/ppermute | solution.py:202
  45.3 7.0 %shard_map.57.rest_0_ = f32[1024,2048]{1,0:T(8,128)} custom-call(bf16[1024,2048]{1,0:T(8,128)(2,1)} %q_ref.9, bf16[1024,2048]{1,0:T(8,128)(2,1)} %k_ref.9, bf16[1024,2048]{1,0:T(8,128)(2,1)} %v_ref.9, f32[16,1024,10]{2,1,0:T(8,128)} %bitcast.32, f32[3,256,256]{2,1,0:T(8,128)} %constant.27.clone.c_ref, ...), custom_call_target="tpu_custom_call", output_to_operand_aliasing={{}: (5, {})} | custom-call | flops 1342177280 | bytes 5242880 | tf_op jit(solution)/shard_map/pallas_call | solution.py:123
  52.2 7.0 %shard_map.58.rest_0_ = f32[1024,2048]{1,0:T(8,128)} custom-call(bf16[1024,2048]{1,0:T(8,128)(2,1)} %q_ref.9, bf16[1024,2048]{1,0:T(8,128)(2,1)} %k_ref.9, bf16[1024,2048]{1,0:T(8,128)(2,1)} %v_ref.9, f32[16,1024,10]{2,1,0:T(8,128)} %bitcast.33, f32[3,256,256]{2,1,0:T(8,128)} %constant.27.clone.c_ref, ...), custom_call_target="tpu_custom_call", output_to_operand_aliasing={{}: (5, {})} | custom-call | flops 1342177280 | bytes 5242880 | tf_op jit(solution)/shard_map/pallas_call | solution.py:123
  59.2 7.0 %shard_map.59.l_ref = f32[1024,2048]{1,0:T(8,128)} custom-call(bf16[1024,2048]{1,0:T(8,128)(2,1)} %q_ref.9, bf16[1024,2048]{1,0:T(8,128)(2,1)} %k_ref.9, bf16[1024,2048]{1,0:T(8,128)(2,1)} %v_ref.9, f32[16,1024,10]{2,1,0:T(8,128)} %bitcast.34, f32[3,256,256]{2,1,0:T(8,128)} %constant.27.clone.c_ref, ...), custom_call_target="tpu_custom_call", output_to_operand_aliasing={{}: (5, {})} | custom-call | flops 1342177280 | bytes 5242880 | tf_op jit(solution)/shard_map/pallas_call | solution.py:123
  66.2 1.3 %collective-permute-start.6 = (f32[4,128,128]{2,1,0:T(8,128)}, f32[4,128,128]{2,1,0:T(8,128)S(1)}, u32[]{:S(2)}, u32[]{:S(2)}) collective-permute-start(f32[4,128,128]{2,1,0:T(8,128)} %collective-permute-done.3), channel_id=1, source_target_pairs={{0,1},{1,0},{2,3},{3,2},{4,5},{5,4},{6,7},{7,6},{8,9},{9,8},{10,11... | collective-permute-start | bytes 786440 | tf_op jit(solution)/shard_map/ppermute | solution.py:202
  67.5 1.1 add.23
  68.5 1.5 %collective-permute-start.11 = (f32[4,128,128]{2,1,0:T(8,128)S(1)}, f32[4,128,128]{2,1,0:T(8,128)S(1)}, u32[]{:S(2)}, u32[]{:S(2)}) collective-permute-start(f32[4,128,128]{2,1,0:T(8,128)S(1)} %add.23), channel_id=1, source_target_pairs={{0,16},{4,20},{8,24},{12,28},{1,17},{5,21},{9,25},{13,29},{2,18},{... | collective-permute-start | bytes 786440 | tf_op jit(solution)/shard_map/ppermute | solution.py:197
  70.0 0.3 collective-permute-start.8
  70.3 0.4 collective-permute-start.5
  70.7 2.2 %fusion.5 = bf16[5,16,128,128]{3,2,1,0:T(8,128)(2,1)} fusion(f32[16,128,128]{2,1,0:T(8,128)} %copy-done.4, f32[]{:T(128)S(6)} %convert_element_type.58), kind=kLoop, calls=%fused_computation.12 | loop fusion | flops 524287 | bytes 1572868
  72.9 0.9 fusion.9
  73.8 0.1 collective-permute-start.10
  74.0 10.7 %collective-permute-done.11 = f32[4,128,128]{2,1,0:T(8,128)S(1)} collective-permute-done((f32[4,128,128]{2,1,0:T(8,128)S(1)}, f32[4,128,128]{2,1,0:T(8,128)S(1)}, u32[]{:S(2)}, u32[]{:S(2)}) %collective-permute-start.11) | collective-permute-done | bytes 262176 | tf_op jit(solution)/shard_map/ppermute | solution.py:197
  84.7 0.9 collective-permute-start.14
  85.7 0.0 collective-permute-done.6
  85.7 0.3 collective-permute-start.12
  85.9 0.0 collective-permute-done.8
  85.9 0.3 collective-permute-start.9
  86.2 1.1 select_bitcast_fusion.11
  87.4 1.0 select_bitcast_fusion.10
  88.4 0.9 fusion.8
  89.3 4.2 %collective-permute-done.12 = f32[4,128,128]{2,1,0:T(8,128)S(1)} collective-permute-done((f32[4,128,128]{2,1,0:T(8,128)S(1)}, f32[4,128,128]{2,1,0:T(8,128)S(1)}, u32[]{:S(2)}, u32[]{:S(2)}) %collective-permute-start.12) | collective-permute-done | bytes 262176 | tf_op jit(solution)/shard_map/ppermute | solution.py:202
  93.5 0.9 collective-permute-start.13
  94.4 0.0 collective-permute-done.9
  94.4 1.1 select_bitcast_fusion.7
  95.5 1.0 select_bitcast_fusion.6
  96.5 0.9 fusion.7
  97.5 0.1 select_bitcast_fusion.2
  97.5 0.1 select_bitcast_fusion.3
  97.6 0.9 fusion.6.s_ref
  98.6 16.6 %shard_map.60 = f32[1024,2048]{1,0:T(8,128)} custom-call(bf16[1024,2048]{1,0:T(8,128)(2,1)} %q_ref.9, bf16[5,16,128,128]{3,2,1,0:T(8,128)(2,1)} %fusion.6.s_ref, f32[16,1024,10]{2,1,0:T(8,128)} %bitcast.35, f32[1024,2048]{1,0:T(8,128)} %shard_map.59.l_ref), custom_call_target="tpu_custom_call", output_to_operand_aliasing={{}: (3, {})} | custom-call | flops 2684354560 | bytes 20971520 | tf_op jit(solution)/shard_map/pallas_call | solution.py:167
  (18 shorter events, 0.1 us)
Async XLA Ops:
  5.3 3.2 %collective-permute-start = (f32[16,128,128]{2,1,0:T(8,128)}, f32[16,128,128]{2,1,0:T(8,128)S(1)}, u32[]{:S(2)}, u32[]{:S(2)}) collective-permute-start(f32[16,128,128]{2,1,0:T(8,128)} %shard_map.55), channel_id=1, source_target_pairs={{0,1},{1,0},{2,3},{3,2},{4,5},{5,4},{6,7},{7,6},{8,9},{9,8},{10,11... | collective-permute-start | bytes 3145736 | tf_op jit(solution)/shard_map/ppermute | solution.py:197
  8.4 19.0 %copy-start.4 = (f32[16,128,128]{2,1,0:T(8,128)}, f32[16,128,128]{2,1,0:T(8,128)S(1)}, u32[]{:S(2)}) copy-start(f32[16,128,128]{2,1,0:T(8,128)S(1)} %collective-permute-done) | copy-start | bytes 3145732
  10.1 20.1 %copy-start.5 = (f32[10,16,1024]{2,1,0:T(8,128)S(1)}, f32[10,16,1024]{2,1,0:T(8,128)}, u32[]{:S(2)}) copy-start(f32[10,16,1024]{2,1,0:T(8,128)} %param.8) | copy-start | bytes 1966084
  10.2 13.2 %collective-permute-start.1 = (f32[8,128,128]{2,1,0:T(8,128)S(1)}, f32[8,128,128]{2,1,0:T(8,128)S(1)}, u32[]{:S(2)}, u32[]{:S(2)}) collective-permute-start(f32[8,128,128]{2,1,0:T(8,128)S(1)} %constant_dynamic-slice_fusion), channel_id=1, source_target_pairs={{0,2},{2,0},{1,3},{3,1},{4,6},{6,4},{5,7},{7,5},{8,10},{10,8},{9,1... | collective-permute-start | bytes 1572872 | tf_op jit(solution)/shard_map/ppermute | solution.py:197
  23.4 2.9 %collective-permute-start.2 = (f32[8,128,128]{2,1,0:T(8,128)S(1)}, f32[8,128,128]{2,1,0:T(8,128)}, u32[]{:S(2)}, u32[]{:S(2)}) collective-permute-start(f32[8,128,128]{2,1,0:T(8,128)S(1)} %collective-permute-done.1), channel_id=1, source_target_pairs={{0,1},{1,0},{2,3},{3,2},{4,5},{5,4},{6,7},{7,6},{8,9},{9,8},{10,11... | collective-permute-start | bytes 1572872 | tf_op jit(solution)/shard_map/ppermute | solution.py:197
  27.4 0.8 copy-start
  27.4 1.6 %copy-start.2 = (f32[8,128,128]{2,1,0:T(8,128)}, f32[8,128,128]{2,1,0:T(8,128)S(1)}, u32[]{:S(2)}) copy-start(f32[8,128,128]{2,1,0:T(8,128)S(1)} %get-tuple-element.15) | copy-start | bytes 1572868
  29.0 13.1 %collective-permute-start.3 = (f32[4,128,128]{2,1,0:T(8,128)}, f32[4,128,128]{2,1,0:T(8,128)}, u32[]{:S(2)}, u32[]{:S(2)}) collective-permute-start(f32[4,128,128]{2,1,0:T(8,128)} %fusion.11), channel_id=1, source_target_pairs={{0,4},{4,0},{8,12},{12,8},{16,20},{20,16},{24,28},{28,24},{1,5},{5... | collective-permute-start | bytes 786440 | tf_op jit(solution)/shard_map/ppermute | solution.py:197
  43.9 23.6 %collective-permute-start.7 = (f32[4,128,128]{2,1,0:T(8,128)}, f32[4,128,128]{2,1,0:T(8,128)}, u32[]{:S(2)}, u32[]{:S(2)}) collective-permute-start(f32[4,128,128]{2,1,0:T(8,128)} %add.22), channel_id=1, source_target_pairs={{0,8},{8,0},{4,12},{12,4},{16,24},{24,16},{20,28},{28,20},{1,9},{9... | collective-permute-start | bytes 786440 | tf_op jit(solution)/shard_map/ppermute | solution.py:197
  44.1 26.3 %collective-permute-start.4 = (f32[4,128,128]{2,1,0:T(8,128)}, f32[4,128,128]{2,1,0:T(8,128)}, u32[]{:S(2)}, u32[]{:S(2)}) collective-permute-start(f32[4,128,128]{2,1,0:T(8,128)} %collective-permute-done.3), channel_id=1, source_target_pairs={{0,2},{1,3},{2,0},{3,1},{4,6},{5,7},{6,4},{7,5},{8,10},{9,11},{10,... | collective-permute-start | bytes 786440 | tf_op jit(solution)/shard_map/ppermute | solution.py:202
  66.2 6.7 %copy-start.1 = (f32[8,128,128]{2,1,0:T(8,128)S(1)}, f32[8,128,128]{2,1,0:T(8,128)}, u32[]{:S(2)}) copy-start(f32[8,128,128]{2,1,0:T(8,128)} %copy-done) | copy-start | bytes 1572868
  66.2 6.7 %copy-start.3 = (f32[8,128,128]{2,1,0:T(8,128)S(1)}, f32[8,128,128]{2,1,0:T(8,128)}, u32[]{:S(2)}) copy-start(f32[8,128,128]{2,1,0:T(8,128)} %copy-done.2) | copy-start | bytes 1572868
  66.2 19.5 %collective-permute-start.6 = (f32[4,128,128]{2,1,0:T(8,128)}, f32[4,128,128]{2,1,0:T(8,128)S(1)}, u32[]{:S(2)}, u32[]{:S(2)}) collective-permute-start(f32[4,128,128]{2,1,0:T(8,128)} %collective-permute-done.3), channel_id=1, source_target_pairs={{0,1},{1,0},{2,3},{3,2},{4,5},{5,4},{6,7},{7,6},{8,9},{9,8},{10,11... | collective-permute-start | bytes 786440 | tf_op jit(solution)/shard_map/ppermute | solution.py:202
  68.5 16.2 %collective-permute-start.11 = (f32[4,128,128]{2,1,0:T(8,128)S(1)}, f32[4,128,128]{2,1,0:T(8,128)S(1)}, u32[]{:S(2)}, u32[]{:S(2)}) collective-permute-start(f32[4,128,128]{2,1,0:T(8,128)S(1)} %add.23), channel_id=1, source_target_pairs={{0,16},{4,20},{8,24},{12,28},{1,17},{5,21},{9,25},{13,29},{2,18},{... | collective-permute-start | bytes 786440 | tf_op jit(solution)/shard_map/ppermute | solution.py:197
  70.0 15.9 %collective-permute-start.8 = (f32[4,128,128]{2,1,0:T(8,128)}, f32[4,128,128]{2,1,0:T(8,128)S(1)}, u32[]{:S(2)}, u32[]{:S(2)}) collective-permute-start(f32[4,128,128]{2,1,0:T(8,128)} %collective-permute-done.7), channel_id=1, source_target_pairs={{0,2},{1,3},{2,0},{3,1},{4,6},{5,7},{6,4},{7,5},{8,10},{9,11},{10,... | collective-permute-start | bytes 786440 | tf_op jit(solution)/shard_map/ppermute | solution.py:202
  70.3 15.9 %collective-permute-start.5 = (f32[4,128,128]{2,1,0:T(8,128)}, f32[4,128,128]{2,1,0:T(8,128)S(1)}, u32[]{:S(2)}, u32[]{:S(2)}) collective-permute-start(f32[4,128,128]{2,1,0:T(8,128)} %collective-permute-done.4), channel_id=1, source_target_pairs={{0,1},{1,0},{2,3},{3,2},{4,5},{5,4},{6,7},{7,6},{8,9},{9,8},{10,11... | collective-permute-start | bytes 786440 | tf_op jit(solution)/shard_map/ppermute | solution.py:202
  73.8 20.5 %collective-permute-start.10 = (f32[4,128,128]{2,1,0:T(8,128)}, f32[4,128,128]{2,1,0:T(8,128)S(1)}, u32[]{:S(2)}, u32[]{:S(2)}) collective-permute-start(f32[4,128,128]{2,1,0:T(8,128)} %collective-permute-done.7), channel_id=1, source_target_pairs={{0,1},{1,0},{2,3},{3,2},{4,5},{5,4},{6,7},{7,6},{8,9},{9,8},{10,11... | collective-permute-start | bytes 786440 | tf_op jit(solution)/shard_map/ppermute | solution.py:202
  84.7 12.7 %collective-permute-start.14 = (f32[4,128,128]{2,1,0:T(8,128)S(1)}, f32[4,128,128]{2,1,0:T(8,128)S(1)}, u32[]{:S(2)}, u32[]{:S(2)}) collective-permute-start(f32[4,128,128]{2,1,0:T(8,128)S(1)} %collective-permute-done.11), channel_id=1, source_target_pairs={{0,1},{1,0},{2,3},{3,2},{4,5},{5,4},{6,7},{7,6},{8,9},{9,8},{10,11... | collective-permute-start | bytes 786440 | tf_op jit(solution)/shard_map/ppermute | solution.py:202
  85.7 7.9 %collective-permute-start.12 = (f32[4,128,128]{2,1,0:T(8,128)S(1)}, f32[4,128,128]{2,1,0:T(8,128)S(1)}, u32[]{:S(2)}, u32[]{:S(2)}) collective-permute-start(f32[4,128,128]{2,1,0:T(8,128)S(1)} %collective-permute-done.11), channel_id=1, source_target_pairs={{0,2},{1,3},{2,0},{3,1},{4,6},{5,7},{6,4},{7,5},{8,10},{9,11},{10,... | collective-permute-start | bytes 786440 | tf_op jit(solution)/shard_map/ppermute | solution.py:202
  85.9 8.5 %collective-permute-start.9 = (f32[4,128,128]{2,1,0:T(8,128)S(1)}, f32[4,128,128]{2,1,0:T(8,128)S(1)}, u32[]{:S(2)}, u32[]{:S(2)}) collective-permute-start(f32[4,128,128]{2,1,0:T(8,128)S(1)} %collective-permute-done.8), channel_id=1, source_target_pairs={{0,1},{1,0},{2,3},{3,2},{4,5},{5,4},{6,7},{7,6},{8,9},{9,8},{10,11... | collective-permute-start | bytes 786440 | tf_op jit(solution)/shard_map/ppermute | solution.py:202
  93.5 3.9 %collective-permute-start.13 = (f32[4,128,128]{2,1,0:T(8,128)S(1)}, f32[4,128,128]{2,1,0:T(8,128)S(1)}, u32[]{:S(2)}, u32[]{:S(2)}) collective-permute-start(f32[4,128,128]{2,1,0:T(8,128)S(1)} %collective-permute-done.12), channel_id=1, source_target_pairs={{0,1},{1,0},{2,3},{3,2},{4,5},{5,4},{6,7},{7,6},{8,9},{9,8},{10,11... | collective-permute-start | bytes 786440 | tf_op jit(solution)/shard_map/ppermute | solution.py:202

commit v6 on v5

--- a/solution.py
+++ b/solution.py
@@ -12,7 +12,6 @@
 TQ = 256
 CHUNKS = 4
 LOCAL_GROUP = 2
-CROSS_GROUP = 4
 
 
 def level_masks(block, level_count):
@@ -136,12 +135,14 @@
     )(*operands)
 
 
-def cross_kernel(scale, rows, first_level, group, q_ref, s_ref, m_ref, l_ref, o_ref):
-    bits = s_ref.shape[0]
-    dk = s_ref.shape[2]
-    dv = s_ref.shape[3]
+def cross2_kernel(scale, rows, first_level, group, sp_ref, q_ref, e_ref, t_ref, m_ref, l_ref, o_ref):
+    bits = e_ref.shape[0] + 1
+    dk = e_ref.shape[2]
+    dv = e_ref.shape[3]
     for j in range(group):
-        sib = jnp.concatenate([s_ref[b, j] for b in range(bits)], axis=1)
+        sib = jnp.concatenate(
+            [e_ref[b, j] for b in range(bits - 1)] + [t_ref[0, j]], axis=1
+        )
         for a in range(rows // TQ):
             r0 = a * TQ
             t = jnp.dot(
@@ -157,32 +158,41 @@
             )
 
 
-def cross_all(queries, sibs, mix_t, local, scale, first_level, group):
+def cross_part2(queries, scalars, early, lastx, mix_t, prev, scale, first_level, group, base):
     rows = queries.shape[0]
     head_count = mix_t.shape[0]
     dk = queries.shape[1] // head_count
-    dv = sibs.shape[3]
+    dv = early.shape[3]
     levels = mix_t.shape[2]
-    bits = sibs.shape[0]
+    bits = early.shape[0] + 1
+    steps = lastx.shape[1] // group
+
+    def quarter(g, sp):
+        return jnp.bitwise_xor(sp[0], g + base)
+
     return pl.pallas_call(
-        functools.partial(cross_kernel, scale, rows, first_level, group),
-        grid=(head_count // group,),
-        in_specs=[
-            pl.BlockSpec((rows, dk * group), lambda g: (0, g)),
-            pl.BlockSpec((bits, group, dk, dv), lambda g: (0, g, 0, 0)),
-            pl.BlockSpec((group, rows, levels), lambda g: (g, 0, 0)),
-            pl.BlockSpec((rows, dv * group), lambda g: (0, g)),
-        ],
-        out_specs=pl.BlockSpec((rows, dv * group), lambda g: (0, g)),
+        functools.partial(cross2_kernel, scale, rows, first_level, group),
+        grid_spec=pltpu.PrefetchScalarGridSpec(
+            num_scalar_prefetch=1,
+            grid=(steps,),
+            in_specs=[
+                pl.BlockSpec((rows, dk * group), lambda g, sp: (0, quarter(g, sp))),
+                pl.BlockSpec((bits - 1, group, dk, dv), lambda g, sp: (0, quarter(g, sp), 0, 0)),
+                pl.BlockSpec((1, group, dk, dv), lambda g, sp: (0, g, 0, 0)),
+                pl.BlockSpec((group, rows, levels), lambda g, sp: (quarter(g, sp), 0, 0)),
+                pl.BlockSpec((rows, dv * group), lambda g, sp: (0, quarter(g, sp))),
+            ],
+            out_specs=pl.BlockSpec((rows, dv * group), lambda g, sp: (0, quarter(g, sp))),
+        ),
         out_shape=jax.ShapeDtypeStruct((rows, dv * head_count), jnp.float32),
-        input_output_aliases={3: 0},
+        input_output_aliases={5: 0},
         cost_estimate=pl.CostEstimate(
-            flops=2 * rows * dk * dv * bits * head_count,
-            bytes_accessed=(2 * rows * dk + 8 * rows * dv) * head_count,
+            flops=2 * rows * dk * dv * bits * group * steps,
+            bytes_accessed=(2 * rows * dk + 8 * rows * dv) * group * steps,
             transcendentals=0,
         ),
         compiler_params=pltpu.CompilerParams(vmem_limit_bytes=64 * 1024 * 1024),
-    )(queries, sibs, mix_t, local)
+    )(scalars, queries, early, lastx, mix_t, prev)
 
 
 def swap(block, axis, bit, one_way=False):
@@ -248,6 +258,7 @@
         if bit != ctx_bits - 1:
             quarter = quarter + got
 
+    gathered = []
     for bit in range(ctx_bits):
         part = lax.optimization_barrier(ctx_sibs[bit])
         parts = {0: part}
@@ -256,18 +267,33 @@
                 parts[offset] = to_offset(parts[offset ^ 1], "seq", 1)
             else:
                 parts[offset] = to_offset(part, "seq", offset)
+        gathered.append(parts)
+        flags.append(ctx_place >> bit & 1)
+    for bit in range(ctx_bits - 1):
+        parts = gathered[bit]
         full = []
         for owner in range(seq_count):
-            pick = jnp.zeros_like(part)
+            pick = jnp.zeros_like(parts[0])
             for offset in range(seq_count):
                 pick = jnp.where((seq_place ^ offset) == owner, parts[offset], pick)
             full.append(pick)
         sibs.append(jnp.concatenate(full, axis=0))
-        flags.append(ctx_place >> bit & 1)
-
-    rounded = jnp.stack(
+
+    early = jnp.stack(
         [(flags[i].astype(jnp.float32) * sibs[i]).astype(jnp.bfloat16) for i in range(len(sibs))]
     )
+    last_flag = flags[-1].astype(jnp.float32)
+    last_parts = gathered[-1]
+    split = seq_count // 2
+    share = head_count // seq_count
+
+    def last_of(offsets):
+        picked = [(last_flag * last_parts[o]).astype(jnp.bfloat16) for o in offsets]
+        return jnp.concatenate(picked, axis=0)[None]
+
+    last_a = last_of(range(split))
+    last_b = last_of(range(split, seq_count))
+    scalars = seq_place.astype(jnp.int32)[None]
 
     per = head_count // CHUNKS
     local = None
@@ -275,7 +301,10 @@
         local = local_part(
             queries, keys, values, mix_t, masks, c * per, per, LOCAL_GROUP, scale, local
         )
-    return cross_all(queries, rounded, mix_t, local, scale, level_count, CROSS_GROUP)
+    out = cross_part2(queries, scalars, early, last_a, mix_t, local, scale, level_count, share, 0)
+    return cross_part2(
+        queries, scalars, early, last_b, mix_t, out, scale, level_count, share, split
+    )
 
 
 def solution(mesh):

time: 116 us -> 118 us (1.017)
  the two profiles are of different devices: /device:TPU:25 before, /device:TPU:0 now
where the time goes in v6:
time: 118 us; the launch traced here: 117 us
  Pallas kernels  53.4 us (45%)
  waiting for transfers between devices  23.4 us (20%)
  starting transfers between devices  17.8 us (15%)
  other arithmetic  17.1 us (14%)
  local copies, waits for them, and re-layouts  5.64 us (5%)
    pallas_call x4, Pallas kernels, local_part(): pl.pallas_call(functools.partial(local_kernel, scale, rows, group), grid=...  28 us
    ppermute x6, waiting for transfers between devices, swap(): return lax.ppermute(block, axis, route)  23.3 us
    pallas_call x2, Pallas kernels, cross_part2(): pl.pallas_call(functools.partial(cross2_kernel, scale, rows, first_level,...  20.1 us
    ppermute x6, starting transfers between devices, swap(): return lax.ppermute(block, axis, route)  12.2 us
    ppermute x9, starting transfers between devices, to_offset(): return lax.ppermute(block, axis, [(s, s ^ offset) for s in range(count)])  5.62 us
    unnamed x9, local copies, waits for them, and re-layouts  5.6 us
    pallas_call x1, Pallas kernels, own_state(): pl.pallas_call(functools.partial(state_kernel, head_count), grid=(rows //...  5.25 us
    another operation x2, other arithmetic, shards(): jnp.stack([(flags[i].astype(jnp.float32) * sibs[i]).astype(jnp.bfloat16)...  3.91 us
  transfers between devices with their start and end apart: 15, of which 4 were waited for; matrix products, arithmetic and copies ran while one was open for 14% of the time, Pallas kernels for 32%

profile of v6, /device:TPU:0, one launch (start us, length us, event | category | flops | bytes accessed | tf_op | source)
XLA Modules:
  0.0 117.5 jit_solution(9561992379689395531)
XLA Ops:
  0.0 5.3 %shard_map.55 = f32[16,128,128]{2,1,0:T(8,128)} custom-call(bf16[1024,2048]{1,0:T(8,128)(2,1)} %k_ref.9, bf16[1024,2048]{1,0:T(8,128)(2,1)} %v_ref.9), custom_call_target="tpu_custom_call" | custom-call | flops 536870912 | bytes 9437184 | tf_op jit(solution)/shard_map/pallas_call | solution.py:50
  5.3 0.5 collective-permute-start
  5.7 2.5 %collective-permute-done = f32[16,128,128]{2,1,0:T(8,128)S(1)} collective-permute-done((f32[16,128,128]{2,1,0:T(8,128)}, f32[16,128,128]{2,1,0:T(8,128)S(1)}, u32[]{:S(2)}, u32[]{:S(2)}) %collective-permute-start) | collective-permute-done | bytes 1048608 | tf_op jit(solution)/shard_map/ppermute | solution.py:207
  8.2 2.3 %fusion.3 = (bf16[1,16,128,128]{3,2,1,0:T(8,128)(2,1)}, f32[16,128,128]{2,1,0:T(8,128)S(1)}) fusion(f32[16,128,128]{2,1,0:T(8,128)S(1)} %collective-permute-done, f32[]{:T(128)S(6)} %convert_element_type.60, f32[16,128,128]{2,1,0:T(8,128)} %shard_map.55), kind=kLoop, calls=%fused_computation.10 | loop fusion | flops 786432 | bytes 3670020 | tf_op jit(solution)/shard_map/stack | solution.py:282
  10.5 2.9 %collective-permute-start.1 = (f32[8,128,128]{2,1,0:T(8,128)S(1)}, f32[8,128,128]{2,1,0:T(8,128)S(1)}, u32[]{:S(2)}, u32[]{:S(2)}) collective-permute-start(f32[8,128,128]{2,1,0:T(8,128)S(1)} %constant_dynamic-slice_fusion), channel_id=1, source_target_pairs={{0,2},{2,0},{1,3},{3,1},{4,6},{6,4},{5,7},{7,5},{8,10},{10,8},{9,1... | collective-permute-start | bytes 1572872 | tf_op jit(solution)/shard_map/ppermute | solution.py:207
  13.4 12.2 %collective-permute-done.1 = f32[8,128,128]{2,1,0:T(8,128)S(1)} collective-permute-done((f32[8,128,128]{2,1,0:T(8,128)S(1)}, f32[8,128,128]{2,1,0:T(8,128)S(1)}, u32[]{:S(2)}, u32[]{:S(2)}) %collective-permute-start.1) | collective-permute-done | bytes 524320 | tf_op jit(solution)/shard_map/ppermute | solution.py:207
  25.7 1.9 %collective-permute-done.2 = f32[8,128,128]{2,1,0:T(8,128)S(1)} collective-permute-done((f32[8,128,128]{2,1,0:T(8,128)S(1)}, f32[8,128,128]{2,1,0:T(8,128)S(1)}, u32[]{:S(2)}, u32[]{:S(2)}) %collective-permute-start.2) | collective-permute-done | bytes 524320 | tf_op jit(solution)/shard_map/ppermute | solution.py:207
  27.6 0.1 broadcast_select_fusion
  27.7 0.8 copy-done
  28.5 0.1 fusion.5
  28.5 0.1 copy-done.1
  28.6 1.8 %collective-permute-start.3 = (f32[4,128,128]{2,1,0:T(8,128)S(1)}, f32[4,128,128]{2,1,0:T(8,128)}, u32[]{:S(2)}, u32[]{:S(2)}) collective-permute-start(f32[4,128,128]{2,1,0:T(8,128)S(1)} %fusion.5), channel_id=1, source_target_pairs={{0,4},{4,0},{8,12},{12,8},{16,20},{20,16},{24,28},{28,24},{1,5},{5... | collective-permute-start | bytes 786440 | tf_op jit(solution)/shard_map/ppermute | solution.py:207
  30.4 6.7 %collective-permute-done.3 = f32[4,128,128]{2,1,0:T(8,128)} collective-permute-done((f32[4,128,128]{2,1,0:T(8,128)S(1)}, f32[4,128,128]{2,1,0:T(8,128)}, u32[]{:S(2)}, u32[]{:S(2)}) %collective-permute-start.3) | collective-permute-done | bytes 262176 | tf_op jit(solution)/shard_map/ppermute | solution.py:207
  37.1 1.7 %add.22 = f32[4,128,128]{2,1,0:T(8,128)} add(f32[4,128,128]{2,1,0:T(8,128)S(1)} %fusion.5, f32[4,128,128]{2,1,0:T(8,128)} %collective-permute-done.3) | non-fusion elementwise | flops 65536 | bytes 786432 | tf_op jit(solution)/shard_map/add | solution.py:259
  38.8 1.8 %collective-permute-start.7 = (f32[4,128,128]{2,1,0:T(8,128)}, f32[4,128,128]{2,1,0:T(8,128)}, u32[]{:S(2)}, u32[]{:S(2)}) collective-permute-start(f32[4,128,128]{2,1,0:T(8,128)} %add.22), channel_id=1, source_target_pairs={{0,8},{8,0},{4,12},{12,4},{16,24},{24,16},{20,28},{28,20},{1,9},{9... | collective-permute-start | bytes 786440 | tf_op jit(solution)/shard_map/ppermute | solution.py:207
  40.6 1.5 %collective-permute-start.4 = (f32[4,128,128]{2,1,0:T(8,128)}, f32[4,128,128]{2,1,0:T(8,128)}, u32[]{:S(2)}, u32[]{:S(2)}) collective-permute-start(f32[4,128,128]{2,1,0:T(8,128)} %collective-permute-done.3), channel_id=1, source_target_pairs={{0,2},{1,3},{2,0},{3,1},{4,6},{5,7},{6,4},{7,5},{8,10},{9,11},{10,... | collective-permute-start | bytes 786440 | tf_op jit(solution)/shard_map/ppermute | solution.py:212
  42.1 4.7 %copy.11 = f32[10,16,1024]{0,2,1:T(8,128)} copy(f32[10,16,1024]{2,1,0:T(8,128)S(1)} %copy-done.3) | data formatting | bytes 1310720 | tf_op args[3]
  46.8 7.1 %shard_map.56.rest_0_ = f32[1024,2048]{1,0:T(8,128)} custom-call(bf16[1024,2048]{1,0:T(8,128)(2,1)} %q_ref.11, bf16[1024,2048]{1,0:T(8,128)(2,1)} %k_ref.9, bf16[1024,2048]{1,0:T(8,128)(2,1)} %v_ref.9, f32[16,1024,10]{2,1,0:T(8,128)} %bitcast.26, f32[3,256,256]{2,1,0:T(8,128)} %constant.27.clone.c_ref), custom_call_target="tpu_custom_call" | custom-call | flops 1342177280 | bytes 5242880 | tf_op jit(solution)/shard_map/pallas_call | solution.py:122
  53.9 7.0 %shard_map.57.rest_0_ = f32[1024,2048]{1,0:T(8,128)} custom-call(bf16[1024,2048]{1,0:T(8,128)(2,1)} %q_ref.11, bf16[1024,2048]{1,0:T(8,128)(2,1)} %k_ref.9, bf16[1024,2048]{1,0:T(8,128)(2,1)} %v_ref.9, f32[16,1024,10]{2,1,0:T(8,128)} %bitcast.27, f32[3,256,256]{2,1,0:T(8,128)} %constant.27.clone.c_ref, ...), custom_call_target="tpu_custom_call", output_to_operand_aliasing={{}: (5, {})} | custom-call | flops 1342177280 | bytes 5242880 | tf_op jit(solution)/shard_map/pallas_call | solution.py:122
  60.9 0.0 collective-permute-start.6
  60.9 0.0 collective-permute-done.7
  60.9 1.8 %add.23 = f32[4,128,128]{2,1,0:T(8,128)} add(f32[4,128,128]{2,1,0:T(8,128)} %add.22, f32[4,128,128]{2,1,0:T(8,128)} %collective-permute-done.7) | non-fusion elementwise | flops 65536 | bytes 786432 | tf_op jit(solution)/shard_map/add | solution.py:259
  62.7 5.2 %collective-permute-start.11 = (f32[4,128,128]{2,1,0:T(8,128)}, f32[4,128,128]{2,1,0:T(8,128)}, u32[]{:S(2)}, u32[]{:S(2)}) collective-permute-start(f32[4,128,128]{2,1,0:T(8,128)} %add.23), channel_id=1, source_target_pairs={{0,16},{4,20},{8,24},{12,28},{1,17},{5,21},{9,25},{13,29},{2,18},{... | collective-permute-start | bytes 786440 | tf_op jit(solution)/shard_map/ppermute | solution.py:207
  67.9 0.5 collective-permute-start.8
  68.4 7.0 %shard_map.58.rest_0_ = f32[1024,2048]{1,0:T(8,128)} custom-call(bf16[1024,2048]{1,0:T(8,128)(2,1)} %q_ref.11, bf16[1024,2048]{1,0:T(8,128)(2,1)} %k_ref.9, bf16[1024,2048]{1,0:T(8,128)(2,1)} %v_ref.9, f32[16,1024,10]{2,1,0:T(8,128)} %bitcast.28, f32[3,256,256]{2,1,0:T(8,128)} %constant.27.clone.c_ref, ...), custom_call_target="tpu_custom_call", output_to_operand_aliasing={{}: (5, {})} | custom-call | flops 1342177280 | bytes 5242880 | tf_op jit(solution)/shard_map/pallas_call | solution.py:122
  75.4 7.0 %shard_map.59.l_ref = f32[1024,2048]{1,0:T(8,128)} custom-call(bf16[1024,2048]{1,0:T(8,128)(2,1)} %q_ref.11, bf16[1024,2048]{1,0:T(8,128)(2,1)} %k_ref.9, bf16[1024,2048]{1,0:T(8,128)(2,1)} %v_ref.9, f32[16,1024,10]{2,1,0:T(8,128)} %bitcast.29, f32[3,256,256]{2,1,0:T(8,128)} %constant.27.clone.c_ref, ...), custom_call_target="tpu_custom_call", output_to_operand_aliasing={{}: (5, {})} | custom-call | flops 1342177280 | bytes 5242880 | tf_op jit(solution)/shard_map/pallas_call | solution.py:122
  82.4 1.3 %fusion = bf16[1,16,128,128]{3,2,1,0:T(8,128)(2,1)S(1)} fusion(f32[1,8,128,128]{3,2,1,0:T(8,128)} %bitcast.32, f32[1,8,128,128]{3,2,1,0:T(8,128)} %bitcast.33, f32[]{:T(128)S(6)} %convert_element_type.62), kind=kLoop, calls=%fused_computation.2 | loop fusion | flops 786432 | bytes 1572868 | tf_op jit(solution)/shard_map/convert_element_type | solution.py:283
  83.7 0.6 collective-permute-start.10
  84.2 0.0 collective-permute-done.11
  84.2 0.1 collective-permute-start.14
  84.3 1.5 %collective-permute-start.12 = (f32[4,128,128]{2,1,0:T(8,128)}, f32[4,128,128]{2,1,0:T(8,128)}, u32[]{:S(2)}, u32[]{:S(2)}) collective-permute-start(f32[4,128,128]{2,1,0:T(8,128)} %collective-permute-done.11), channel_id=1, source_target_pairs={{0,2},{1,3},{2,0},{3,1},{4,6},{5,7},{6,4},{7,5},{8,10},{9,11},{10,... | collective-permute-start | bytes 786440 | tf_op jit(solution)/shard_map/ppermute | solution.py:212
  85.8 0.0 collective-permute-done.8
  85.8 0.1 collective-permute-start.9
  86.0 1.0 select_bitcast_fusion.6
  87.0 1.3 %select_bitcast_fusion.7 = (f32[1,4,128,128]{3,2,1,0:T(8,128)S(1)}, f32[1,4,128,128]{3,2,1,0:T(8,128)S(1)}, f32[1,4,128,128]{3,2,1,0:T(8,128)S(1)}) fusion(f32[4,128,128]{2,1,0:T(8,128)} %collective-permute-done.5, f32[4,128,128]{2,1,0:T(8,128)} %collective-permute-done.4, f32[4,128,128]{2,1,0:T(8,128)} %collective-permute-done.6, ...), kind=kLoop, calls=%fused_computation.26 | loop fusion | flops 786432 | bytes 1835020 | tf_op jit(solution)/shard_map/concatenate | solution.py:280
  88.3 0.1 fusion.1
  88.4 1.0 multiply_convert_fusion.2
  89.5 1.1 select_bitcast_fusion.3
  90.6 0.1 select_bitcast_fusion.2
  90.7 0.1 fusion.2
  90.9 0.7 maximum_bitcast_fusion.1.t_ref
  91.6 1.7 %pad_maximum_fusion.e_ref = bf16[4,16,128,128]{3,2,1,0:T(8,128)(2,1)} fusion(bf16[1,16,128,128]{3,2,1,0:T(8,128)(2,1)S(1)} %fusion.2, bf16[1,16,128,128]{3,2,1,0:T(8,128)(2,1)S(1)} %fusion.1, bf16[1,16,128,128]{3,2,1,0:T(8,128)(2,1)S(1)} %fusion, bf16[1,16,128,128]{3,2,1,0:T(8,128)(2,1)S(1)} %copy-done.2), kind=kLoop, calls=%fused_computation | loop fusion | flops 3145728 | bytes 4194304 | tf_op jit(solution)/shard_map/stack | solution.py:282
  93.3 1.3 %collective-permute-start.13 = (f32[4,128,128]{2,1,0:T(8,128)}, f32[4,128,128]{2,1,0:T(8,128)}, u32[]{:S(2)}, u32[]{:S(2)}) collective-permute-start(f32[4,128,128]{2,1,0:T(8,128)} %collective-permute-done.12), channel_id=1, source_target_pairs={{0,1},{1,0},{2,3},{3,2},{4,5},{5,4},{6,7},{7,6},{8,9},{9,8},{10,11... | collective-permute-start | bytes 786440 | tf_op jit(solution)/shard_map/ppermute | solution.py:212
  94.6 10.1 %shard_map.60.l_ref = f32[1024,2048]{1,0:T(8,128)} custom-call(s32[1]{0:T(128)} %bitcast.sp_ref, bf16[1024,2048]{1,0:T(8,128)(2,1)} %q_ref.11, bf16[4,16,128,128]{3,2,1,0:T(8,128)(2,1)} %pad_maximum_fusion.e_ref, bf16[1,8,128,128]{3,2,1,0:T(8,128)(2,1)} %maximum_bitcast_fusion.1.t_ref, f32[16,1024,10]{2,1,0:T(8,128)} %bitcast.30, ...), custom_call_target="tpu_custom_call", output_to_operand_aliasing={{}: (5, {})} | custom-call | flops 1342177280 | bytes 10485760 | tf_op jit(solution)/shard_map/pallas_call | solution.py:173
  104.7 1.0 multiply_convert_fusion.4
  105.7 1.0 multiply_convert_fusion.3
  106.6 0.7 maximum_bitcast_fusion.t_ref
  107.4 10.1 %shard_map.61 = f32[1024,2048]{1,0:T(8,128)} custom-call(s32[1]{0:T(128)} %bitcast.sp_ref, bf16[1024,2048]{1,0:T(8,128)(2,1)} %q_ref.11, bf16[4,16,128,128]{3,2,1,0:T(8,128)(2,1)} %pad_maximum_fusion.e_ref, bf16[1,8,128,128]{3,2,1,0:T(8,128)(2,1)} %maximum_bitcast_fusion.t_ref, f32[16,1024,10]{2,1,0:T(8,128)} %bitcast.31, ...), custom_call_target="tpu_custom_call", output_to_operand_aliasing={{}: (5, {})} | custom-call | flops 1342177280 | bytes 10485760 | tf_op jit(solution)/shard_map/pallas_call | solution.py:173
  (18 shorter events, 0.1 us)
Async XLA Ops:
  5.3 3.0 %collective-permute-start = (f32[16,128,128]{2,1,0:T(8,128)}, f32[16,128,128]{2,1,0:T(8,128)S(1)}, u32[]{:S(2)}, u32[]{:S(2)}) collective-permute-start(f32[16,128,128]{2,1,0:T(8,128)} %shard_map.55), channel_id=1, source_target_pairs={{0,1},{1,0},{2,3},{3,2},{4,5},{5,4},{6,7},{7,6},{8,9},{9,8},{10,11... | collective-permute-start | bytes 3145736 | tf_op jit(solution)/shard_map/ppermute | solution.py:207
  5.7 36.3 %copy-start.3 = (f32[10,16,1024]{2,1,0:T(8,128)S(1)}, f32[10,16,1024]{2,1,0:T(8,128)}, u32[]{:S(2)}) copy-start(f32[10,16,1024]{2,1,0:T(8,128)} %param.8) | copy-start | bytes 1966084
  10.5 15.1 %collective-permute-start.1 = (f32[8,128,128]{2,1,0:T(8,128)S(1)}, f32[8,128,128]{2,1,0:T(8,128)S(1)}, u32[]{:S(2)}, u32[]{:S(2)}) collective-permute-start(f32[8,128,128]{2,1,0:T(8,128)S(1)} %constant_dynamic-slice_fusion), channel_id=1, source_target_pairs={{0,2},{2,0},{1,3},{3,1},{4,6},{6,4},{5,7},{7,5},{8,10},{10,8},{9,1... | collective-permute-start | bytes 1572872 | tf_op jit(solution)/shard_map/ppermute | solution.py:207
  25.7 1.9 %collective-permute-start.2 = (f32[8,128,128]{2,1,0:T(8,128)S(1)}, f32[8,128,128]{2,1,0:T(8,128)S(1)}, u32[]{:S(2)}, u32[]{:S(2)}) collective-permute-start(f32[8,128,128]{2,1,0:T(8,128)S(1)} %collective-permute-done.1), channel_id=1, source_target_pairs={{0,1},{1,0},{2,3},{3,2},{4,5},{5,4},{6,7},{7,6},{8,9},{9,8},{10,11... | collective-permute-start | bytes 1572872 | tf_op jit(solution)/shard_map/ppermute | solution.py:207
  27.7 0.8 copy-start
  27.7 1.0 copy-start.1
  28.6 8.5 %collective-permute-start.3 = (f32[4,128,128]{2,1,0:T(8,128)S(1)}, f32[4,128,128]{2,1,0:T(8,128)}, u32[]{:S(2)}, u32[]{:S(2)}) collective-permute-start(f32[4,128,128]{2,1,0:T(8,128)S(1)} %fusion.5), channel_id=1, source_target_pairs={{0,4},{4,0},{8,12},{12,8},{16,20},{20,16},{24,28},{28,24},{1,5},{5... | collective-permute-start | bytes 786440 | tf_op jit(solution)/shard_map/ppermute | solution.py:207
  38.8 22.1 %collective-permute-start.7 = (f32[4,128,128]{2,1,0:T(8,128)}, f32[4,128,128]{2,1,0:T(8,128)}, u32[]{:S(2)}, u32[]{:S(2)}) collective-permute-start(f32[4,128,128]{2,1,0:T(8,128)} %add.22), channel_id=1, source_target_pairs={{0,8},{8,0},{4,12},{12,4},{16,24},{24,16},{20,28},{28,20},{1,9},{9... | collective-permute-start | bytes 786440 | tf_op jit(solution)/shard_map/ppermute | solution.py:207
  40.6 27.8 %collective-permute-start.4 = (f32[4,128,128]{2,1,0:T(8,128)}, f32[4,128,128]{2,1,0:T(8,128)}, u32[]{:S(2)}, u32[]{:S(2)}) collective-permute-start(f32[4,128,128]{2,1,0:T(8,128)} %collective-permute-done.3), channel_id=1, source_target_pairs={{0,2},{1,3},{2,0},{3,1},{4,6},{5,7},{6,4},{7,5},{8,10},{9,11},{10,... | collective-permute-start | bytes 786440 | tf_op jit(solution)/shard_map/ppermute | solution.py:212
  60.9 23.4 %collective-permute-start.6 = (f32[4,128,128]{2,1,0:T(8,128)}, f32[4,128,128]{2,1,0:T(8,128)}, u32[]{:S(2)}, u32[]{:S(2)}) collective-permute-start(f32[4,128,128]{2,1,0:T(8,128)} %collective-permute-done.3), channel_id=1, source_target_pairs={{0,1},{1,0},{2,3},{3,2},{4,5},{5,4},{6,7},{7,6},{8,9},{9,8},{10,11... | collective-permute-start | bytes 786440 | tf_op jit(solution)/shard_map/ppermute | solution.py:212
  62.7 21.6 %collective-permute-start.11 = (f32[4,128,128]{2,1,0:T(8,128)}, f32[4,128,128]{2,1,0:T(8,128)}, u32[]{:S(2)}, u32[]{:S(2)}) collective-permute-start(f32[4,128,128]{2,1,0:T(8,128)} %add.23), channel_id=1, source_target_pairs={{0,16},{4,20},{8,24},{12,28},{1,17},{5,21},{9,25},{13,29},{2,18},{... | collective-permute-start | bytes 786440 | tf_op jit(solution)/shard_map/ppermute | solution.py:207
  67.9 18.0 %collective-permute-start.8 = (f32[4,128,128]{2,1,0:T(8,128)}, f32[4,128,128]{2,1,0:T(8,128)}, u32[]{:S(2)}, u32[]{:S(2)}) collective-permute-start(f32[4,128,128]{2,1,0:T(8,128)} %collective-permute-done.7), channel_id=1, source_target_pairs={{0,2},{1,3},{2,0},{3,1},{4,6},{5,7},{6,4},{7,5},{8,10},{9,11},{10,... | collective-permute-start | bytes 786440 | tf_op jit(solution)/shard_map/ppermute | solution.py:212
  68.4 17.6 %collective-permute-start.5 = (f32[4,128,128]{2,1,0:T(8,128)}, f32[4,128,128]{2,1,0:T(8,128)}, u32[]{:S(2)}, u32[]{:S(2)}) collective-permute-start(f32[4,128,128]{2,1,0:T(8,128)} %collective-permute-done.4), channel_id=1, source_target_pairs={{0,1},{1,0},{2,3},{3,2},{4,5},{5,4},{6,7},{7,6},{8,9},{9,8},{10,11... | collective-permute-start | bytes 786440 | tf_op jit(solution)/shard_map/ppermute | solution.py:212
  83.7 5.8 %collective-permute-start.10 = (f32[4,128,128]{2,1,0:T(8,128)}, f32[4,128,128]{2,1,0:T(8,128)S(1)}, u32[]{:S(2)}, u32[]{:S(2)}) collective-permute-start(f32[4,128,128]{2,1,0:T(8,128)} %collective-permute-done.7), channel_id=1, source_target_pairs={{0,1},{1,0},{2,3},{3,2},{4,5},{5,4},{6,7},{7,6},{8,9},{9,8},{10,11... | collective-permute-start | bytes 786440 | tf_op jit(solution)/shard_map/ppermute | solution.py:212
  84.2 6.6 %collective-permute-start.14 = (f32[4,128,128]{2,1,0:T(8,128)}, f32[4,128,128]{2,1,0:T(8,128)S(1)}, u32[]{:S(2)}, u32[]{:S(2)}) collective-permute-start(f32[4,128,128]{2,1,0:T(8,128)} %collective-permute-done.11), channel_id=1, source_target_pairs={{0,1},{1,0},{2,3},{3,2},{4,5},{5,4},{6,7},{7,6},{8,9},{9,8},{10,11... | collective-permute-start | bytes 786440 | tf_op jit(solution)/shard_map/ppermute | solution.py:212
  84.3 9.0 %collective-permute-start.12 = (f32[4,128,128]{2,1,0:T(8,128)}, f32[4,128,128]{2,1,0:T(8,128)}, u32[]{:S(2)}, u32[]{:S(2)}) collective-permute-start(f32[4,128,128]{2,1,0:T(8,128)} %collective-permute-done.11), channel_id=1, source_target_pairs={{0,2},{1,3},{2,0},{3,1},{4,6},{5,7},{6,4},{7,5},{8,10},{9,11},{10,... | collective-permute-start | bytes 786440 | tf_op jit(solution)/shard_map/ppermute | solution.py:212
  85.8 3.6 %collective-permute-start.9 = (f32[4,128,128]{2,1,0:T(8,128)}, f32[4,128,128]{2,1,0:T(8,128)S(1)}, u32[]{:S(2)}, u32[]{:S(2)}) collective-permute-start(f32[4,128,128]{2,1,0:T(8,128)} %collective-permute-done.8), channel_id=1, source_target_pairs={{0,1},{1,0},{2,3},{3,2},{4,5},{5,4},{6,7},{7,6},{8,9},{9,8},{10,11... | collective-permute-start | bytes 786440 | tf_op jit(solution)/shard_map/ppermute | solution.py:212
  88.3 3.3 %copy-start.2 = (bf16[1,16,128,128]{3,2,1,0:T(8,128)(2,1)S(1)}, bf16[1,16,128,128]{3,2,1,0:T(8,128)(2,1)}, u32[]{:S(2)}) copy-start(bf16[1,16,128,128]{3,2,1,0:T(8,128)(2,1)} %get-tuple-element.5) | copy-start | bytes 1572868
  93.3 12.4 %collective-permute-start.13 = (f32[4,128,128]{2,1,0:T(8,128)}, f32[4,128,128]{2,1,0:T(8,128)}, u32[]{:S(2)}, u32[]{:S(2)}) collective-permute-start(f32[4,128,128]{2,1,0:T(8,128)} %collective-permute-done.12), channel_id=1, source_target_pairs={{0,1},{1,0},{2,3},{3,2},{4,5},{5,4},{6,7},{7,6},{8,9},{9,8},{10,11... | collective-permute-start | bytes 786440 | tf_op jit(solution)/shard_map/ppermute | solution.py:212

commit v7 on v5

--- a/solution.py
+++ b/solution.py
@@ -66,7 +66,7 @@
     )(keys, values)
 
 
-def local_kernel(scale, rows, group, q_ref, k_ref, v_ref, m_ref, c_ref, *rest):
+def local_kernel(scale, rows, group, levels, q_ref, k_ref, v_ref, m_ref, c_ref, *rest):
     o_ref = rest[-1]
     blocks = rows // TQ
     inner = c_ref.shape[0]
@@ -82,7 +82,7 @@
                 (((1,), (1,)), ((), ())), preferred_element_type=jnp.float32,
             )
             s = s * scale
-            mix = m_ref[j, r0:r0 + TQ, :]
+            mix = m_ref[r0:r0 + TQ, j * levels:(j + 1) * levels]
             pieces = []
             for b in range(a):
                 level = inner + (a ^ b).bit_length() - 1
@@ -98,12 +98,10 @@
             )
 
 
-def local_part(queries, keys, values, mix_t, masks, first, count, group, scale, prev):
+def local_part(queries, keys, values, mix_t, masks, first, count, group, scale, prev, head_count, levels):
     rows = queries.shape[0]
-    head_count = mix_t.shape[0]
     dk = queries.shape[1] // head_count
     dv = values.shape[1] // head_count
-    levels = mix_t.shape[2]
     blocks = rows // TQ
     tiles = blocks * (blocks + 1) // 2
     base = first // group
@@ -111,7 +109,7 @@
         pl.BlockSpec((rows, dk * group), lambda h: (0, h + base)),
         pl.BlockSpec((rows, dk * group), lambda h: (0, h + base)),
         pl.BlockSpec((rows, dv * group), lambda h: (0, h + base)),
-        pl.BlockSpec((group, rows, levels), lambda h: (h + base, 0, 0)),
+        pl.BlockSpec((rows, 128), lambda h: (0, h + base)),
         pl.BlockSpec(masks.shape, lambda h: (0, 0, 0)),
     ]
     operands = [queries, keys, values, mix_t, masks]
@@ -121,7 +119,7 @@
         operands.append(prev)
         aliases = {5: 0}
     return pl.pallas_call(
-        functools.partial(local_kernel, scale, rows, group),
+        functools.partial(local_kernel, scale, rows, group, levels),
         grid=(count // group,),
         in_specs=in_specs,
         out_specs=pl.BlockSpec((rows, dv * group), lambda h: (0, h + base)),
@@ -136,7 +134,7 @@
     )(*operands)
 
 
-def cross_kernel(scale, rows, first_level, group, q_ref, s_ref, m_ref, l_ref, o_ref):
+def cross_kernel(scale, rows, first_level, group, levels, q_ref, s_ref, m_ref, l_ref, o_ref):
     bits = s_ref.shape[0]
     dk = s_ref.shape[2]
     dv = s_ref.shape[3]
@@ -148,7 +146,8 @@
                 q_ref[r0:r0 + TQ, j * dk:(j + 1) * dk], sib,
                 preferred_element_type=jnp.float32,
             )
-            w_all = m_ref[j, r0:r0 + TQ, first_level:first_level + bits] * scale
+            c0 = (j // 2) * 128 + (j % 2) * levels + first_level
+            w_all = m_ref[r0:r0 + TQ, c0:c0 + bits] * scale
             cross = w_all[:, 0:1] * t[:, 0:dv]
             for b in range(1, bits):
                 cross = cross + w_all[:, b:b + 1] * t[:, b * dv:(b + 1) * dv]
@@ -157,20 +156,18 @@
             )
 
 
-def cross_all(queries, sibs, mix_t, local, scale, first_level, group):
+def cross_all(queries, sibs, mix_t, local, scale, first_level, group, head_count, levels):
     rows = queries.shape[0]
-    head_count = mix_t.shape[0]
     dk = queries.shape[1] // head_count
     dv = sibs.shape[3]
-    levels = mix_t.shape[2]
     bits = sibs.shape[0]
     return pl.pallas_call(
-        functools.partial(cross_kernel, scale, rows, first_level, group),
+        functools.partial(cross_kernel, scale, rows, first_level, group, levels),
         grid=(head_count // group,),
         in_specs=[
             pl.BlockSpec((rows, dk * group), lambda g: (0, g)),
             pl.BlockSpec((bits, group, dk, dv), lambda g: (0, g, 0, 0)),
-            pl.BlockSpec((group, rows, levels), lambda g: (g, 0, 0)),
+            pl.BlockSpec((rows, 128 * group // 2), lambda g: (0, g)),
             pl.BlockSpec((rows, dv * group), lambda g: (0, g)),
         ],
         out_specs=pl.BlockSpec((rows, dv * group), lambda g: (0, g)),
@@ -208,7 +205,10 @@
     dk = queries.shape[1] // head_count
     scale = dk ** (-0.5)
     level_count = (rows // SPAN).bit_length()
-    mix_t = mixing.transpose(1, 2, 0)
+    levels = mixing.shape[0]
+    paired = mixing.reshape(levels, head_count // 2, 2, rows).transpose(3, 1, 2, 0)
+    paired = paired.reshape(rows, head_count // 2, 2 * levels)
+    mix_t = jnp.pad(paired, ((0, 0), (0, 0), (0, 128 - 2 * levels))).reshape(rows, -1)
     masks = jnp.asarray(level_masks(TQ, level_count))
 
     state = own_state(keys, values, head_count)
@@ -273,9 +273,12 @@
     local = None
     for c in range(CHUNKS):
         local = local_part(
-            queries, keys, values, mix_t, masks, c * per, per, LOCAL_GROUP, scale, local
+            queries, keys, values, mix_t, masks, c * per, per, LOCAL_GROUP, scale, local,
+            head_count, levels,
         )
-    return cross_all(queries, rounded, mix_t, local, scale, level_count, CROSS_GROUP)
+    return cross_all(
+        queries, rounded, mix_t, local, scale, level_count, CROSS_GROUP, head_count, levels
+    )
 
 
 def solution(mesh):

time: 116 us -> 119 us (1.026)
  local copies, waits for them, and re-layouts: 5.6 us -> 9.71 us
    pad x0 -> x1, local copies, waits for them, and re-layouts: none -> 2.46 us  [shards(): jnp.pad(paired, ((0, 0), (0, 0), (0, 128 - 2 * levels))).reshape(rows, -1)]
    unnamed x13 -> x14, local copies, waits for them, and re-layouts: 5.55 us -> 6.61 us
  transfers between devices with their start and end apart: 15 -> 15, of which waited for: 5 -> 5; matrix products, arithmetic and copies ran while one was open for 13% -> 16% of each run, Pallas kernels for 24% -> 23%
where the time goes in v7:
time: 119 us; the launch traced here: 118 us
  Pallas kernels  48.9 us (41%)
  waiting for transfers between devices  31.3 us (26%)
  other arithmetic  16.8 us (14%)
  starting transfers between devices  11.6 us (10%)
  local copies, waits for them, and re-layouts  9.71 us (8%)
    pallas_call x4, Pallas kernels, local_part(): pl.pallas_call(functools.partial(local_kernel, scale, rows, group, levels...  27.6 us
    ppermute x6, waiting for transfers between devices, swap(): return lax.ppermute(block, axis, route)  27 us
    pallas_call x1, Pallas kernels, cross_all(): pl.pallas_call(functools.partial(cross_kernel, scale, rows, first_level,...  16 us
    unnamed x14, local copies, waits for them, and re-layouts  6.61 us
    ppermute x6, starting transfers between devices, swap(): return lax.ppermute(block, axis, route)  5.88 us
    ppermute x9, starting transfers between devices, to_offset(): return lax.ppermute(block, axis, [(s, s ^ offset) for s in range(count)])  5.67 us
    pallas_call x1, Pallas kernels, own_state(): pl.pallas_call(functools.partial(state_kernel, head_count), grid=(rows //...  5.25 us
    unnamed x4, other arithmetic  4.95 us
  transfers between devices with their start and end apart: 15, of which 5 were waited for; matrix products, arithmetic and copies ran while one was open for 16% of the time, Pallas kernels for 23%

profile of v7, /device:TPU:25, one launch (start us, length us, event | category | flops | bytes accessed | tf_op | source)
XLA Modules:
  0.0 118.3 jit_solution(7231505215665178767)
XLA Ops:
  0.0 5.2 %shard_map.55 = f32[16,128,128]{2,1,0:T(8,128)} custom-call(bf16[1024,2048]{1,0:T(8,128)(2,1)} %k_ref.9, bf16[1024,2048]{1,0:T(8,128)(2,1)} %v_ref.9), custom_call_target="tpu_custom_call" | custom-call | flops 536870912 | bytes 9437184 | tf_op jit(solution)/shard_map/pallas_call | solution.py:51
  5.3 0.7 collective-permute-start
  5.9 2.5 %collective-permute-done = f32[16,128,128]{2,1,0:T(8,128)S(1)} collective-permute-done((f32[16,128,128]{2,1,0:T(8,128)}, f32[16,128,128]{2,1,0:T(8,128)S(1)}, u32[]{:S(2)}, u32[]{:S(2)}) %collective-permute-start) | collective-permute-done | bytes 1048608 | tf_op jit(solution)/shard_map/ppermute | solution.py:194
  8.4 1.7 %add.20 = f32[16,128,128]{2,1,0:T(8,128)S(1)} add(f32[16,128,128]{2,1,0:T(8,128)} %shard_map.55, f32[16,128,128]{2,1,0:T(8,128)S(1)} %collective-permute-done) | non-fusion elementwise | flops 262144 | bytes 3145728 | tf_op jit(solution)/shard_map/add | solution.py:240
  10.2 1.3 %collective-permute-start.1 = (f32[8,128,128]{2,1,0:T(8,128)S(1)}, f32[8,128,128]{2,1,0:T(8,128)S(1)}, u32[]{:S(2)}, u32[]{:S(2)}) collective-permute-start(f32[8,128,128]{2,1,0:T(8,128)S(1)} %constant_dynamic-slice_fusion), channel_id=1, source_target_pairs={{0,2},{2,0},{1,3},{3,1},{4,6},{6,4},{5,7},{7,5},{8,10},{10,8},{9,1... | collective-permute-start | bytes 1572872 | tf_op jit(solution)/shard_map/ppermute | solution.py:194
  11.5 11.9 %collective-permute-done.1 = f32[8,128,128]{2,1,0:T(8,128)S(1)} collective-permute-done((f32[8,128,128]{2,1,0:T(8,128)S(1)}, f32[8,128,128]{2,1,0:T(8,128)S(1)}, u32[]{:S(2)}, u32[]{:S(2)}) %collective-permute-start.1) | collective-permute-done | bytes 524320 | tf_op jit(solution)/shard_map/ppermute | solution.py:194
  23.4 1.2 %collective-permute-start.2 = (f32[8,128,128]{2,1,0:T(8,128)S(1)}, f32[8,128,128]{2,1,0:T(8,128)}, u32[]{:S(2)}, u32[]{:S(2)}) collective-permute-start(f32[8,128,128]{2,1,0:T(8,128)S(1)} %collective-permute-done.1), channel_id=1, source_target_pairs={{0,1},{1,0},{2,3},{3,2},{4,5},{5,4},{6,7},{7,6},{8,9},{9,8},{10,11... | collective-permute-start | bytes 1572872 | tf_op jit(solution)/shard_map/ppermute | solution.py:194
  24.6 1.7 %collective-permute-done.2 = f32[8,128,128]{2,1,0:T(8,128)} collective-permute-done((f32[8,128,128]{2,1,0:T(8,128)S(1)}, f32[8,128,128]{2,1,0:T(8,128)}, u32[]{:S(2)}, u32[]{:S(2)}) %collective-permute-start.2) | collective-permute-done | bytes 524320 | tf_op jit(solution)/shard_map/ppermute | solution.py:194
  26.3 1.1 broadcast_select_fusion.1
  27.5 0.8 copy-done
  28.3 0.8 fusion.11
  29.1 1.2 %collective-permute-start.3 = (f32[4,128,128]{2,1,0:T(8,128)}, f32[4,128,128]{2,1,0:T(8,128)}, u32[]{:S(2)}, u32[]{:S(2)}) collective-permute-start(f32[4,128,128]{2,1,0:T(8,128)} %fusion.11), channel_id=1, source_target_pairs={{0,4},{4,0},{8,12},{12,8},{16,20},{20,16},{24,28},{28,24},{1,5},{5... | collective-permute-start | bytes 786440 | tf_op jit(solution)/shard_map/ppermute | solution.py:194
  30.3 0.4 reshape.215
  30.7 0.2 copy.12
  30.9 2.8 %copy.14 = f32[1024,8,20]{2,1,0:T(8,128)} copy(f32[1024,8,20]{0,1,2:T(8,128)S(1)} %bitcast.44) | data formatting | bytes 1310720
  33.7 2.5 %pad.4.clone = f32[1024,8,128]{2,1,0:T(8,128)S(1)} pad(f32[1024,8,20]{2,1,0:T(8,128)} %copy.14, f32[]{:T(128)} %constant.27.clone.1), padding=0_0x0_0x0_108 | pad | bytes 4849668 | tf_op jit(solution)/shard_map/jit(_pad)/pad | solution.py:211
  36.2 3.0 %copy.17 = f32[128,8,8,128]{3,1,2,0:T(8,128)} copy(f32[128,8,8,128]{3,2,1,0:T(8,128)S(1)} %bitcast.41) | data formatting | bytes 8388608
  39.1 7.0 %shard_map.56.rest_0_ = f32[1024,2048]{1,0:T(8,128)} custom-call(bf16[1024,2048]{1,0:T(8,128)(2,1)} %q_ref.9, bf16[1024,2048]{1,0:T(8,128)(2,1)} %k_ref.9, bf16[1024,2048]{1,0:T(8,128)(2,1)} %v_ref.9, f32[1024,1024]{1,0:T(8,128)} %bitcast.36, f32[3,256,256]{2,1,0:T(8,128)} %constant.28.clone.c_ref), custom_call_target="tpu_custom_call" | custom-call | flops 1342177280 | bytes 5242880 | tf_op jit(solution)/shard_map/pallas_call | solution.py:121
  46.1 1.8 %add.24 = f32[4,128,128]{2,1,0:T(8,128)} add(f32[4,128,128]{2,1,0:T(8,128)} %fusion.11, f32[4,128,128]{2,1,0:T(8,128)} %collective-permute-done.3) | non-fusion elementwise | flops 65536 | bytes 786432 | tf_op jit(solution)/shard_map/add | solution.py:249
  47.9 0.2 collective-permute-start.7
  48.1 1.2 %collective-permute-start.4 = (f32[4,128,128]{2,1,0:T(8,128)}, f32[4,128,128]{2,1,0:T(8,128)}, u32[]{:S(2)}, u32[]{:S(2)}) collective-permute-start(f32[4,128,128]{2,1,0:T(8,128)} %collective-permute-done.3), channel_id=1, source_target_pairs={{0,2},{1,3},{2,0},{3,1},{4,6},{5,7},{6,4},{7,5},{8,10},{9,11},{10,... | collective-permute-start | bytes 786440 | tf_op jit(solution)/shard_map/ppermute | solution.py:199
  49.3 6.8 %shard_map.57.rest_0_ = f32[1024,2048]{1,0:T(8,128)} custom-call(bf16[1024,2048]{1,0:T(8,128)(2,1)} %q_ref.9, bf16[1024,2048]{1,0:T(8,128)(2,1)} %k_ref.9, bf16[1024,2048]{1,0:T(8,128)(2,1)} %v_ref.9, f32[1024,1024]{1,0:T(8,128)} %bitcast.37, f32[3,256,256]{2,1,0:T(8,128)} %constant.28.clone.c_ref, ...), custom_call_target="tpu_custom_call", output_to_operand_aliasing={{}: (5, {})} | custom-call | flops 1342177280 | bytes 5242880 | tf_op jit(solution)/shard_map/pallas_call | solution.py:121
  56.1 6.8 %shard_map.58.rest_0_ = f32[1024,2048]{1,0:T(8,128)} custom-call(bf16[1024,2048]{1,0:T(8,128)(2,1)} %q_ref.9, bf16[1024,2048]{1,0:T(8,128)(2,1)} %k_ref.9, bf16[1024,2048]{1,0:T(8,128)(2,1)} %v_ref.9, f32[1024,1024]{1,0:T(8,128)} %bitcast.38, f32[3,256,256]{2,1,0:T(8,128)} %constant.28.clone.c_ref, ...), custom_call_target="tpu_custom_call", output_to_operand_aliasing={{}: (5, {})} | custom-call | flops 1342177280 | bytes 5242880 | tf_op jit(solution)/shard_map/pallas_call | solution.py:121
  62.9 7.0 %shard_map.59.l_ref = f32[1024,2048]{1,0:T(8,128)} custom-call(bf16[1024,2048]{1,0:T(8,128)(2,1)} %q_ref.9, bf16[1024,2048]{1,0:T(8,128)(2,1)} %k_ref.9, bf16[1024,2048]{1,0:T(8,128)(2,1)} %v_ref.9, f32[1024,1024]{1,0:T(8,128)} %bitcast.39, f32[3,256,256]{2,1,0:T(8,128)} %constant.28.clone.c_ref, ...), custom_call_target="tpu_custom_call", output_to_operand_aliasing={{}: (5, {})} | custom-call | flops 1342177280 | bytes 5242880 | tf_op jit(solution)/shard_map/pallas_call | solution.py:121
  69.9 1.3 %collective-permute-start.6 = (f32[4,128,128]{2,1,0:T(8,128)}, f32[4,128,128]{2,1,0:T(8,128)S(1)}, u32[]{:S(2)}, u32[]{:S(2)}) collective-permute-start(f32[4,128,128]{2,1,0:T(8,128)} %collective-permute-done.3), channel_id=1, source_target_pairs={{0,1},{1,0},{2,3},{3,2},{4,5},{5,4},{6,7},{7,6},{8,9},{9,8},{10,11... | collective-permute-start | bytes 786440 | tf_op jit(solution)/shard_map/ppermute | solution.py:199
  71.2 1.1 add.25
  72.2 1.3 %collective-permute-start.11 = (f32[4,128,128]{2,1,0:T(8,128)S(1)}, f32[4,128,128]{2,1,0:T(8,128)S(1)}, u32[]{:S(2)}, u32[]{:S(2)}) collective-permute-start(f32[4,128,128]{2,1,0:T(8,128)S(1)} %add.25), channel_id=1, source_target_pairs={{0,16},{4,20},{8,24},{12,28},{1,17},{5,21},{9,25},{13,29},{2,18},{... | collective-permute-start | bytes 786440 | tf_op jit(solution)/shard_map/ppermute | solution.py:194
  73.5 0.3 collective-permute-start.8
  73.9 0.4 collective-permute-start.5
  74.2 2.1 %fusion.5 = bf16[5,16,128,128]{3,2,1,0:T(8,128)(2,1)} fusion(f32[16,128,128]{2,1,0:T(8,128)} %copy-done.4, f32[]{:T(128)S(6)} %convert_element_type.60), kind=kLoop, calls=%fused_computation.13 | loop fusion | flops 524287 | bytes 1572868
  76.4 0.9 fusion.9
  77.3 0.1 collective-permute-start.10
  77.5 11.0 %collective-permute-done.11 = f32[4,128,128]{2,1,0:T(8,128)S(1)} collective-permute-done((f32[4,128,128]{2,1,0:T(8,128)S(1)}, f32[4,128,128]{2,1,0:T(8,128)S(1)}, u32[]{:S(2)}, u32[]{:S(2)}) %collective-permute-start.11) | collective-permute-done | bytes 262176 | tf_op jit(solution)/shard_map/ppermute | solution.py:194
  88.4 0.9 collective-permute-start.14
  89.4 0.3 collective-permute-start.12
  89.6 0.3 collective-permute-start.9
  89.9 1.1 select_bitcast_fusion.11
  91.1 1.0 select_bitcast_fusion.10
  92.1 0.9 fusion.8
  93.0 4.2 %collective-permute-done.12 = f32[4,128,128]{2,1,0:T(8,128)S(1)} collective-permute-done((f32[4,128,128]{2,1,0:T(8,128)S(1)}, f32[4,128,128]{2,1,0:T(8,128)S(1)}, u32[]{:S(2)}, u32[]{:S(2)}) %collective-permute-start.12) | collective-permute-done | bytes 262176 | tf_op jit(solution)/shard_map/ppermute | solution.py:199
  97.2 0.9 collective-permute-start.13
  98.1 1.1 select_bitcast_fusion.7
  99.2 1.0 select_bitcast_fusion.6
  100.2 0.9 fusion.7
  101.2 0.1 select_bitcast_fusion.2
  101.2 0.1 select_bitcast_fusion.3
  101.4 0.9 fusion.6.s_ref
  102.3 16.0 %shard_map.60 = f32[1024,2048]{1,0:T(8,128)} custom-call(bf16[1024,2048]{1,0:T(8,128)(2,1)} %q_ref.9, bf16[5,16,128,128]{3,2,1,0:T(8,128)(2,1)} %fusion.6.s_ref, f32[1024,1024]{1,0:T(8,128)} %bitcast.40, f32[1024,2048]{1,0:T(8,128)} %shard_map.59.l_ref), custom_call_target="tpu_custom_call", output_to_operand_aliasing={{}: (3, {})} | custom-call | flops 2684354560 | bytes 20971520 | tf_op jit(solution)/shard_map/pallas_call | solution.py:164
  (22 shorter events, 0.1 us)
Async XLA Ops:
  5.3 3.2 %collective-permute-start = (f32[16,128,128]{2,1,0:T(8,128)}, f32[16,128,128]{2,1,0:T(8,128)S(1)}, u32[]{:S(2)}, u32[]{:S(2)}) collective-permute-start(f32[16,128,128]{2,1,0:T(8,128)} %shard_map.55), channel_id=1, source_target_pairs={{0,1},{1,0},{2,3},{3,2},{4,5},{5,4},{6,7},{7,6},{8,9},{9,8},{10,11... | collective-permute-start | bytes 3145736 | tf_op jit(solution)/shard_map/ppermute | solution.py:194
  8.4 19.0 %copy-start.4 = (f32[16,128,128]{2,1,0:T(8,128)}, f32[16,128,128]{2,1,0:T(8,128)S(1)}, u32[]{:S(2)}) copy-start(f32[16,128,128]{2,1,0:T(8,128)S(1)} %collective-permute-done) | copy-start | bytes 3145732
  10.1 20.2 %copy-start.5 = (f32[10,16,1024]{2,1,0:T(8,128)S(1)}, f32[10,16,1024]{2,1,0:T(8,128)}, u32[]{:S(2)}) copy-start(f32[10,16,1024]{2,1,0:T(8,128)} %param.8) | copy-start | bytes 1966084
  10.2 13.2 %collective-permute-start.1 = (f32[8,128,128]{2,1,0:T(8,128)S(1)}, f32[8,128,128]{2,1,0:T(8,128)S(1)}, u32[]{:S(2)}, u32[]{:S(2)}) collective-permute-start(f32[8,128,128]{2,1,0:T(8,128)S(1)} %constant_dynamic-slice_fusion), channel_id=1, source_target_pairs={{0,2},{2,0},{1,3},{3,1},{4,6},{6,4},{5,7},{7,5},{8,10},{10,8},{9,1... | collective-permute-start | bytes 1572872 | tf_op jit(solution)/shard_map/ppermute | solution.py:194
  23.4 2.9 %collective-permute-start.2 = (f32[8,128,128]{2,1,0:T(8,128)S(1)}, f32[8,128,128]{2,1,0:T(8,128)}, u32[]{:S(2)}, u32[]{:S(2)}) collective-permute-start(f32[8,128,128]{2,1,0:T(8,128)S(1)} %collective-permute-done.1), channel_id=1, source_target_pairs={{0,1},{1,0},{2,3},{3,2},{4,5},{5,4},{6,7},{7,6},{8,9},{9,8},{10,11... | collective-permute-start | bytes 1572872 | tf_op jit(solution)/shard_map/ppermute | solution.py:194
  27.4 0.9 copy-start
  27.4 1.6 %copy-start.2 = (f32[8,128,128]{2,1,0:T(8,128)}, f32[8,128,128]{2,1,0:T(8,128)S(1)}, u32[]{:S(2)}) copy-start(f32[8,128,128]{2,1,0:T(8,128)S(1)} %get-tuple-element.15) | copy-start | bytes 1572868
  29.1 17.0 %collective-permute-start.3 = (f32[4,128,128]{2,1,0:T(8,128)}, f32[4,128,128]{2,1,0:T(8,128)}, u32[]{:S(2)}, u32[]{:S(2)}) collective-permute-start(f32[4,128,128]{2,1,0:T(8,128)} %fusion.11), channel_id=1, source_target_pairs={{0,4},{4,0},{8,12},{12,8},{16,20},{20,16},{24,28},{28,24},{1,5},{5... | collective-permute-start | bytes 786440 | tf_op jit(solution)/shard_map/ppermute | solution.py:194
  47.9 23.3 %collective-permute-start.7 = (f32[4,128,128]{2,1,0:T(8,128)}, f32[4,128,128]{2,1,0:T(8,128)}, u32[]{:S(2)}, u32[]{:S(2)}) collective-permute-start(f32[4,128,128]{2,1,0:T(8,128)} %add.24), channel_id=1, source_target_pairs={{0,8},{8,0},{4,12},{12,4},{16,24},{24,16},{20,28},{28,20},{1,9},{9... | collective-permute-start | bytes 786440 | tf_op jit(solution)/shard_map/ppermute | solution.py:194
  48.1 25.8 %collective-permute-start.4 = (f32[4,128,128]{2,1,0:T(8,128)}, f32[4,128,128]{2,1,0:T(8,128)}, u32[]{:S(2)}, u32[]{:S(2)}) collective-permute-start(f32[4,128,128]{2,1,0:T(8,128)} %collective-permute-done.3), channel_id=1, source_target_pairs={{0,2},{1,3},{2,0},{3,1},{4,6},{5,7},{6,4},{7,5},{8,10},{9,11},{10,... | collective-permute-start | bytes 786440 | tf_op jit(solution)/shard_map/ppermute | solution.py:199
  69.9 6.5 %copy-start.1 = (f32[8,128,128]{2,1,0:T(8,128)S(1)}, f32[8,128,128]{2,1,0:T(8,128)}, u32[]{:S(2)}) copy-start(f32[8,128,128]{2,1,0:T(8,128)} %copy-done) | copy-start | bytes 1572868
  69.9 6.5 %copy-start.3 = (f32[8,128,128]{2,1,0:T(8,128)S(1)}, f32[8,128,128]{2,1,0:T(8,128)}, u32[]{:S(2)}) copy-start(f32[8,128,128]{2,1,0:T(8,128)} %copy-done.2) | copy-start | bytes 1572868
  69.9 19.5 %collective-permute-start.6 = (f32[4,128,128]{2,1,0:T(8,128)}, f32[4,128,128]{2,1,0:T(8,128)S(1)}, u32[]{:S(2)}, u32[]{:S(2)}) collective-permute-start(f32[4,128,128]{2,1,0:T(8,128)} %collective-permute-done.3), channel_id=1, source_target_pairs={{0,1},{1,0},{2,3},{3,2},{4,5},{5,4},{6,7},{7,6},{8,9},{9,8},{10,11... | collective-permute-start | bytes 786440 | tf_op jit(solution)/shard_map/ppermute | solution.py:199
  72.2 16.2 %collective-permute-start.11 = (f32[4,128,128]{2,1,0:T(8,128)S(1)}, f32[4,128,128]{2,1,0:T(8,128)S(1)}, u32[]{:S(2)}, u32[]{:S(2)}) collective-permute-start(f32[4,128,128]{2,1,0:T(8,128)S(1)} %add.25), channel_id=1, source_target_pairs={{0,16},{4,20},{8,24},{12,28},{1,17},{5,21},{9,25},{13,29},{2,18},{... | collective-permute-start | bytes 786440 | tf_op jit(solution)/shard_map/ppermute | solution.py:194
  73.5 16.1 %collective-permute-start.8 = (f32[4,128,128]{2,1,0:T(8,128)}, f32[4,128,128]{2,1,0:T(8,128)S(1)}, u32[]{:S(2)}, u32[]{:S(2)}) collective-permute-start(f32[4,128,128]{2,1,0:T(8,128)} %collective-permute-done.7), channel_id=1, source_target_pairs={{0,2},{1,3},{2,0},{3,1},{4,6},{5,7},{6,4},{7,5},{8,10},{9,11},{10,... | collective-permute-start | bytes 786440 | tf_op jit(solution)/shard_map/ppermute | solution.py:199
  73.9 16.1 %collective-permute-start.5 = (f32[4,128,128]{2,1,0:T(8,128)}, f32[4,128,128]{2,1,0:T(8,128)S(1)}, u32[]{:S(2)}, u32[]{:S(2)}) collective-permute-start(f32[4,128,128]{2,1,0:T(8,128)} %collective-permute-done.4), channel_id=1, source_target_pairs={{0,1},{1,0},{2,3},{3,2},{4,5},{5,4},{6,7},{7,6},{8,9},{9,8},{10,11... | collective-permute-start | bytes 786440 | tf_op jit(solution)/shard_map/ppermute | solution.py:199
  77.3 20.8 %collective-permute-start.10 = (f32[4,128,128]{2,1,0:T(8,128)}, f32[4,128,128]{2,1,0:T(8,128)S(1)}, u32[]{:S(2)}, u32[]{:S(2)}) collective-permute-start(f32[4,128,128]{2,1,0:T(8,128)} %collective-permute-done.7), channel_id=1, source_target_pairs={{0,1},{1,0},{2,3},{3,2},{4,5},{5,4},{6,7},{7,6},{8,9},{9,8},{10,11... | collective-permute-start | bytes 786440 | tf_op jit(solution)/shard_map/ppermute | solution.py:199
  88.4 12.7 %collective-permute-start.14 = (f32[4,128,128]{2,1,0:T(8,128)S(1)}, f32[4,128,128]{2,1,0:T(8,128)S(1)}, u32[]{:S(2)}, u32[]{:S(2)}) collective-permute-start(f32[4,128,128]{2,1,0:T(8,128)S(1)} %collective-permute-done.11), channel_id=1, source_target_pairs={{0,1},{1,0},{2,3},{3,2},{4,5},{5,4},{6,7},{7,6},{8,9},{9,8},{10,11... | collective-permute-start | bytes 786440 | tf_op jit(solution)/shard_map/ppermute | solution.py:199
  89.4 7.9 %collective-permute-start.12 = (f32[4,128,128]{2,1,0:T(8,128)S(1)}, f32[4,128,128]{2,1,0:T(8,128)S(1)}, u32[]{:S(2)}, u32[]{:S(2)}) collective-permute-start(f32[4,128,128]{2,1,0:T(8,128)S(1)} %collective-permute-done.11), channel_id=1, source_target_pairs={{0,2},{1,3},{2,0},{3,1},{4,6},{5,7},{6,4},{7,5},{8,10},{9,11},{10,... | collective-permute-start | bytes 786440 | tf_op jit(solution)/shard_map/ppermute | solution.py:199
  89.6 8.5 %collective-permute-start.9 = (f32[4,128,128]{2,1,0:T(8,128)S(1)}, f32[4,128,128]{2,1,0:T(8,128)S(1)}, u32[]{:S(2)}, u32[]{:S(2)}) collective-permute-start(f32[4,128,128]{2,1,0:T(8,128)S(1)} %collective-permute-done.8), channel_id=1, source_target_pairs={{0,1},{1,0},{2,3},{3,2},{4,5},{5,4},{6,7},{7,6},{8,9},{9,8},{10,11... | collective-permute-start | bytes 786440 | tf_op jit(solution)/shard_map/ppermute | solution.py:199
  97.2 3.9 %collective-permute-start.13 = (f32[4,128,128]{2,1,0:T(8,128)S(1)}, f32[4,128,128]{2,1,0:T(8,128)S(1)}, u32[]{:S(2)}, u32[]{:S(2)}) collective-permute-start(f32[4,128,128]{2,1,0:T(8,128)S(1)} %collective-permute-done.12), channel_id=1, source_target_pairs={{0,1},{1,0},{2,3},{3,2},{4,5},{5,4},{6,7},{7,6},{8,9},{9,8},{10,11... | collective-permute-start | bytes 786440 | tf_op jit(solution)/shard_map/ppermute | solution.py:199

commit v8 on v5

--- a/solution.py
+++ b/solution.py
@@ -136,41 +136,46 @@
     )(*operands)
 
 
-def cross_kernel(scale, rows, first_level, group, q_ref, s_ref, m_ref, l_ref, o_ref):
+def cross_kernel(scale, rows, group, width, steps, q_ref, s_ref, m_ref, l_ref, o_ref):
     bits = s_ref.shape[0]
     dk = s_ref.shape[2]
     dv = s_ref.shape[3]
-    for j in range(group):
-        sib = jnp.concatenate([s_ref[b, j] for b in range(bits)], axis=1)
-        for a in range(rows // TQ):
-            r0 = a * TQ
-            t = jnp.dot(
-                q_ref[r0:r0 + TQ, j * dk:(j + 1) * dk], sib,
-                preferred_element_type=jnp.float32,
-            )
-            w_all = m_ref[j, r0:r0 + TQ, first_level:first_level + bits] * scale
-            cross = w_all[:, 0:1] * t[:, 0:dv]
-            for b in range(1, bits):
-                cross = cross + w_all[:, b:b + 1] * t[:, b * dv:(b + 1) * dv]
-            o_ref[r0:r0 + TQ, j * dv:(j + 1) * dv] = (
-                l_ref[r0:r0 + TQ, j * dv:(j + 1) * dv] + cross
-            )
-
-
-def cross_all(queries, sibs, mix_t, local, scale, first_level, group):
+
+    def body(step):
+        for j in range(group):
+            c0 = (step * group + j) * width
+            sib = jnp.concatenate([s_ref[b, j] for b in range(bits)], axis=1)
+            for a in range(rows // TQ):
+                r0 = a * TQ
+                t = jnp.dot(
+                    q_ref[r0:r0 + TQ, j * dk:(j + 1) * dk], sib,
+                    preferred_element_type=jnp.float32,
+                )
+                w_all = m_ref[r0:r0 + TQ, c0:c0 + bits] * scale
+                cross = w_all[:, 0:1] * t[:, 0:dv]
+                for b in range(1, bits):
+                    cross = cross + w_all[:, b:b + 1] * t[:, b * dv:(b + 1) * dv]
+                o_ref[r0:r0 + TQ, j * dv:(j + 1) * dv] = (
+                    l_ref[r0:r0 + TQ, j * dv:(j + 1) * dv] + cross
+                )
+
+    for step in range(steps):
+        pl.when(pl.program_id(0) == step)(functools.partial(body, step))
+
+
+def cross_all(queries, sibs, mix_c, local, scale, group, head_count, width):
     rows = queries.shape[0]
-    head_count = mix_t.shape[0]
     dk = queries.shape[1] // head_count
     dv = sibs.shape[3]
-    levels = mix_t.shape[2]
     bits = sibs.shape[0]
+    steps = head_count // group
     return pl.pallas_call(
-        functools.partial(cross_kernel, scale, rows, first_level, group),
-        grid=(head_count // group,),
+        functools.partial(cross_kernel, scale, rows, group, width, steps),
+        grid=(steps,),
         in_specs=[
             pl.BlockSpec((rows, dk * group), lambda g: (0, g)),
             pl.BlockSpec((bits, group, dk, dv), lambda g: (0, g, 0, 0)),
-            pl.BlockSpec((group, rows, levels), lambda g: (g, 0, 0)),
+            pl.BlockSpec(mix_c.shape, lambda g: (0, 0)),
             pl.BlockSpec((rows, dv * group), lambda g: (0, g)),
         ],
         out_specs=pl.BlockSpec((rows, dv * group), lambda g: (0, g)),
@@ -182,7 +187,7 @@
             transcendentals=0,
         ),
         compiler_params=pltpu.CompilerParams(vmem_limit_bytes=64 * 1024 * 1024),
-    )(queries, sibs, mix_t, local)
+    )(queries, sibs, mix_c, local)
 
 
 def swap(block, axis, bit, one_way=False):
@@ -275,7 +280,11 @@
         local = local_part(
             queries, keys, values, mix_t, masks, c * per, per, LOCAL_GROUP, scale, local
         )
-    return cross_all(queries, rounded, mix_t, local, scale, level_count, CROSS_GROUP)
+    bits = mixing.shape[0] - level_count
+    width = 8 * -(-bits // 8)
+    upper = jnp.pad(mixing[level_count:], ((0, width - bits), (0, 0), (0, 0)))
+    mix_c = upper.transpose(2, 1, 0).reshape(rows, head_count * width)
+    return cross_all(queries, rounded, mix_c, local, scale, CROSS_GROUP, head_count, width)
 
 
 def solution(mesh):

time: 116 us -> 117 us (level)
  local copies, waits for them, and re-layouts: 5.6 us -> 8.67 us
  waiting for transfers between devices: 31 us -> 29.3 us
    reshape x0 -> x2, local copies, waits for them, and re-layouts: none -> 2.08 us  [shards(): mix_c = upper.transpose(2, 1, 0).reshape(rows, head_count * width)]
    ppermute x9, waiting for transfers between devices: 4.24 us -> 2.26 us  [to_offset(): return lax.ppermute(block, axis, [(s, s ^ offset) for s in range(count)])]
    unnamed x13 -> x14, local copies, waits for them, and re-layouts: 5.55 us -> 6.55 us
  transfers between devices with their start and end apart: 15 -> 15, of which waited for: 5 -> 5; matrix products, arithmetic and copies ran while one was open for 13% -> 16% of each run, Pallas kernels for 24% -> 24%
where the time goes in v8:
time: 117 us; the launch traced here: 116 us
  Pallas kernels  49 us (42%)
  waiting for transfers between devices  29.3 us (25%)
  other arithmetic  16.7 us (14%)
  starting transfers between devices  12.6 us (11%)
  local copies, waits for them, and re-layouts  8.67 us (7%)
    pallas_call x4, Pallas kernels, local_part(): pl.pallas_call(functools.partial(local_kernel, scale, rows, group), grid=...  28 us
    ppermute x6, waiting for transfers between devices, swap(): return lax.ppermute(block, axis, route)  27 us
    pallas_call x1, Pallas kernels, cross_all(): pl.pallas_call(functools.partial(cross_kernel, scale, rows, group, width,...  15.7 us
    ppermute x9, starting transfers between devices, to_offset(): return lax.ppermute(block, axis, [(s, s ^ offset) for s in range(count)])  6.68 us
    unnamed x14, local copies, waits for them, and re-layouts  6.55 us
    ppermute x6, starting transfers between devices, swap(): return lax.ppermute(block, axis, route)  5.88 us
    pallas_call x1, Pallas kernels, own_state(): pl.pallas_call(functools.partial(state_kernel, head_count), grid=(rows //...  5.25 us
    unnamed x4, other arithmetic  4.94 us
  transfers between devices with their start and end apart: 15, of which 5 were waited for; matrix products, arithmetic and copies ran while one was open for 16% of the time, Pallas kernels for 24%

profile of v8, /device:TPU:25, one launch (start us, length us, event | category | flops | bytes accessed | tf_op | source)
XLA Modules:
  0.0 116.4 jit_solution(14285786318431687078)
XLA Ops:
  0.0 5.2 %shard_map.55 = f32[16,128,128]{2,1,0:T(8,128)} custom-call(bf16[1024,2048]{1,0:T(8,128)(2,1)} %k_ref.9, bf16[1024,2048]{1,0:T(8,128)(2,1)} %v_ref.9), custom_call_target="tpu_custom_call" | custom-call | flops 536870912 | bytes 9437184 | tf_op jit(solution)/shard_map/pallas_call | solution.py:51
  5.3 0.7 collective-permute-start
  5.9 2.5 %collective-permute-done = f32[16,128,128]{2,1,0:T(8,128)S(1)} collective-permute-done((f32[16,128,128]{2,1,0:T(8,128)}, f32[16,128,128]{2,1,0:T(8,128)S(1)}, u32[]{:S(2)}, u32[]{:S(2)}) %collective-permute-start) | collective-permute-done | bytes 1048608 | tf_op jit(solution)/shard_map/ppermute | solution.py:202
  8.4 1.7 %add.20 = f32[16,128,128]{2,1,0:T(8,128)S(1)} add(f32[16,128,128]{2,1,0:T(8,128)} %shard_map.55, f32[16,128,128]{2,1,0:T(8,128)S(1)} %collective-permute-done) | non-fusion elementwise | flops 262144 | bytes 3145728 | tf_op jit(solution)/shard_map/add | solution.py:245
  10.1 0.0 copy-start.5
  10.2 1.3 %collective-permute-start.1 = (f32[8,128,128]{2,1,0:T(8,128)S(1)}, f32[8,128,128]{2,1,0:T(8,128)S(1)}, u32[]{:S(2)}, u32[]{:S(2)}) collective-permute-start(f32[8,128,128]{2,1,0:T(8,128)S(1)} %constant_dynamic-slice_fusion), channel_id=1, source_target_pairs={{0,2},{2,0},{1,3},{3,1},{4,6},{6,4},{5,7},{7,5},{8,10},{10,8},{9,1... | collective-permute-start | bytes 1572872 | tf_op jit(solution)/shard_map/ppermute | solution.py:202
  11.5 11.9 %collective-permute-done.1 = f32[8,128,128]{2,1,0:T(8,128)S(1)} collective-permute-done((f32[8,128,128]{2,1,0:T(8,128)S(1)}, f32[8,128,128]{2,1,0:T(8,128)S(1)}, u32[]{:S(2)}, u32[]{:S(2)}) %collective-permute-start.1) | collective-permute-done | bytes 524320 | tf_op jit(solution)/shard_map/ppermute | solution.py:202
  23.4 1.2 %collective-permute-start.2 = (f32[8,128,128]{2,1,0:T(8,128)S(1)}, f32[8,128,128]{2,1,0:T(8,128)}, u32[]{:S(2)}, u32[]{:S(2)}) collective-permute-start(f32[8,128,128]{2,1,0:T(8,128)S(1)} %collective-permute-done.1), channel_id=1, source_target_pairs={{0,1},{1,0},{2,3},{3,2},{4,5},{5,4},{6,7},{7,6},{8,9},{9,8},{10,11... | collective-permute-start | bytes 1572872 | tf_op jit(solution)/shard_map/ppermute | solution.py:202
  24.6 1.7 %collective-permute-done.2 = f32[8,128,128]{2,1,0:T(8,128)} collective-permute-done((f32[8,128,128]{2,1,0:T(8,128)S(1)}, f32[8,128,128]{2,1,0:T(8,128)}, u32[]{:S(2)}, u32[]{:S(2)}) %collective-permute-start.2) | collective-permute-done | bytes 524320 | tf_op jit(solution)/shard_map/ppermute | solution.py:202
  26.3 1.1 broadcast_select_fusion.1
  27.5 0.8 copy-done
  28.3 0.8 fusion.11
  29.0 1.2 %collective-permute-start.3 = (f32[4,128,128]{2,1,0:T(8,128)}, f32[4,128,128]{2,1,0:T(8,128)}, u32[]{:S(2)}, u32[]{:S(2)}) collective-permute-start(f32[4,128,128]{2,1,0:T(8,128)} %fusion.11), channel_id=1, source_target_pairs={{0,4},{4,0},{8,12},{12,8},{16,20},{20,16},{24,28},{28,24},{1,5},{5... | collective-permute-start | bytes 786440 | tf_op jit(solution)/shard_map/ppermute | solution.py:202
  30.3 4.7 %copy.13 = f32[10,16,1024]{0,2,1:T(8,128)} copy(f32[10,16,1024]{2,1,0:T(8,128)S(1)} %copy-done.5) | data formatting | bytes 1310720 | tf_op args[3]
  35.0 1.0 copy.15
  36.0 7.1 %shard_map.56.rest_0_ = f32[1024,2048]{1,0:T(8,128)} custom-call(bf16[1024,2048]{1,0:T(8,128)(2,1)} %q_ref.9, bf16[1024,2048]{1,0:T(8,128)(2,1)} %k_ref.9, bf16[1024,2048]{1,0:T(8,128)(2,1)} %v_ref.9, f32[16,1024,10]{2,1,0:T(8,128)} %bitcast.35, f32[3,256,256]{2,1,0:T(8,128)} %constant.28.clone.c_ref), custom_call_target="tpu_custom_call" | custom-call | flops 1342177280 | bytes 5242880 | tf_op jit(solution)/shard_map/pallas_call | solution.py:123
  43.1 7.0 %shard_map.57.rest_0_ = f32[1024,2048]{1,0:T(8,128)} custom-call(bf16[1024,2048]{1,0:T(8,128)(2,1)} %q_ref.9, bf16[1024,2048]{1,0:T(8,128)(2,1)} %k_ref.9, bf16[1024,2048]{1,0:T(8,128)(2,1)} %v_ref.9, f32[16,1024,10]{2,1,0:T(8,128)} %bitcast.36, f32[3,256,256]{2,1,0:T(8,128)} %constant.28.clone.c_ref, ...), custom_call_target="tpu_custom_call", output_to_operand_aliasing={{}: (5, {})} | custom-call | flops 1342177280 | bytes 5242880 | tf_op jit(solution)/shard_map/pallas_call | solution.py:123
  50.1 1.8 %add.24 = f32[4,128,128]{2,1,0:T(8,128)} add(f32[4,128,128]{2,1,0:T(8,128)} %fusion.11, f32[4,128,128]{2,1,0:T(8,128)} %collective-permute-done.3) | non-fusion elementwise | flops 65536 | bytes 786432 | tf_op jit(solution)/shard_map/add | solution.py:254
  51.8 0.2 collective-permute-start.7
  52.0 1.2 %collective-permute-start.4 = (f32[4,128,128]{2,1,0:T(8,128)}, f32[4,128,128]{2,1,0:T(8,128)}, u32[]{:S(2)}, u32[]{:S(2)}) collective-permute-start(f32[4,128,128]{2,1,0:T(8,128)} %collective-permute-done.3), channel_id=1, source_target_pairs={{0,2},{1,3},{2,0},{3,1},{4,6},{5,7},{6,4},{7,5},{8,10},{9,11},{10,... | collective-permute-start | bytes 786440 | tf_op jit(solution)/shard_map/ppermute | solution.py:207
  53.2 1.1 pad_bitcast_fusion
  54.4 1.0 copy.14.m_ref
  55.4 7.0 %shard_map.58.rest_0_ = f32[1024,2048]{1,0:T(8,128)} custom-call(bf16[1024,2048]{1,0:T(8,128)(2,1)} %q_ref.9, bf16[1024,2048]{1,0:T(8,128)(2,1)} %k_ref.9, bf16[1024,2048]{1,0:T(8,128)(2,1)} %v_ref.9, f32[16,1024,10]{2,1,0:T(8,128)} %bitcast.37, f32[3,256,256]{2,1,0:T(8,128)} %constant.28.clone.c_ref, ...), custom_call_target="tpu_custom_call", output_to_operand_aliasing={{}: (5, {})} | custom-call | flops 1342177280 | bytes 5242880 | tf_op jit(solution)/shard_map/pallas_call | solution.py:123
  62.3 7.0 %shard_map.59.l_ref = f32[1024,2048]{1,0:T(8,128)} custom-call(bf16[1024,2048]{1,0:T(8,128)(2,1)} %q_ref.9, bf16[1024,2048]{1,0:T(8,128)(2,1)} %k_ref.9, bf16[1024,2048]{1,0:T(8,128)(2,1)} %v_ref.9, f32[16,1024,10]{2,1,0:T(8,128)} %bitcast.38, f32[3,256,256]{2,1,0:T(8,128)} %constant.28.clone.c_ref, ...), custom_call_target="tpu_custom_call", output_to_operand_aliasing={{}: (5, {})} | custom-call | flops 1342177280 | bytes 5242880 | tf_op jit(solution)/shard_map/pallas_call | solution.py:123
  69.3 1.3 %collective-permute-start.6 = (f32[4,128,128]{2,1,0:T(8,128)}, f32[4,128,128]{2,1,0:T(8,128)S(1)}, u32[]{:S(2)}, u32[]{:S(2)}) collective-permute-start(f32[4,128,128]{2,1,0:T(8,128)} %collective-permute-done.3), channel_id=1, source_target_pairs={{0,1},{1,0},{2,3},{3,2},{4,5},{5,4},{6,7},{7,6},{8,9},{9,8},{10,11... | collective-permute-start | bytes 786440 | tf_op jit(solution)/shard_map/ppermute | solution.py:207
  70.6 1.1 add.25
  71.6 1.3 %collective-permute-start.11 = (f32[4,128,128]{2,1,0:T(8,128)S(1)}, f32[4,128,128]{2,1,0:T(8,128)S(1)}, u32[]{:S(2)}, u32[]{:S(2)}) collective-permute-start(f32[4,128,128]{2,1,0:T(8,128)S(1)} %add.25), channel_id=1, source_target_pairs={{0,16},{4,20},{8,24},{12,28},{1,17},{5,21},{9,25},{13,29},{2,18},{... | collective-permute-start | bytes 786440 | tf_op jit(solution)/shard_map/ppermute | solution.py:202
  72.9 0.3 collective-permute-start.8
  73.3 0.4 collective-permute-start.5
  73.6 2.1 %fusion.5 = bf16[5,16,128,128]{3,2,1,0:T(8,128)(2,1)} fusion(f32[16,128,128]{2,1,0:T(8,128)} %copy-done.4, f32[]{:T(128)S(6)} %convert_element_type.60), kind=kLoop, calls=%fused_computation.12 | loop fusion | flops 524287 | bytes 1572868
  75.8 0.9 fusion.9
  76.7 0.1 collective-permute-start.10
  76.9 11.0 %collective-permute-done.11 = f32[4,128,128]{2,1,0:T(8,128)S(1)} collective-permute-done((f32[4,128,128]{2,1,0:T(8,128)S(1)}, f32[4,128,128]{2,1,0:T(8,128)S(1)}, u32[]{:S(2)}, u32[]{:S(2)}) %collective-permute-start.11) | collective-permute-done | bytes 262176 | tf_op jit(solution)/shard_map/ppermute | solution.py:202
  87.8 0.3 collective-permute-start.12
  88.1 1.2 %collective-permute-start.14 = (f32[4,128,128]{2,1,0:T(8,128)S(1)}, f32[4,128,128]{2,1,0:T(8,128)S(1)}, u32[]{:S(2)}, u32[]{:S(2)}) collective-permute-start(f32[4,128,128]{2,1,0:T(8,128)S(1)} %collective-permute-done.11), channel_id=1, source_target_pairs={{0,1},{1,0},{2,3},{3,2},{4,5},{5,4},{6,7},{7,6},{8,9},{9,8},{10,11... | collective-permute-start | bytes 786440 | tf_op jit(solution)/shard_map/ppermute | solution.py:207
  89.3 0.1 collective-permute-start.9
  89.4 1.1 select_bitcast_fusion.11
  90.5 1.0 select_bitcast_fusion.10
  91.6 0.9 fusion.8
  92.5 2.2 %collective-permute-done.12 = f32[4,128,128]{2,1,0:T(8,128)S(1)} collective-permute-done((f32[4,128,128]{2,1,0:T(8,128)S(1)}, f32[4,128,128]{2,1,0:T(8,128)S(1)}, u32[]{:S(2)}, u32[]{:S(2)}) %collective-permute-start.12) | collective-permute-done | bytes 262176 | tf_op jit(solution)/shard_map/ppermute | solution.py:207
  94.7 1.8 %collective-permute-start.13 = (f32[4,128,128]{2,1,0:T(8,128)S(1)}, f32[4,128,128]{2,1,0:T(8,128)S(1)}, u32[]{:S(2)}, u32[]{:S(2)}) collective-permute-start(f32[4,128,128]{2,1,0:T(8,128)S(1)} %collective-permute-done.12), channel_id=1, source_target_pairs={{0,1},{1,0},{2,3},{3,2},{4,5},{5,4},{6,7},{7,6},{8,9},{9,8},{10,11... | collective-permute-start | bytes 786440 | tf_op jit(solution)/shard_map/ppermute | solution.py:207
  96.5 1.1 select_bitcast_fusion.7
  97.6 1.0 select_bitcast_fusion.6
  98.7 0.9 fusion.7
  99.6 0.1 select_bitcast_fusion.2
  99.6 0.1 select_bitcast_fusion.3
  99.8 0.9 fusion.6.s_ref
  100.7 15.7 %shard_map.60 = f32[1024,2048]{1,0:T(8,128)} custom-call(bf16[1024,2048]{1,0:T(8,128)(2,1)} %q_ref.9, bf16[5,16,128,128]{3,2,1,0:T(8,128)(2,1)} %fusion.6.s_ref, f32[1024,128]{1,0:T(8,128)} %copy.14.m_ref, f32[1024,2048]{1,0:T(8,128)} %shard_map.59.l_ref), custom_call_target="tpu_custom_call", output_to_operand_aliasing={{}: (3, {})} | custom-call | flops 2684354560 | bytes 20971520 | tf_op jit(solution)/shard_map/pallas_call | solution.py:172
  (23 shorter events, 0.1 us)
Async XLA Ops:
  5.3 3.2 %collective-permute-start = (f32[16,128,128]{2,1,0:T(8,128)}, f32[16,128,128]{2,1,0:T(8,128)S(1)}, u32[]{:S(2)}, u32[]{:S(2)}) collective-permute-start(f32[16,128,128]{2,1,0:T(8,128)} %shard_map.55), channel_id=1, source_target_pairs={{0,1},{1,0},{2,3},{3,2},{4,5},{5,4},{6,7},{7,6},{8,9},{9,8},{10,11... | collective-permute-start | bytes 3145736 | tf_op jit(solution)/shard_map/ppermute | solution.py:202
  8.4 19.0 %copy-start.4 = (f32[16,128,128]{2,1,0:T(8,128)}, f32[16,128,128]{2,1,0:T(8,128)S(1)}, u32[]{:S(2)}) copy-start(f32[16,128,128]{2,1,0:T(8,128)S(1)} %collective-permute-done) | copy-start | bytes 3145732
  10.1 20.1 %copy-start.5 = (f32[10,16,1024]{2,1,0:T(8,128)S(1)}, f32[10,16,1024]{2,1,0:T(8,128)}, u32[]{:S(2)}) copy-start(f32[10,16,1024]{2,1,0:T(8,128)} %param.8) | copy-start | bytes 1966084
  10.2 13.2 %collective-permute-start.1 = (f32[8,128,128]{2,1,0:T(8,128)S(1)}, f32[8,128,128]{2,1,0:T(8,128)S(1)}, u32[]{:S(2)}, u32[]{:S(2)}) collective-permute-start(f32[8,128,128]{2,1,0:T(8,128)S(1)} %constant_dynamic-slice_fusion), channel_id=1, source_target_pairs={{0,2},{2,0},{1,3},{3,1},{4,6},{6,4},{5,7},{7,5},{8,10},{10,8},{9,1... | collective-permute-start | bytes 1572872 | tf_op jit(solution)/shard_map/ppermute | solution.py:202
  23.4 2.9 %collective-permute-start.2 = (f32[8,128,128]{2,1,0:T(8,128)S(1)}, f32[8,128,128]{2,1,0:T(8,128)}, u32[]{:S(2)}, u32[]{:S(2)}) collective-permute-start(f32[8,128,128]{2,1,0:T(8,128)S(1)} %collective-permute-done.1), channel_id=1, source_target_pairs={{0,1},{1,0},{2,3},{3,2},{4,5},{5,4},{6,7},{7,6},{8,9},{9,8},{10,11... | collective-permute-start | bytes 1572872 | tf_op jit(solution)/shard_map/ppermute | solution.py:202
  27.4 0.8 copy-start
  27.4 1.6 %copy-start.2 = (f32[8,128,128]{2,1,0:T(8,128)}, f32[8,128,128]{2,1,0:T(8,128)S(1)}, u32[]{:S(2)}) copy-start(f32[8,128,128]{2,1,0:T(8,128)S(1)} %get-tuple-element.15) | copy-start | bytes 1572868
  29.0 6.0 %slice-start = ((f32[10,16,1024]{2,1,0:T(8,128)}), f32[5,16,1024]{2,1,0:T(8,128)S(1)}, s32[]{:S(2)}) async-start(f32[10,16,1024]{2,1,0:T(8,128)} %param.8), calls=%async_computation | async-start | bytes 655360 | tf_op jit(solution)/shard_map/slice | solution.py:285
  29.0 21.1 %collective-permute-start.3 = (f32[4,128,128]{2,1,0:T(8,128)}, f32[4,128,128]{2,1,0:T(8,128)}, u32[]{:S(2)}, u32[]{:S(2)}) collective-permute-start(f32[4,128,128]{2,1,0:T(8,128)} %fusion.11), channel_id=1, source_target_pairs={{0,4},{4,0},{8,12},{12,8},{16,20},{20,16},{24,28},{28,24},{1,5},{5... | collective-permute-start | bytes 786440 | tf_op jit(solution)/shard_map/ppermute | solution.py:202
  51.8 18.7 %collective-permute-start.7 = (f32[4,128,128]{2,1,0:T(8,128)}, f32[4,128,128]{2,1,0:T(8,128)}, u32[]{:S(2)}, u32[]{:S(2)}) collective-permute-start(f32[4,128,128]{2,1,0:T(8,128)} %add.24), channel_id=1, source_target_pairs={{0,8},{8,0},{4,12},{12,4},{16,24},{24,16},{20,28},{28,20},{1,9},{9... | collective-permute-start | bytes 786440 | tf_op jit(solution)/shard_map/ppermute | solution.py:202
  52.0 21.2 %collective-permute-start.4 = (f32[4,128,128]{2,1,0:T(8,128)}, f32[4,128,128]{2,1,0:T(8,128)}, u32[]{:S(2)}, u32[]{:S(2)}) collective-permute-start(f32[4,128,128]{2,1,0:T(8,128)} %collective-permute-done.3), channel_id=1, source_target_pairs={{0,2},{1,3},{2,0},{3,1},{4,6},{5,7},{6,4},{7,5},{8,10},{9,11},{10,... | collective-permute-start | bytes 786440 | tf_op jit(solution)/shard_map/ppermute | solution.py:207
  69.3 6.5 %copy-start.1 = (f32[8,128,128]{2,1,0:T(8,128)S(1)}, f32[8,128,128]{2,1,0:T(8,128)}, u32[]{:S(2)}) copy-start(f32[8,128,128]{2,1,0:T(8,128)} %copy-done) | copy-start | bytes 1572868
  69.3 6.5 %copy-start.3 = (f32[8,128,128]{2,1,0:T(8,128)S(1)}, f32[8,128,128]{2,1,0:T(8,128)}, u32[]{:S(2)}) copy-start(f32[8,128,128]{2,1,0:T(8,128)} %copy-done.2) | copy-start | bytes 1572868
  69.3 18.8 %collective-permute-start.6 = (f32[4,128,128]{2,1,0:T(8,128)}, f32[4,128,128]{2,1,0:T(8,128)S(1)}, u32[]{:S(2)}, u32[]{:S(2)}) collective-permute-start(f32[4,128,128]{2,1,0:T(8,128)} %collective-permute-done.3), channel_id=1, source_target_pairs={{0,1},{1,0},{2,3},{3,2},{4,5},{5,4},{6,7},{7,6},{8,9},{9,8},{10,11... | collective-permute-start | bytes 786440 | tf_op jit(solution)/shard_map/ppermute | solution.py:207
  71.6 16.2 %collective-permute-start.11 = (f32[4,128,128]{2,1,0:T(8,128)S(1)}, f32[4,128,128]{2,1,0:T(8,128)S(1)}, u32[]{:S(2)}, u32[]{:S(2)}) collective-permute-start(f32[4,128,128]{2,1,0:T(8,128)S(1)} %add.25), channel_id=1, source_target_pairs={{0,16},{4,20},{8,24},{12,28},{1,17},{5,21},{9,25},{13,29},{2,18},{... | collective-permute-start | bytes 786440 | tf_op jit(solution)/shard_map/ppermute | solution.py:202
  72.9 16.4 %collective-permute-start.8 = (f32[4,128,128]{2,1,0:T(8,128)}, f32[4,128,128]{2,1,0:T(8,128)S(1)}, u32[]{:S(2)}, u32[]{:S(2)}) collective-permute-start(f32[4,128,128]{2,1,0:T(8,128)} %collective-permute-done.7), channel_id=1, source_target_pairs={{0,2},{1,3},{2,0},{3,1},{4,6},{5,7},{6,4},{7,5},{8,10},{9,11},{10,... | collective-permute-start | bytes 786440 | tf_op jit(solution)/shard_map/ppermute | solution.py:207
  73.3 16.1 %collective-permute-start.5 = (f32[4,128,128]{2,1,0:T(8,128)}, f32[4,128,128]{2,1,0:T(8,128)S(1)}, u32[]{:S(2)}, u32[]{:S(2)}) collective-permute-start(f32[4,128,128]{2,1,0:T(8,128)} %collective-permute-done.4), channel_id=1, source_target_pairs={{0,1},{1,0},{2,3},{3,2},{4,5},{5,4},{6,7},{7,6},{8,9},{9,8},{10,11... | collective-permute-start | bytes 786440 | tf_op jit(solution)/shard_map/ppermute | solution.py:207
  76.7 19.8 %collective-permute-start.10 = (f32[4,128,128]{2,1,0:T(8,128)}, f32[4,128,128]{2,1,0:T(8,128)S(1)}, u32[]{:S(2)}, u32[]{:S(2)}) collective-permute-start(f32[4,128,128]{2,1,0:T(8,128)} %collective-permute-done.7), channel_id=1, source_target_pairs={{0,1},{1,0},{2,3},{3,2},{4,5},{5,4},{6,7},{7,6},{8,9},{9,8},{10,11... | collective-permute-start | bytes 786440 | tf_op jit(solution)/shard_map/ppermute | solution.py:207
  87.8 6.9 %collective-permute-start.12 = (f32[4,128,128]{2,1,0:T(8,128)S(1)}, f32[4,128,128]{2,1,0:T(8,128)S(1)}, u32[]{:S(2)}, u32[]{:S(2)}) collective-permute-start(f32[4,128,128]{2,1,0:T(8,128)S(1)} %collective-permute-done.11), channel_id=1, source_target_pairs={{0,2},{1,3},{2,0},{3,1},{4,6},{5,7},{6,4},{7,5},{8,10},{9,11},{10,... | collective-permute-start | bytes 786440 | tf_op jit(solution)/shard_map/ppermute | solution.py:207
  88.1 11.5 %collective-permute-start.14 = (f32[4,128,128]{2,1,0:T(8,128)S(1)}, f32[4,128,128]{2,1,0:T(8,128)S(1)}, u32[]{:S(2)}, u32[]{:S(2)}) collective-permute-start(f32[4,128,128]{2,1,0:T(8,128)S(1)} %collective-permute-done.11), channel_id=1, source_target_pairs={{0,1},{1,0},{2,3},{3,2},{4,5},{5,4},{6,7},{7,6},{8,9},{9,8},{10,11... | collective-permute-start | bytes 786440 | tf_op jit(solution)/shard_map/ppermute | solution.py:207
  89.3 7.2 %collective-permute-start.9 = (f32[4,128,128]{2,1,0:T(8,128)S(1)}, f32[4,128,128]{2,1,0:T(8,128)S(1)}, u32[]{:S(2)}, u32[]{:S(2)}) collective-permute-start(f32[4,128,128]{2,1,0:T(8,128)S(1)} %collective-permute-done.8), channel_id=1, source_target_pairs={{0,1},{1,0},{2,3},{3,2},{4,5},{5,4},{6,7},{7,6},{8,9},{9,8},{10,11... | collective-permute-start | bytes 786440 | tf_op jit(solution)/shard_map/ppermute | solution.py:207
  94.7 4.9 %collective-permute-start.13 = (f32[4,128,128]{2,1,0:T(8,128)S(1)}, f32[4,128,128]{2,1,0:T(8,128)S(1)}, u32[]{:S(2)}, u32[]{:S(2)}) collective-permute-start(f32[4,128,128]{2,1,0:T(8,128)S(1)} %collective-permute-done.12), channel_id=1, source_target_pairs={{0,1},{1,0},{2,3},{3,2},{4,5},{5,4},{6,7},{7,6},{8,9},{9,8},{10,11... | collective-permute-start | bytes 786440 | tf_op jit(solution)/shard_map/ppermute | solution.py:207
